TPU v7x, 512 devices: a whole 4x4x16 slice. The times are simulated.
512 devices in a mesh: fsdp: 32 (over x_lo, z), tp: 16 (over x_hi, y, core).
Axes of the slice: x: 4 (x_hi: 2, x_lo: 2; x = x_hi * 2 + x_lo), y: 4, z: 16, core: 2. Of those that a mesh axis runs over, the one named last changes fastest.
Arguments:
- activations: bfloat16 [16384, 4096], P(('fsdp', 'tp')), may hold values from -6 to 6
- norm_gain: float32 [4096], replicated, may hold values from 0.5 to 1.5
- proj_weight: bfloat16 [3, 4096, 4096], P(None, 'fsdp', 'tp'), may hold values from -0.09375 to 0.09375
- short_filter: float32 [256, 7], P('tp'), may hold values from -3 to 3
- segment_ids: int32 [32, 512], P('fsdp'), may hold values from 0 to 7, never falling along the last dimension, each value on 1 to 256 neighbouring positions
- needle_pos: int32 [32, 16], P('fsdp'), may hold values from 0 to 511
- readout: float32 [4096], replicated, may hold values from -6 to 6
Outputs:
- mixer_out: bfloat16 [16384, 4096], P(('fsdp', 'tp'))
- needle_score: float32 [32, 16], P('fsdp')
Inputs may be any that keep to these rules, and one draw needn't show every extreme that they name: segment_ids never fall along a slab; each document covers 1 to 256 positions.
All inputs are finite; a program needn't handle non-finite values.
Results may differ from a plain program's by a relative error of at most 0.0068.
Values may be sent and summed in bfloat16 or wider, within the bound.
No kernel may reach another device: no remote copies, remote signals or barrier semaphores. Data moves between devices by JAX's collectives and lax.ppermute only.
A program may use at most 64 MiB of HBM per device.

v0:
```python
import math

import jax
import jax.numpy as jnp
from jax import lax
from jax.sharding import PartitionSpec as P

EPSILON = 1e-06


def short_conv(gated_prod, tap_table, segments):
    length = gated_prod.shape[0]
    filtered = jnp.zeros(gated_prod.shape, jnp.float32)
    for offset in range(tap_table.shape[1]):
        shifted = jnp.pad(gated_prod, ((offset, 0), (0, 0)))[:length]
        earlier = jnp.pad(segments, (offset, 0), constant_values=-1)[:length]
        same_doc = (earlier == segments).astype(jnp.float32)
        filtered = filtered + shifted * same_doc[:, None] * tap_table[:, offset][None, :]
    return filtered


def local(activations, norm_gain, proj_weight, short_filter, segment_ids, needle_pos, readout):
    model_width = activations.shape[1]
    local_rows = activations.shape[0]
    values = activations.astype(jnp.float32)
    scaled = lax.rsqrt(jnp.mean(values * values, axis=1, keepdims=True) + EPSILON)
    normed = (values * scaled * norm_gain[None, :]).astype(jnp.bfloat16)
    slab_rows = lax.all_gather(normed, "tp", axis=0, tiled=True)
    channels = proj_weight.shape[2]
    projected = jnp.einsum(
        "sk,ikc->isc",
        slab_rows,
        lax.all_gather(proj_weight, "fsdp", axis=1, tiled=True),
        preferred_element_type=jnp.float32,
    )
    gated_prod = projected[1] * projected[2]
    tap_table = jnp.repeat(short_filter, channels // short_filter.shape[0], axis=0)
    filtered = short_conv(gated_prod, tap_table, segment_ids[0])
    mixed_local = (projected[0] * filtered).astype(jnp.bfloat16)
    device_rank = lax.axis_index("tp")
    full_rows = lax.all_gather(mixed_local, "tp", axis=1, tiled=True)
    own_rows = lax.dynamic_slice_in_dim(full_rows, device_rank * local_rows, local_rows, 0)
    positions = needle_pos[0]
    local_pos = positions - device_rank * local_rows
    picker = (local_pos[:, None] == jnp.arange(local_rows, dtype=jnp.int32)[None, :]).astype(
        jnp.bfloat16
    )
    picked = jnp.dot(picker, own_rows, preferred_element_type=jnp.float32)
    partial_sum = jnp.sum(picked * readout[None, :], axis=1)
    summed_score = lax.psum(partial_sum, "tp")
    needle_score = (summed_score / math.sqrt(model_width))[None, :]
    return (own_rows, needle_score)


def solution(mesh):
    in_specs = (
        P(("fsdp", "tp"), None),
        P(),
        P(None, "fsdp", "tp"),
        P("tp", None),
        P("fsdp", None),
        P("fsdp", None),
        P(),
    )
    out_specs = (P(("fsdp", "tp"), None), P("fsdp", None))
    return jax.shard_map(local, mesh=mesh, in_specs=in_specs, out_specs=out_specs, check_vma=False)
```

profile of v0, /device:TPU:1, one launch (start us, length us, event | category | flops | bytes accessed | tf_op | source)
XLA Modules:
  0.0 348.2 jit_solution(14428492473865925798)
XLA Ops:
  7.2 0.0 all-gather.4.cloned.1.call-start
  7.2 1.1 fusion.26
  8.3 1.8 fusion.28
  10.1 0.0 all-gather.4.cloned.1.call-update
  10.1 0.0 all-gather.6.cloned.1.call-start
  10.2 0.7 all-gather.6.cloned.1.call-update
  10.9 0.0 all-gather.8.cloned.1.call-start
  10.9 0.8 broadcast_in_dim.4
  11.7 0.1 reshape.38
  11.8 1.0 fusion.42
  12.8 0.0 copy-start.2
  12.8 0.0 copy-start.1
  12.9 75.4 %all-gather.4.cloned.1.call-done = bf16[512,4096]{1,0:T(8,128)(2,1)} async-done(((bf16[32,4096]{1,0:T(8,128)(2,1)}), bf16[512,4096]{1,0:T(8,128)(2,1)}) %all-gather.4.cloned.1.call-update) | async-done | bytes 4194320 | tf_op jit(solution)/shard_map/all_gather | solution.py:28
  88.3 123.8 %all-gather.6.cloned.1.call-done = bf16[3,4096,256]{2,1,0:T(8,128)(2,1)} async-done(((bf16[3,128,256]{2,1,0:T(8,128)(2,1)}), bf16[3,4096,256]{2,1,0:T(8,128)(2,1)}) %all-gather.6.cloned.1.call-update) | async-done | bytes 6291472 | tf_op jit(solution)/shard_map/all_gather | solution.py:33
  212.0 7.0 %fusion.2 = f32[3,512,256]{2,1,0:T(8,128)S(1)} fusion(bf16[3,4096,256]{2,1,0:T(8,128)(2,1)} %all-gather.6.cloned.1.call-done, bf16[512,4096]{1,0:T(8,128)(2,1)} %all-gather.4.cloned.1.call-done), kind=kOutput, calls=%fused_computation.3 | convolution fusion | flops 3221225472 | bytes 12058624 | tf_op jit(solution)/shard_map/sk,ikc->isc/dot_general | solution.py:30
  219.1 0.1 fusion.29
  219.1 1.5 fusion.15
  220.6 0.0 all-gather.8.cloned.1.call-update
  220.7 86.4 %all-gather.8.cloned.1.call-done = bf16[512,4096]{1,0:T(8,128)(2,1)} async-done(((bf16[512,256]{1,0:T(8,128)(2,1)}), bf16[512,4096]{1,0:T(8,128)(2,1)}) %all-gather.8.cloned.1.call-update) | async-done | bytes 4194320 | tf_op jit(solution)/shard_map/all_gather | solution.py:41
  307.1 1.0 constant_dynamic-slice_fusion
  308.0 0.0 copy-start
  308.0 0.3 fusion.5
  308.4 32.8 %psum.7 = f32[16]{0:T(128)S(1)} all-reduce(f32[16]{0:T(128)S(1)} %fusion.5), channel_id=1, replica_groups=mesh['fsdp'=32,'tp'=16] {'tp'}, use_global_device_ids=true, to_apply=%region_2.3 | all-reduce | flops 16 | bytes 128 | tf_op jit(solution)/shard_map/psum | solution.py:50
  341.1 0.5 multiply_bitcast_fusion
  (6 shorter events, 0.0 us)
Async XLA Ops:
  7.2 81.1 %all-gather.4.cloned.1.call-start = ((), (), s32[]{:S(2)}) async-start(), calls=%async_computation | async-start | bytes 4456448 | tf_op jit(solution)/shard_map/all_gather | solution.py:28
  10.1 201.9 %all-gather.6.cloned.1.call-start = ((), (), s32[]{:S(2)}) async-start(), calls=%async_computation.1 | async-start | bytes 6488064 | tf_op jit(solution)/shard_map/all_gather | solution.py:33
  10.9 296.2 %all-gather.8.cloned.1.call-start = ((), (), s32[]{:S(2)}) async-start(), calls=%async_computation.2 | async-start | bytes 4456448 | tf_op jit(solution)/shard_map/all_gather | solution.py:41
  12.8 207.8 %copy-start.2 = (s32[1,16]{1,0:T(1,128)S(1)}, s32[1,16]{1,0:T(1,128)}, u32[]{:S(2)}) copy-start(s32[1,16]{1,0:T(1,128)} %param.12) | copy-start | bytes 196
  12.8 295.2 %copy-start.1 = (f32[4096]{0:T(1024)S(1)}, f32[4096]{0:T(1024)}, u32[]{:S(2)}) copy-start(f32[4096]{0:T(1024)} %param.13) | copy-start | bytes 49156
  308.0 33.6 %copy-start = (bf16[32,4096]{1,0:T(8,128)(2,1)}, bf16[32,4096]{1,0:T(8,128)(2,1)S(1)}, u32[]{:S(2)}) copy-start(bf16[32,4096]{1,0:T(8,128)(2,1)S(1)} %constant_dynamic-slice_fusion) | copy-start | bytes 786436
Sparse Core Ops, SparseCore 0:
  11.9 76.3 all-gather.3
  90.4 121.6 all-gather.5
  220.8 86.2 all-gather.7
where the time goes:
time: 348 us
  waiting for transfers between devices  286 us (82%)
  blocking collectives  32.8 us (9%)
  between operations  13.8 us (4%)
  matrix products  7.37 us (2%)
  other arithmetic  5.98 us (2%)
    all_gather x1, waiting for transfers between devices, local(): lax.all_gather(proj_weight, 'fsdp', axis=1, tiled=True)  124 us
    all_gather x1, waiting for transfers between devices, local(): full_rows = lax.all_gather(mixed_local, 'tp', axis=1, tiled=True)  86.4 us
    all_gather x1, waiting for transfers between devices, local(): slab_rows = lax.all_gather(normed, 'tp', axis=0, tiled=True)  75.4 us
    psum x1, blocking collectives, local(): summed_score = lax.psum(partial_sum, 'tp')  32.8 us
    dot_general x1, matrix products, local(): jnp.einsum('sk,ikc->isc', slab_rows, lax.all_gather(proj_weight, 'fsdp',...  7.03 us
  transfers between devices with their start and end apart: 3, of which 3 were waited for; matrix products, arithmetic and copies ran while one was open for 1% of the time, Pallas kernels for 0%

commit v1 on v0

--- a/solution.py
+++ b/solution.py
@@ -22,33 +22,37 @@
 def local(activations, norm_gain, proj_weight, short_filter, segment_ids, needle_pos, readout):
     model_width = activations.shape[1]
     local_rows = activations.shape[0]
+    tp_size = lax.axis_size("tp")
+    channels = proj_weight.shape[2]
+    weights = lax.all_gather(proj_weight, "fsdp", axis=1, tiled=True)
     values = activations.astype(jnp.float32)
     scaled = lax.rsqrt(jnp.mean(values * values, axis=1, keepdims=True) + EPSILON)
     normed = (values * scaled * norm_gain[None, :]).astype(jnp.bfloat16)
-    slab_rows = lax.all_gather(normed, "tp", axis=0, tiled=True)
-    channels = proj_weight.shape[2]
-    projected = jnp.einsum(
-        "sk,ikc->isc",
-        slab_rows,
-        lax.all_gather(proj_weight, "fsdp", axis=1, tiled=True),
-        preferred_element_type=jnp.float32,
+    spread = jnp.broadcast_to(normed[None], (tp_size,) + normed.shape)
+    slab_rows = lax.all_to_all(spread, "tp", 0, 0, tiled=False).reshape(
+        tp_size * local_rows, model_width
     )
+    projected = jnp.einsum("sk,ikc->isc", slab_rows, weights, preferred_element_type=jnp.float32)
     gated_prod = projected[1] * projected[2]
     tap_table = jnp.repeat(short_filter, channels // short_filter.shape[0], axis=0)
     filtered = short_conv(gated_prod, tap_table, segment_ids[0])
     mixed_local = (projected[0] * filtered).astype(jnp.bfloat16)
     device_rank = lax.axis_index("tp")
-    full_rows = lax.all_gather(mixed_local, "tp", axis=1, tiled=True)
-    own_rows = lax.dynamic_slice_in_dim(full_rows, device_rank * local_rows, local_rows, 0)
     positions = needle_pos[0]
-    local_pos = positions - device_rank * local_rows
-    picker = (local_pos[:, None] == jnp.arange(local_rows, dtype=jnp.int32)[None, :]).astype(
+    slab_len = tp_size * local_rows
+    picker = (positions[:, None] == jnp.arange(slab_len, dtype=jnp.int32)[None, :]).astype(
         jnp.bfloat16
     )
-    picked = jnp.dot(picker, own_rows, preferred_element_type=jnp.float32)
-    partial_sum = jnp.sum(picked * readout[None, :], axis=1)
-    summed_score = lax.psum(partial_sum, "tp")
-    needle_score = (summed_score / math.sqrt(model_width))[None, :]
+    picked = jnp.dot(picker, mixed_local, preferred_element_type=jnp.float32)
+    own_readout = lax.dynamic_slice_in_dim(readout, device_rank * channels, channels, 0)
+    partial_sum = jnp.sum(picked * own_readout[None, :], axis=1)
+    partials = lax.all_to_all(
+        jnp.broadcast_to(partial_sum[None], (tp_size,) + partial_sum.shape), "tp", 0, 0, tiled=False
+    )
+    needle_score = (jnp.sum(partials, axis=0) / math.sqrt(model_width))[None, :]
+    blocks = mixed_local.reshape(tp_size, local_rows, channels)
+    gathered = lax.all_to_all(blocks, "tp", 0, 0, tiled=False)
+    own_rows = jnp.transpose(gathered, (1, 0, 2)).reshape(local_rows, tp_size * channels)
     return (own_rows, needle_score)
 
 

time: 348 us -> 203 us (0.58)
  waiting for transfers between devices: 286 us -> 126 us
  starting transfers between devices: 0.12 us -> 15.3 us
    all_gather x3 -> x1, waiting for transfers between devices: 286 us -> 18.9 us  [local(): weights = lax.all_gather(proj_weight, 'fsdp', axis=1, tiled=True)]
    all_to_all x0 -> x2, waiting for transfers between devices: none -> 106 us  [the longest x1 98.3 us: local(): lax.all_to_all(spread, 'tp', 0, 0, tiled=False)]
    psum x1 -> x0, blocking collectives: 32.8 us -> none  [local(): summed_score = lax.psum(partial_sum, 'tp')]
    all_to_all x0 -> x1, blocking collectives: none -> 30.6 us  [local(): lax.all_to_all(jnp.broadcast_to(partial_sum[None], (tp_size,) + partial_s...]
    all_to_all x0 -> x2, starting transfers between devices: none -> 15.3 us  [the longest x1 11.3 us: local(): lax.all_to_all(spread, 'tp', 0, 0, tiled=False)]
  transfers between devices with their start and end apart: 3 -> 3, of which waited for: 3 -> 3; matrix products, arithmetic and copies ran while one was open for 1% -> 3% of each run, Pallas kernels for 0% -> 0%
where the time goes in v1:
time: 203 us
  waiting for transfers between devices  126 us (62%)
  blocking collectives  30.6 us (15%)
  starting transfers between devices  15.3 us (8%)
  between operations  14.1 us (7%)
  matrix products  8.29 us (4%)
  other arithmetic  4.34 us (2%)
  local copies, waits for them, and re-layouts  4.24 us (2%)
    all_to_all x1, waiting for transfers between devices, local(): lax.all_to_all(spread, 'tp', 0, 0, tiled=False)  98.3 us
    all_to_all x1, blocking collectives, local(): lax.all_to_all(jnp.broadcast_to(partial_sum[None], (tp_size,) + partial_s...  30.6 us
    all_gather x1, waiting for transfers between devices, local(): weights = lax.all_gather(proj_weight, 'fsdp', axis=1, tiled=True)  18.9 us
    all_to_all x1, starting transfers between devices, local(): lax.all_to_all(spread, 'tp', 0, 0, tiled=False)  11.3 us
    all_to_all x1, waiting for transfers between devices, local(): gathered = lax.all_to_all(blocks, 'tp', 0, 0, tiled=False)  8.21 us
    dot_general x1, matrix products, local(): jnp.einsum('sk,ikc->isc', slab_rows, weights, preferred_element_type=jnp....  7.04 us
  transfers between devices with their start and end apart: 3, of which 3 were waited for; matrix products, arithmetic and copies ran while one was open for 3% of the time, Pallas kernels for 0%

profile of v1, /device:TPU:1, one launch (start us, length us, event | category | flops | bytes accessed | tf_op | source)
XLA Modules:
  0.0 202.9 jit_solution(14651823412645313950)
XLA Ops:
  7.2 0.0 all-gather.2.cloned.1.call-start
  7.2 0.7 all-gather.2.cloned.1.call-update
  7.9 1.1 fusion.21
  9.0 1.1 fusion.23
  10.1 2.6 %broadcast_in_dim.6 = bf16[16,32,4096]{2,1,0:T(8,128)(2,1)} broadcast(bf16[32,4096]{1,0:T(8,128)(2,1)S(1)} %fusion.23), dimensions={1,2} | broadcast | bytes 4456448 | tf_op jit(solution)/shard_map/broadcast_in_dim | solution.py:31
  12.7 11.3 %all-to-all-start = ((bf16[16,32,4096]{2,1,0:T(8,128)(2,1)}), bf16[16,32,4096]{2,1,0:T(8,128)(2,1)}, u32[]{:S(2)}, u32[]{:S(2)}) async-start(bf16[16,32,4096]{2,1,0:T(8,128)(2,1)} %broadcast_in_dim.6), calls=%async_computation | async-start | bytes 8388608 | tf_op jit(solution)/shard_map/all_to_all | solution.py:32
  24.0 0.0 copy-done
  24.0 0.1 broadcast_in_dim.7
  24.0 0.1 reshape.58
  24.1 0.8 dynamic_slice.3
  24.9 0.0 copy-done.1
  24.9 0.1 fusion.37
  25.0 98.3 %all-to-all-done = bf16[16,32,4096]{2,1,0:T(8,128)(2,1)} async-done(((bf16[16,32,4096]{2,1,0:T(8,128)(2,1)}), bf16[16,32,4096]{2,1,0:T(8,128)(2,1)}, u32[]{:S(2)}, u32[]{:S(2)}) %all-to-all-start) | async-done | bytes 4194336 | tf_op jit(solution)/shard_map/all_to_all | solution.py:32
  123.3 18.9 %all-gather.2.cloned.1.call-done = bf16[3,4096,256]{2,1,0:T(8,128)(2,1)} async-done(((bf16[3,128,256]{2,1,0:T(8,128)(2,1)}), bf16[3,4096,256]{2,1,0:T(8,128)(2,1)}) %all-gather.2.cloned.1.call-update) | async-done | bytes 6291472 | tf_op jit(solution)/shard_map/all_gather | solution.py:27
  142.2 7.0 %convolution_bitcast_fusion = f32[3,512,256]{2,1,0:T(8,128)S(1)} fusion(bf16[512,4096,1]{1,0,2:T(8,128)(2,1)} %bitcast.1, bf16[3,4096,256]{2,1,0:T(8,128)(2,1)} %all-gather.2.cloned.1.call-done), kind=kOutput, calls=%fused_computation | convolution fusion | flops 3221225472 | bytes 12058624 | tf_op jit(solution)/shard_map/sk,ikc->isc/dot_general | solution.py:35
  149.2 0.1 fusion.24
  149.3 1.5 fusion.10
  150.8 0.0 copy-done.2
  150.8 1.2 fusion
  152.0 30.6 %all_to_all.16 = f32[16,1,16]{2,1,0:T(1,128)S(1)} all-to-all(f32[16,1,16]{2,1,0:T(1,128)S(1)} %broadcast_in_dim.8), channel_id=1, replica_groups=mesh['fsdp'=32,'tp'=16] {'tp'}, dimensions={0} | all-to-all | bytes 2048 | tf_op jit(solution)/shard_map/all_to_all | solution.py:49
  182.6 4.0 %all-to-all-start.1 = ((bf16[16,32,256]{2,1,0:T(8,128)(2,1)}), bf16[16,32,256]{2,1,0:T(8,128)(2,1)S(1)}, u32[]{:S(2)}, u32[]{:S(2)}) async-start(bf16[16,32,256]{2,1,0:T(8,128)(2,1)} %bitcast.13), calls=%async_computation.1 | async-start | bytes 524288 | tf_op jit(solution)/shard_map/all_to_all | solution.py:54
  186.7 0.5 multiply_bitcast_fusion
  187.2 8.2 %all-to-all-done.1 = bf16[16,32,256]{2,1,0:T(8,128)(2,1)S(1)} async-done(((bf16[16,32,256]{2,1,0:T(8,128)(2,1)}), bf16[16,32,256]{2,1,0:T(8,128)(2,1)S(1)}, u32[]{:S(2)}, u32[]{:S(2)}) %all-to-all-start.1) | async-done | bytes 262176 | tf_op jit(solution)/shard_map/all_to_all | solution.py:54
  195.4 0.7 copy.15
  (7 shorter events, 0.0 us)
Async XLA Ops:
  7.2 135.0 %all-gather.2.cloned.1.call-start = ((), (), s32[]{:S(2)}) async-start(), calls=%async_computation.3 | async-start | bytes 6488064 | tf_op jit(solution)/shard_map/all_gather | solution.py:27
  12.7 11.3 %copy-start = (f32[16,7]{0,1:T(8,128)S(1)}, f32[16,7]{0,1:T(8,128)}, u32[]{:S(2)}) copy-start(f32[16,7]{0,1:T(8,128)} %param.10) | copy-start | bytes 1348
  12.7 12.2 %copy-start.1 = (s32[1,512]{1,0:T(1,128)S(1)}, s32[1,512]{1,0:T(1,128)}, u32[]{:S(2)}) copy-start(s32[1,512]{1,0:T(1,128)} %param.11) | copy-start | bytes 6148
  12.7 110.6 %all-to-all-start = ((bf16[16,32,4096]{2,1,0:T(8,128)(2,1)}), bf16[16,32,4096]{2,1,0:T(8,128)(2,1)}, u32[]{:S(2)}, u32[]{:S(2)}) async-start(bf16[16,32,4096]{2,1,0:T(8,128)(2,1)} %broadcast_in_dim.6), calls=%async_computation | async-start | bytes 8388608 | tf_op jit(solution)/shard_map/all_to_all | solution.py:32
  142.2 8.6 %copy-start.2 = (s32[1,16]{1,0:T(1,128)S(1)}, s32[1,16]{1,0:T(1,128)}, u32[]{:S(2)}) copy-start(s32[1,16]{1,0:T(1,128)} %param.12) | copy-start | bytes 196
  182.6 12.7 %all-to-all-start.1 = ((bf16[16,32,256]{2,1,0:T(8,128)(2,1)}), bf16[16,32,256]{2,1,0:T(8,128)(2,1)S(1)}, u32[]{:S(2)}, u32[]{:S(2)}) async-start(bf16[16,32,256]{2,1,0:T(8,128)(2,1)} %bitcast.13), calls=%async_computation.1 | async-start | bytes 524288 | tf_op jit(solution)/shard_map/all_to_all | solution.py:54
Sparse Core Ops, SparseCore 0:
  10.1 132.0 all-gather.1

commit v2 on v1

--- a/solution.py
+++ b/solution.py
@@ -19,16 +19,52 @@
     return filtered
 
 
+def gather_weights(proj_weight, fsdp_size, z_size):
+    fsdp = lax.axis_index("fsdp")
+    x_lo = fsdp // z_size
+    x_swap = [(f, (f + z_size) % fsdp_size) for f in range(fsdp_size)]
+    z_up = [(f, (f // z_size) * z_size + (f + 1) % z_size) for f in range(fsdp_size)]
+    z_down = [(f, (f // z_size) * z_size + (f - 1) % z_size) for f in range(fsdp_size)]
+    other = lax.ppermute(proj_weight, "fsdp", x_swap)
+    first = jnp.where(x_lo == 0, proj_weight, other)
+    second = jnp.where(x_lo == 0, other, proj_weight)
+    pair = jnp.stack([first, second], axis=1)
+    ahead = [pair]
+    behind = []
+    right = pair
+    left = pair
+    for _ in range(1, z_size // 2):
+        right = lax.ppermute(right, "fsdp", z_up)
+        left = lax.ppermute(left, "fsdp", z_down)
+        behind.append(right)
+        ahead.append(left)
+    last_a = lax.ppermute(right[:, :1], "fsdp", z_up)
+    last_b = lax.ppermute(left[:, 1:], "fsdp", z_down)
+    ahead.append(jnp.concatenate([last_a, last_b], axis=1))
+    pieces = ahead + behind[::-1]
+    stacked = jnp.stack(pieces, axis=2)
+    return stacked.reshape(
+        proj_weight.shape[0], fsdp_size * proj_weight.shape[1], proj_weight.shape[2]
+    )
+
+
 def local(activations, norm_gain, proj_weight, short_filter, segment_ids, needle_pos, readout):
     model_width = activations.shape[1]
     local_rows = activations.shape[0]
     tp_size = lax.axis_size("tp")
+    fsdp_size = lax.axis_size("fsdp")
+    z_size = fsdp_size // 2
     channels = proj_weight.shape[2]
-    weights = lax.all_gather(proj_weight, "fsdp", axis=1, tiled=True)
+    block = proj_weight.shape[1]
+    weights = gather_weights(proj_weight, fsdp_size, z_size)
     values = activations.astype(jnp.float32)
     scaled = lax.rsqrt(jnp.mean(values * values, axis=1, keepdims=True) + EPSILON)
     normed = (values * scaled * norm_gain[None, :]).astype(jnp.bfloat16)
-    spread = jnp.broadcast_to(normed[None], (tp_size,) + normed.shape)
+    z = lax.axis_index("fsdp") % z_size
+    grid = normed.reshape(local_rows, 2, z_size, block)
+    doubled = jnp.concatenate([grid, grid], axis=2)
+    rotated = lax.dynamic_slice_in_dim(doubled, z, z_size, axis=2).reshape(local_rows, model_width)
+    spread = jnp.broadcast_to(rotated[None], (tp_size,) + rotated.shape)
     slab_rows = lax.all_to_all(spread, "tp", 0, 0, tiled=False).reshape(
         tp_size * local_rows, model_width
     )

time: 203 us -> 192 us (0.946)
  waiting for transfers between devices: 126 us -> 45.5 us
  starting transfers between devices: 15.3 us -> 93.5 us
  local copies, waits for them, and re-layouts: 4.24 us -> 36.9 us
  blocking collectives: 30.6 us -> 0 us
  between operations: 14.1 us -> 1.01 us
  other arithmetic: 4.34 us -> 6.9 us
    all_to_all x1, waiting for transfers between devices: 98.3 us -> 0.01 us  [local(): lax.all_to_all(spread, 'tp', 0, 0, tiled=False)]
    ppermute x0 -> x17, starting transfers between devices: none -> 68.1 us  [the longest x7 44.2 us: gather_weights(): left = lax.ppermute(left, 'fsdp', z_down)]
    ppermute x0 -> x17, waiting for transfers between devices: none -> 31.2 us  [the longest x7 18.7 us: gather_weights(): left = lax.ppermute(left, 'fsdp', z_down)]
    all_to_all x1 -> x0, blocking collectives: 30.6 us -> none  [local(): lax.all_to_all(jnp.broadcast_to(partial_sum[None], (tp_size,) + partial_s...]
    all_gather x1 -> x0, waiting for transfers between devices: 18.9 us -> none  [local(): weights = lax.all_gather(proj_weight, 'fsdp', axis=1, tiled=True)]
    unnamed x6 -> x21, local copies, waits for them, and re-layouts: 0.01 us -> 11.3 us
    all_to_all x0 -> x1, starting transfers between devices: none -> 10.8 us  [local(): lax.all_to_all(jnp.broadcast_to(partial_sum[None], (tp_size,) + partial_s...]
    reshape x0 -> x1, local copies, waits for them, and re-layouts: none -> 10.3 us  [gather_weights(): stacked.reshape(proj_weight.shape[0], fsdp_size * proj_weight.shape[1], p...]
  transfers between devices with their start and end apart: 3 -> 20, of which waited for: 3 -> 11; matrix products, arithmetic and copies ran while one was open for 3% -> 21% of each run, Pallas kernels for 0% -> 0%
where the time goes in v2:
time: 192 us; the launch traced here: 191 us
  starting transfers between devices  93.5 us (49%)
  waiting for transfers between devices  45.5 us (24%)
  local copies, waits for them, and re-layouts  36.9 us (19%)
  matrix products  7.13 us (4%)
  other arithmetic  6.9 us (4%)
    ppermute x7, starting transfers between devices, gather_weights(): left = lax.ppermute(left, 'fsdp', z_down)  44.2 us
    ppermute x7, waiting for transfers between devices, gather_weights(): left = lax.ppermute(left, 'fsdp', z_down)  18.7 us
    ppermute x7, starting transfers between devices, gather_weights(): right = lax.ppermute(right, 'fsdp', z_up)  13.4 us
    unnamed x21, local copies, waits for them, and re-layouts  11.3 us
    all_to_all x1, starting transfers between devices, local(): lax.all_to_all(jnp.broadcast_to(partial_sum[None], (tp_size,) + partial_s...  10.8 us
    all_to_all x1, starting transfers between devices, local(): lax.all_to_all(spread, 'tp', 0, 0, tiled=False)  10.6 us
    reshape x1, local copies, waits for them, and re-layouts, gather_weights(): stacked.reshape(proj_weight.shape[0], fsdp_size * proj_weight.shape[1], p...  10.3 us
    another operation x2, local copies, waits for them, and re-layouts, gather_weights(): stacked = jnp.stack(pieces, axis=2)  9.71 us
  transfers between devices with their start and end apart: 20, of which 11 were waited for; matrix products, arithmetic and copies ran while one was open for 21% of the time, Pallas kernels for 0%

profile of v2, /device:TPU:1, one launch (start us, length us, event | category | flops | bytes accessed | tf_op | source)
XLA Modules:
  0.0 190.9 jit_solution(3349767197133745388)
XLA Ops:
  0.6 3.9 %collective-permute-start = (bf16[3,128,256]{2,1,0:T(8,128)(2,1)}, bf16[3,128,256]{2,1,0:T(8,128)(2,1)S(1)}, u32[]{:S(2)}, u32[]{:S(2)}) collective-permute-start(bf16[3,128,256]{2,1,0:T(8,128)(2,1)} %param.9), channel_id=1, source_target_pairs={{0,256},{16,272},{32,288},{48,304},{64,320},{80,336},{96,352},{112... | collective-permute-start | bytes 589832 | tf_op jit(solution)/shard_map/ppermute | solution.py:28
  4.6 3.2 %collective-permute-done = bf16[3,128,256]{2,1,0:T(8,128)(2,1)S(1)} collective-permute-done((bf16[3,128,256]{2,1,0:T(8,128)(2,1)}, bf16[3,128,256]{2,1,0:T(8,128)(2,1)S(1)}, u32[]{:S(2)}, u32[]{:S(2)}) %collective-permute-start) | collective-permute-done | bytes 196640 | tf_op jit(solution)/shard_map/ppermute | solution.py:28
  8.8 12.6 %collective-permute-start.1 = (bf16[3,2,128,256]{3,2,0,1:T(8,128)(2,1)S(1)}, bf16[3,2,128,256]{3,2,0,1:T(8,128)(2,1)S(1)}, u32[]{:S(2)}, u32[]{:S(2)}) collective-permute-start(bf16[3,2,128,256]{3,2,0,1:T(8,128)(2,1)S(1)} %pad_maximum_fusion), channel_id=1, source_target_pairs={{0,240},{16,0},{32,16},{48,32},{64,48},{80,64},{96,80},{112,96},{1... | collective-permute-start | bytes 1179656 | tf_op jit(solution)/shard_map/ppermute | solution.py:38
  23.4 4.9 %collective-permute-done.1 = bf16[3,2,128,256]{3,2,0,1:T(8,128)(2,1)S(1)} collective-permute-done((bf16[3,2,128,256]{3,2,0,1:T(8,128)(2,1)S(1)}, bf16[3,2,128,256]{3,2,0,1:T(8,128)(2,1)S(1)}, u32[]{:S(2)}, u32[]{:S(2)}) %collective-permute-start.1) | collective-permute-done | bytes 393248 | tf_op jit(solution)/shard_map/ppermute | solution.py:38
  28.3 5.3 %collective-permute-start.2 = (bf16[3,2,128,256]{3,2,0,1:T(8,128)(2,1)S(1)}, bf16[3,2,128,256]{3,2,0,1:T(8,128)(2,1)S(1)}, u32[]{:S(2)}, u32[]{:S(2)}) collective-permute-start(bf16[3,2,128,256]{3,2,0,1:T(8,128)(2,1)S(1)} %collective-permute-done.1), channel_id=1, source_target_pairs={{0,240},{16,0},{32,16},{48,32},{64,48},{80,64},{96,80},{112,96},{1... | collective-permute-start | bytes 1179656 | tf_op jit(solution)/shard_map/ppermute | solution.py:38
  36.7 2.9 %collective-permute-done.2 = bf16[3,2,128,256]{3,2,0,1:T(8,128)(2,1)S(1)} collective-permute-done((bf16[3,2,128,256]{3,2,0,1:T(8,128)(2,1)S(1)}, bf16[3,2,128,256]{3,2,0,1:T(8,128)(2,1)S(1)}, u32[]{:S(2)}, u32[]{:S(2)}) %collective-permute-start.2) | collective-permute-done | bytes 393248 | tf_op jit(solution)/shard_map/ppermute | solution.py:38
  39.5 5.3 %collective-permute-start.3 = (bf16[3,2,128,256]{3,2,0,1:T(8,128)(2,1)S(1)}, bf16[3,2,128,256]{3,2,0,1:T(8,128)(2,1)S(1)}, u32[]{:S(2)}, u32[]{:S(2)}) collective-permute-start(bf16[3,2,128,256]{3,2,0,1:T(8,128)(2,1)S(1)} %collective-permute-done.2), channel_id=1, source_target_pairs={{0,240},{16,0},{32,16},{48,32},{64,48},{80,64},{96,80},{112,96},{1... | collective-permute-start | bytes 1179656 | tf_op jit(solution)/shard_map/ppermute | solution.py:38
  48.3 2.5 %broadcast_in_dim.9 = bf16[16,32,4096]{2,1,0:T(8,128)(2,1)} broadcast(bf16[32,4096]{1,0:T(8,128)(2,1)S(1)} %bitcast.83), dimensions={1,2} | broadcast | bytes 4456448 | tf_op jit(solution)/shard_map/broadcast_in_dim | solution.py:67
  50.8 10.6 %all-to-all-start = ((bf16[16,32,4096]{2,1,0:T(8,128)(2,1)}), bf16[16,32,4096]{2,1,0:T(8,128)(2,1)}, u32[]{:S(2)}, u32[]{:S(2)}) async-start(bf16[16,32,4096]{2,1,0:T(8,128)(2,1)} %broadcast_in_dim.9), calls=%async_computation | async-start | bytes 8388608 | tf_op jit(solution)/shard_map/all_to_all | solution.py:68
  61.4 4.9 %collective-permute-start.4 = (bf16[3,2,128,256]{3,2,0,1:T(8,128)(2,1)S(1)}, bf16[3,2,128,256]{3,2,0,1:T(8,128)(2,1)}, u32[]{:S(2)}, u32[]{:S(2)}) collective-permute-start(bf16[3,2,128,256]{3,2,0,1:T(8,128)(2,1)S(1)} %collective-permute-done.3), channel_id=1, source_target_pairs={{0,240},{16,0},{32,16},{48,32},{64,48},{80,64},{96,80},{112,96},{1... | collective-permute-start | bytes 1179656 | tf_op jit(solution)/shard_map/ppermute | solution.py:38
  70.0 4.6 %collective-permute-done.4 = bf16[3,2,128,256]{3,2,0,1:T(8,128)(2,1)} collective-permute-done((bf16[3,2,128,256]{3,2,0,1:T(8,128)(2,1)S(1)}, bf16[3,2,128,256]{3,2,0,1:T(8,128)(2,1)}, u32[]{:S(2)}, u32[]{:S(2)}) %collective-permute-start.4) | collective-permute-done | bytes 393248 | tf_op jit(solution)/shard_map/ppermute | solution.py:38
  74.6 5.4 %collective-permute-start.5 = (bf16[3,2,128,256]{3,2,0,1:T(8,128)(2,1)}, bf16[3,2,128,256]{3,2,0,1:T(8,128)(2,1)S(1)}, u32[]{:S(2)}, u32[]{:S(2)}) collective-permute-start(bf16[3,2,128,256]{3,2,0,1:T(8,128)(2,1)} %collective-permute-done.4), channel_id=1, source_target_pairs={{0,240},{16,0},{32,16},{48,32},{64,48},{80,64},{96,80},{112,96},{1... | collective-permute-start | bytes 1179656 | tf_op jit(solution)/shard_map/ppermute | solution.py:38
  83.5 4.2 %collective-permute-done.5 = bf16[3,2,128,256]{3,2,0,1:T(8,128)(2,1)S(1)} collective-permute-done((bf16[3,2,128,256]{3,2,0,1:T(8,128)(2,1)}, bf16[3,2,128,256]{3,2,0,1:T(8,128)(2,1)S(1)}, u32[]{:S(2)}, u32[]{:S(2)}) %collective-permute-start.5) | collective-permute-done | bytes 393248 | tf_op jit(solution)/shard_map/ppermute | solution.py:38
  87.8 5.3 %collective-permute-start.6 = (bf16[3,2,128,256]{3,2,0,1:T(8,128)(2,1)S(1)}, bf16[3,2,128,256]{3,2,0,1:T(8,128)(2,1)S(1)}, u32[]{:S(2)}, u32[]{:S(2)}) collective-permute-start(bf16[3,2,128,256]{3,2,0,1:T(8,128)(2,1)S(1)} %collective-permute-done.5), channel_id=1, source_target_pairs={{0,240},{16,0},{32,16},{48,32},{64,48},{80,64},{96,80},{112,96},{1... | collective-permute-start | bytes 1179656 | tf_op jit(solution)/shard_map/ppermute | solution.py:38
  99.7 5.4 %collective-permute-start.7 = (bf16[3,2,128,256]{3,2,0,1:T(8,128)(2,1)S(1)}, bf16[3,2,128,256]{3,2,0,1:T(8,128)(2,1)S(1)}, u32[]{:S(2)}, u32[]{:S(2)}) collective-permute-start(bf16[3,2,128,256]{3,2,0,1:T(8,128)(2,1)S(1)} %collective-permute-done.6), channel_id=1, source_target_pairs={{0,240},{16,0},{32,16},{48,32},{64,48},{80,64},{96,80},{112,96},{1... | collective-permute-start | bytes 1179656 | tf_op jit(solution)/shard_map/ppermute | solution.py:38
  108.6 7.4 %collective-permute-done.14 = bf16[3,2,128,256]{3,2,0,1:T(8,128)(2,1)S(1)} collective-permute-done((bf16[3,2,128,256]{3,2,0,1:T(8,128)(2,1)S(1)}, bf16[3,2,128,256]{3,2,0,1:T(8,128)(2,1)S(1)}, u32[]{:S(2)}, u32[]{:S(2)}) %collective-permute-start.14) | collective-permute-done | bytes 393248 | tf_op jit(solution)/shard_map/ppermute | solution.py:37
  118.0 4.6 %collective-permute-start.16 = (bf16[3,1,128,256]{3,2,0,1:T(8,128)(2,1)S(1)}, bf16[3,1,128,256]{3,2,0,1:T(8,128)(2,1)S(1)}, u32[]{:S(2)}, u32[]{:S(2)}) collective-permute-start(bf16[3,1,128,256]{3,2,0,1:T(8,128)(2,1)S(1)} %slice.97), channel_id=1, source_target_pairs={{0,240},{16,0},{32,16},{48,32},{64,48},{80,64},{96,80},{112,96},{1... | collective-permute-start | bytes 589832 | tf_op jit(solution)/shard_map/ppermute | solution.py:42
  131.4 8.9 %copy.20 = bf16[3,2,16,128,256]{3,2,1,4,0:T(8,128)(2,1)} copy(bf16[3,2,16,128,256]{4,3,0,1,2:T(8,128)(2,1)} %bitcast_dynamic-update-slice_fusion) | data formatting | bytes 12582912 | tf_op jit(solution)/shard_map/stack | solution.py:45
  140.3 10.3 %reshape.63 = bf16[3,4096,256]{1,2,0:T(8,128)(2,1)} reshape(bf16[3,2,16,128,256]{3,2,1,4,0:T(8,128)(2,1)} %copy.20) | data formatting | bytes 12582912 | tf_op jit(solution)/shard_map/reshape | solution.py:46
  150.7 6.8 %convolution_bitcast_fusion = f32[3,512,256]{1,2,0:T(8,128)S(1)} fusion(bf16[3,4096,256]{1,2,0:T(8,128)(2,1)} %reshape.63, bf16[512,4096,1]{1,0,2:T(8,128)(2,1)} %bitcast.19), kind=kOutput, calls=%fused_computation | convolution fusion | flops 3221225472 | bytes 12058624 | tf_op jit(solution)/shard_map/sk,ikc->isc/dot_general | solution.py:71
  159.7 10.8 %all-to-all-start.2 = ((f32[16,1,16]{2,1,0:T(1,128)}), f32[16,1,16]{2,1,0:T(1,128)S(1)}, u32[]{:S(2)}, u32[]{:S(2)}) async-start(f32[16,1,16]{2,1,0:T(1,128)} %broadcast_in_dim.11), calls=%async_computation.2 | async-start | bytes 16384 | tf_op jit(solution)/shard_map/all_to_all | solution.py:85
  171.3 6.1 %all-to-all-done.2 = f32[16,1,16]{2,1,0:T(1,128)S(1)} async-done(((f32[16,1,16]{2,1,0:T(1,128)}), f32[16,1,16]{2,1,0:T(1,128)S(1)}, u32[]{:S(2)}, u32[]{:S(2)}) %all-to-all-start.2) | async-done | bytes 1056 | tf_op jit(solution)/shard_map/all_to_all | solution.py:85
  177.5 4.0 %all-to-all-start.1 = ((bf16[16,32,256]{2,1,0:T(8,128)(2,1)}), bf16[16,32,256]{2,1,0:T(8,128)(2,1)S(1)}, u32[]{:S(2)}, u32[]{:S(2)}) async-start(bf16[16,32,256]{2,1,0:T(8,128)(2,1)} %bitcast.31), calls=%async_computation.1 | async-start | bytes 524288 | tf_op jit(solution)/shard_map/all_to_all | solution.py:90
  182.0 8.2 %all-to-all-done.1 = bf16[16,32,256]{2,1,0:T(8,128)(2,1)S(1)} async-done(((bf16[16,32,256]{2,1,0:T(8,128)(2,1)}), bf16[16,32,256]{2,1,0:T(8,128)(2,1)S(1)}, u32[]{:S(2)}, u32[]{:S(2)}) %all-to-all-start.1) | async-done | bytes 262176 | tf_op jit(solution)/shard_map/all_to_all | solution.py:90
  (65 shorter events, 41.8 us)
Async XLA Ops:
  0.6 7.2 %collective-permute-start = (bf16[3,128,256]{2,1,0:T(8,128)(2,1)}, bf16[3,128,256]{2,1,0:T(8,128)(2,1)S(1)}, u32[]{:S(2)}, u32[]{:S(2)}) collective-permute-start(bf16[3,128,256]{2,1,0:T(8,128)(2,1)} %param.9), channel_id=1, source_target_pairs={{0,256},{16,272},{32,288},{48,304},{64,320},{80,336},{96,352},{112... | collective-permute-start | bytes 589832 | tf_op jit(solution)/shard_map/ppermute | solution.py:28
  8.8 19.5 %collective-permute-start.1 = (bf16[3,2,128,256]{3,2,0,1:T(8,128)(2,1)S(1)}, bf16[3,2,128,256]{3,2,0,1:T(8,128)(2,1)S(1)}, u32[]{:S(2)}, u32[]{:S(2)}) collective-permute-start(bf16[3,2,128,256]{3,2,0,1:T(8,128)(2,1)S(1)} %pad_maximum_fusion), channel_id=1, source_target_pairs={{0,240},{16,0},{32,16},{48,32},{64,48},{80,64},{96,80},{112,96},{1... | collective-permute-start | bytes 1179656 | tf_op jit(solution)/shard_map/ppermute | solution.py:38
  21.5 12.2 %collective-permute-start.8 = (bf16[3,2,128,256]{3,2,0,1:T(8,128)(2,1)S(1)}, bf16[3,2,128,256]{3,2,0,1:T(8,128)(2,1)S(1)}, u32[]{:S(2)}, u32[]{:S(2)}) collective-permute-start(bf16[3,2,128,256]{3,2,0,1:T(8,128)(2,1)S(1)} %pad_maximum_fusion), channel_id=1, source_target_pairs={{0,16},{16,32},{32,48},{48,64},{64,80},{80,96},{96,112},{112,128},... | collective-permute-start | bytes 1179656 | tf_op jit(solution)/shard_map/ppermute | solution.py:37
  28.3 11.2 %collective-permute-start.2 = (bf16[3,2,128,256]{3,2,0,1:T(8,128)(2,1)S(1)}, bf16[3,2,128,256]{3,2,0,1:T(8,128)(2,1)S(1)}, u32[]{:S(2)}, u32[]{:S(2)}) collective-permute-start(bf16[3,2,128,256]{3,2,0,1:T(8,128)(2,1)S(1)} %collective-permute-done.1), channel_id=1, source_target_pairs={{0,240},{16,0},{32,16},{48,32},{64,48},{80,64},{96,80},{112,96},{1... | collective-permute-start | bytes 1179656 | tf_op jit(solution)/shard_map/ppermute | solution.py:38
  33.6 11.2 %collective-permute-start.9 = (bf16[3,2,128,256]{3,2,0,1:T(8,128)(2,1)S(1)}, bf16[3,2,128,256]{3,2,0,1:T(8,128)(2,1)S(1)}, u32[]{:S(2)}, u32[]{:S(2)}) collective-permute-start(bf16[3,2,128,256]{3,2,0,1:T(8,128)(2,1)S(1)} %collective-permute-done.8), channel_id=1, source_target_pairs={{0,16},{16,32},{32,48},{48,64},{64,80},{80,96},{96,112},{112,128},... | collective-permute-start | bytes 1179656 | tf_op jit(solution)/shard_map/ppermute | solution.py:37
  39.5 21.9 %collective-permute-start.3 = (bf16[3,2,128,256]{3,2,0,1:T(8,128)(2,1)S(1)}, bf16[3,2,128,256]{3,2,0,1:T(8,128)(2,1)S(1)}, u32[]{:S(2)}, u32[]{:S(2)}) collective-permute-start(bf16[3,2,128,256]{3,2,0,1:T(8,128)(2,1)S(1)} %collective-permute-done.2), channel_id=1, source_target_pairs={{0,240},{16,0},{32,16},{48,32},{64,48},{80,64},{96,80},{112,96},{1... | collective-permute-start | bytes 1179656 | tf_op jit(solution)/shard_map/ppermute | solution.py:38
  44.9 21.4 %collective-permute-start.10 = (bf16[3,2,128,256]{3,2,0,1:T(8,128)(2,1)S(1)}, bf16[3,2,128,256]{3,2,0,1:T(8,128)(2,1)S(1)}, u32[]{:S(2)}, u32[]{:S(2)}) collective-permute-start(bf16[3,2,128,256]{3,2,0,1:T(8,128)(2,1)S(1)} %collective-permute-done.9), channel_id=1, source_target_pairs={{0,16},{16,32},{32,48},{48,64},{64,80},{80,96},{96,112},{112,128},... | collective-permute-start | bytes 1179656 | tf_op jit(solution)/shard_map/ppermute | solution.py:37
  48.3 19.9 %copy-start.1 = (s32[1,512]{1,0:T(1,128)S(1)}, s32[1,512]{1,0:T(1,128)}, u32[]{:S(2)}) copy-start(s32[1,512]{1,0:T(1,128)} %param.11) | copy-start | bytes 6148
  48.3 20.0 %copy-start = (f32[16,7]{0,1:T(8,128)S(1)}, f32[16,7]{0,1:T(8,128)}, u32[]{:S(2)}) copy-start(f32[16,7]{0,1:T(8,128)} %param.10) | copy-start | bytes 1348
  50.8 99.9 %all-to-all-start = ((bf16[16,32,4096]{2,1,0:T(8,128)(2,1)}), bf16[16,32,4096]{2,1,0:T(8,128)(2,1)}, u32[]{:S(2)}, u32[]{:S(2)}) async-start(bf16[16,32,4096]{2,1,0:T(8,128)(2,1)} %broadcast_in_dim.9), calls=%async_computation | async-start | bytes 8388608 | tf_op jit(solution)/shard_map/all_to_all | solution.py:68
  61.4 13.2 %collective-permute-start.4 = (bf16[3,2,128,256]{3,2,0,1:T(8,128)(2,1)S(1)}, bf16[3,2,128,256]{3,2,0,1:T(8,128)(2,1)}, u32[]{:S(2)}, u32[]{:S(2)}) collective-permute-start(bf16[3,2,128,256]{3,2,0,1:T(8,128)(2,1)S(1)} %collective-permute-done.3), channel_id=1, source_target_pairs={{0,240},{16,0},{32,16},{48,32},{64,48},{80,64},{96,80},{112,96},{1... | collective-permute-start | bytes 1179656 | tf_op jit(solution)/shard_map/ppermute | solution.py:38
  66.3 13.8 %collective-permute-start.11 = (bf16[3,2,128,256]{3,2,0,1:T(8,128)(2,1)S(1)}, bf16[3,2,128,256]{3,2,0,1:T(8,128)(2,1)S(1)}, u32[]{:S(2)}, u32[]{:S(2)}) collective-permute-start(bf16[3,2,128,256]{3,2,0,1:T(8,128)(2,1)S(1)} %collective-permute-done.10), channel_id=1, source_target_pairs={{0,16},{16,32},{32,48},{48,64},{64,80},{80,96},{96,112},{112,128},... | collective-permute-start | bytes 1179656 | tf_op jit(solution)/shard_map/ppermute | solution.py:37
  74.6 13.2 %collective-permute-start.5 = (bf16[3,2,128,256]{3,2,0,1:T(8,128)(2,1)}, bf16[3,2,128,256]{3,2,0,1:T(8,128)(2,1)S(1)}, u32[]{:S(2)}, u32[]{:S(2)}) collective-permute-start(bf16[3,2,128,256]{3,2,0,1:T(8,128)(2,1)} %collective-permute-done.4), channel_id=1, source_target_pairs={{0,240},{16,0},{32,16},{48,32},{64,48},{80,64},{96,80},{112,96},{1... | collective-permute-start | bytes 1179656 | tf_op jit(solution)/shard_map/ppermute | solution.py:38
  80.0 13.1 %collective-permute-start.12 = (bf16[3,2,128,256]{3,2,0,1:T(8,128)(2,1)S(1)}, bf16[3,2,128,256]{3,2,0,1:T(8,128)(2,1)S(1)}, u32[]{:S(2)}, u32[]{:S(2)}) collective-permute-start(bf16[3,2,128,256]{3,2,0,1:T(8,128)(2,1)S(1)} %collective-permute-done.11), channel_id=1, source_target_pairs={{0,16},{16,32},{32,48},{48,64},{64,80},{80,96},{96,112},{112,128},... | collective-permute-start | bytes 1179656 | tf_op jit(solution)/shard_map/ppermute | solution.py:37
  87.8 11.9 %collective-permute-start.6 = (bf16[3,2,128,256]{3,2,0,1:T(8,128)(2,1)S(1)}, bf16[3,2,128,256]{3,2,0,1:T(8,128)(2,1)S(1)}, u32[]{:S(2)}, u32[]{:S(2)}) collective-permute-start(bf16[3,2,128,256]{3,2,0,1:T(8,128)(2,1)S(1)} %collective-permute-done.5), channel_id=1, source_target_pairs={{0,240},{16,0},{32,16},{48,32},{64,48},{80,64},{96,80},{112,96},{1... | collective-permute-start | bytes 1179656 | tf_op jit(solution)/shard_map/ppermute | solution.py:38
  93.1 12.0 %collective-permute-start.13 = (bf16[3,2,128,256]{3,2,0,1:T(8,128)(2,1)S(1)}, bf16[3,2,128,256]{3,2,0,1:T(8,128)(2,1)S(1)}, u32[]{:S(2)}, u32[]{:S(2)}) collective-permute-start(bf16[3,2,128,256]{3,2,0,1:T(8,128)(2,1)S(1)} %collective-permute-done.12), channel_id=1, source_target_pairs={{0,16},{16,32},{32,48},{48,64},{64,80},{80,96},{96,112},{112,128},... | collective-permute-start | bytes 1179656 | tf_op jit(solution)/shard_map/ppermute | solution.py:37
  99.7 18.2 %collective-permute-start.7 = (bf16[3,2,128,256]{3,2,0,1:T(8,128)(2,1)S(1)}, bf16[3,2,128,256]{3,2,0,1:T(8,128)(2,1)S(1)}, u32[]{:S(2)}, u32[]{:S(2)}) collective-permute-start(bf16[3,2,128,256]{3,2,0,1:T(8,128)(2,1)S(1)} %collective-permute-done.6), channel_id=1, source_target_pairs={{0,240},{16,0},{32,16},{48,32},{64,48},{80,64},{96,80},{112,96},{1... | collective-permute-start | bytes 1179656 | tf_op jit(solution)/shard_map/ppermute | solution.py:38
  105.1 10.8 %collective-permute-start.14 = (bf16[3,2,128,256]{3,2,0,1:T(8,128)(2,1)S(1)}, bf16[3,2,128,256]{3,2,0,1:T(8,128)(2,1)S(1)}, u32[]{:S(2)}, u32[]{:S(2)}) collective-permute-start(bf16[3,2,128,256]{3,2,0,1:T(8,128)(2,1)S(1)} %collective-permute-done.13), channel_id=1, source_target_pairs={{0,16},{16,32},{32,48},{48,64},{64,80},{80,96},{96,112},{112,128},... | collective-permute-start | bytes 1179656 | tf_op jit(solution)/shard_map/ppermute | solution.py:37
  116.0 7.6 %collective-permute-start.15 = (bf16[3,1,128,256]{3,2,0,1:T(8,128)(2,1)S(1)}, bf16[3,1,128,256]{3,2,0,1:T(8,128)(2,1)S(1)}, u32[]{:S(2)}, u32[]{:S(2)}) collective-permute-start(bf16[3,1,128,256]{3,2,0,1:T(8,128)(2,1)S(1)} %slice.96), channel_id=1, source_target_pairs={{0,16},{16,32},{32,48},{48,64},{64,80},{80,96},{96,112},{112,128},... | collective-permute-start | bytes 589832 | tf_op jit(solution)/shard_map/ppermute | solution.py:41
  118.0 7.2 %collective-permute-start.16 = (bf16[3,1,128,256]{3,2,0,1:T(8,128)(2,1)S(1)}, bf16[3,1,128,256]{3,2,0,1:T(8,128)(2,1)S(1)}, u32[]{:S(2)}, u32[]{:S(2)}) collective-permute-start(bf16[3,1,128,256]{3,2,0,1:T(8,128)(2,1)S(1)} %slice.97), channel_id=1, source_target_pairs={{0,240},{16,0},{32,16},{48,32},{64,48},{80,64},{96,80},{112,96},{1... | collective-permute-start | bytes 589832 | tf_op jit(solution)/shard_map/ppermute | solution.py:42
  150.7 8.2 %copy-start.2 = (s32[1,16]{1,0:T(1,128)S(1)}, s32[1,16]{1,0:T(1,128)}, u32[]{:S(2)}) copy-start(s32[1,16]{1,0:T(1,128)} %param.12) | copy-start | bytes 196
  159.7 17.8 %all-to-all-start.2 = ((f32[16,1,16]{2,1,0:T(1,128)}), f32[16,1,16]{2,1,0:T(1,128)S(1)}, u32[]{:S(2)}, u32[]{:S(2)}) async-start(f32[16,1,16]{2,1,0:T(1,128)} %broadcast_in_dim.11), calls=%async_computation.2 | async-start | bytes 16384 | tf_op jit(solution)/shard_map/all_to_all | solution.py:85
  177.5 12.7 %all-to-all-start.1 = ((bf16[16,32,256]{2,1,0:T(8,128)(2,1)}), bf16[16,32,256]{2,1,0:T(8,128)(2,1)S(1)}, u32[]{:S(2)}, u32[]{:S(2)}) async-start(bf16[16,32,256]{2,1,0:T(8,128)(2,1)} %bitcast.31), calls=%async_computation.1 | async-start | bytes 524288 | tf_op jit(solution)/shard_map/all_to_all | solution.py:90

commit v3 on v2

--- a/solution.py
+++ b/solution.py
@@ -3,6 +3,7 @@
 import jax
 import jax.numpy as jnp
 from jax import lax
+from jax.experimental.layout import Layout, with_layout_constraint
 from jax.sharding import PartitionSpec as P
 
 EPSILON = 1e-06
@@ -42,7 +43,7 @@
     last_b = lax.ppermute(left[:, 1:], "fsdp", z_down)
     ahead.append(jnp.concatenate([last_a, last_b], axis=1))
     pieces = ahead + behind[::-1]
-    stacked = jnp.stack(pieces, axis=2)
+    stacked = with_layout_constraint(jnp.stack(pieces, axis=2), Layout((0, 1, 2, 3, 4)))
     return stacked.reshape(
         proj_weight.shape[0], fsdp_size * proj_weight.shape[1], proj_weight.shape[2]
     )
@@ -69,6 +70,7 @@
         tp_size * local_rows, model_width
     )
     projected = jnp.einsum("sk,ikc->isc", slab_rows, weights, preferred_element_type=jnp.float32)
+    projected = with_layout_constraint(projected, Layout((0, 1, 2)))
     gated_prod = projected[1] * projected[2]
     tap_table = jnp.repeat(short_filter, channels // short_filter.shape[0], axis=0)
     filtered = short_conv(gated_prod, tap_table, segment_ids[0])
@@ -82,13 +84,24 @@
     picked = jnp.dot(picker, mixed_local, preferred_element_type=jnp.float32)
     own_readout = lax.dynamic_slice_in_dim(readout, device_rank * channels, channels, 0)
     partial_sum = jnp.sum(picked * own_readout[None, :], axis=1)
-    partials = lax.all_to_all(
-        jnp.broadcast_to(partial_sum[None], (tp_size,) + partial_sum.shape), "tp", 0, 0, tiled=False
+    high = partial_sum.astype(jnp.bfloat16)
+    low = (partial_sum - high.astype(jnp.float32)).astype(jnp.bfloat16)
+    extra_rows = 16
+    extra = jnp.zeros((extra_rows, channels), jnp.bfloat16)
+    extra = extra.at[0, : high.shape[0]].set(high).at[1, : low.shape[0]].set(low)
+    blocks = mixed_local.reshape(tp_size, local_rows, channels)
+    payload = jnp.concatenate(
+        [blocks, jnp.broadcast_to(extra[None], (tp_size, extra_rows, channels))], axis=1
     )
-    needle_score = (jnp.sum(partials, axis=0) / math.sqrt(model_width))[None, :]
-    blocks = mixed_local.reshape(tp_size, local_rows, channels)
-    gathered = lax.all_to_all(blocks, "tp", 0, 0, tiled=False)
-    own_rows = jnp.transpose(gathered, (1, 0, 2)).reshape(local_rows, tp_size * channels)
+    gathered = lax.all_to_all(payload, "tp", 0, 0, tiled=False)
+    own_rows = jnp.transpose(gathered[:, :local_rows], (1, 0, 2)).reshape(
+        local_rows, tp_size * channels
+    )
+    count = positions.shape[0]
+    received = gathered[:, local_rows, :count].astype(jnp.float32) + gathered[
+        :, local_rows + 1, :count
+    ].astype(jnp.float32)
+    needle_score = (jnp.sum(received, axis=0) / math.sqrt(model_width))[None, :]
     return (own_rows, needle_score)
 
 

time: 192 us -> 163 us (0.85)
  blocking collectives: 0 us -> 20.5 us
  local copies, waits for them, and re-layouts: 36.9 us -> 16.6 us
  starting transfers between devices: 93.5 us -> 78.7 us
  waiting for transfers between devices: 45.5 us -> 31.1 us
    all_to_all x0 -> x1, blocking collectives: none -> 20.5 us  [local(): gathered = lax.all_to_all(payload, 'tp', 0, 0, tiled=False)]
    all_to_all x2 -> x0, starting transfers between devices: 14.8 us -> none  [the longest x1 10.8 us: local(): lax.all_to_all(jnp.broadcast_to(partial_sum[None], (tp_size,) + partial_s...]
    all_to_all x2 -> x0, waiting for transfers between devices: 14.4 us -> none  [the longest x1 8.21 us: local(): gathered = lax.all_to_all(blocks, 'tp', 0, 0, tiled=False)]
    reshape x2 -> x1, local copies, waits for them, and re-layouts: 11 us -> 0.72 us  [local(): jnp.transpose(gathered[:, :local_rows], (1, 0, 2))]
    another operation x2 -> x1, local copies, waits for them, and re-layouts: 9.71 us -> 0.78 us  [gather_weights(): jnp.stack(pieces, axis=2)]
    unnamed x21 -> x22, local copies, waits for them, and re-layouts: 11.3 us -> 11.4 us
  transfers between devices with their start and end apart: 20 -> 18, of which waited for: 11 -> 9; matrix products, arithmetic and copies ran while one was open for 21% -> 12% of each run, Pallas kernels for 0% -> 0%
where the time goes in v3:
time: 163 us; the launch traced here: 162 us
  starting transfers between devices  78.7 us (48%)
  waiting for transfers between devices  31.1 us (19%)
  blocking collectives  20.5 us (13%)
  local copies, waits for them, and re-layouts  16.6 us (10%)
  matrix products  7.34 us (5%)
  other arithmetic  6.53 us (4%)
    ppermute x7, starting transfers between devices, gather_weights(): left = lax.ppermute(left, 'fsdp', z_down)  44.2 us
    all_to_all x1, blocking collectives, local(): gathered = lax.all_to_all(payload, 'tp', 0, 0, tiled=False)  20.5 us
    ppermute x7, waiting for transfers between devices, gather_weights(): left = lax.ppermute(left, 'fsdp', z_down)  18.7 us
    ppermute x7, starting transfers between devices, gather_weights(): right = lax.ppermute(right, 'fsdp', z_up)  13.4 us
    unnamed x22, local copies, waits for them, and re-layouts  11.4 us
    all_to_all x1, starting transfers between devices, local(): lax.all_to_all(spread, 'tp', 0, 0, tiled=False)  10.6 us
    ppermute x7, waiting for transfers between devices, gather_weights(): right = lax.ppermute(right, 'fsdp', z_up)  7.38 us
    dot_general x1, matrix products, local(): jnp.einsum('sk,ikc->isc', slab_rows, weights, preferred_element_type=jnp....  7.04 us
  transfers between devices with their start and end apart: 18, of which 9 were waited for; matrix products, arithmetic and copies ran while one was open for 12% of the time, Pallas kernels for 0%

profile of v3, /device:TPU:1, one launch (start us, length us, event | category | flops | bytes accessed | tf_op | source)
XLA Modules:
  0.0 161.8 jit_solution(8924427992532953752)
XLA Ops:
  0.6 3.9 %collective-permute-start = (bf16[3,128,256]{2,1,0:T(8,128)(2,1)}, bf16[3,128,256]{2,1,0:T(8,128)(2,1)S(1)}, u32[]{:S(2)}, u32[]{:S(2)}) collective-permute-start(bf16[3,128,256]{2,1,0:T(8,128)(2,1)} %param.13), channel_id=1, source_target_pairs={{0,256},{16,272},{32,288},{48,304},{64,320},{80,336},{96,352},{112... | collective-permute-start | bytes 589832 | tf_op jit(solution)/shard_map/ppermute | solution.py:29
  4.6 3.2 %collective-permute-done = bf16[3,128,256]{2,1,0:T(8,128)(2,1)S(1)} collective-permute-done((bf16[3,128,256]{2,1,0:T(8,128)(2,1)}, bf16[3,128,256]{2,1,0:T(8,128)(2,1)S(1)}, u32[]{:S(2)}, u32[]{:S(2)}) %collective-permute-start) | collective-permute-done | bytes 196640 | tf_op jit(solution)/shard_map/ppermute | solution.py:29
  8.8 12.6 %collective-permute-start.1 = (bf16[3,2,128,256]{3,2,1,0:T(8,128)(2,1)S(1)}, bf16[3,2,128,256]{3,2,1,0:T(8,128)(2,1)S(1)}, u32[]{:S(2)}, u32[]{:S(2)}) collective-permute-start(bf16[3,2,128,256]{3,2,1,0:T(8,128)(2,1)S(1)} %pad_maximum_fusion), channel_id=1, source_target_pairs={{0,240},{16,0},{32,16},{48,32},{64,48},{80,64},{96,80},{112,96},{1... | collective-permute-start | bytes 1179656 | tf_op jit(solution)/shard_map/ppermute | solution.py:39
  21.5 1.9 %collective-permute-start.8 = (bf16[3,2,128,256]{3,2,1,0:T(8,128)(2,1)S(1)}, bf16[3,2,128,256]{3,2,1,0:T(8,128)(2,1)S(1)}, u32[]{:S(2)}, u32[]{:S(2)}) collective-permute-start(bf16[3,2,128,256]{3,2,1,0:T(8,128)(2,1)S(1)} %pad_maximum_fusion), channel_id=1, source_target_pairs={{0,16},{16,32},{32,48},{48,64},{64,80},{80,96},{96,112},{112,128},... | collective-permute-start | bytes 1179656 | tf_op jit(solution)/shard_map/ppermute | solution.py:38
  23.4 4.9 %collective-permute-done.1 = bf16[3,2,128,256]{3,2,1,0:T(8,128)(2,1)S(1)} collective-permute-done((bf16[3,2,128,256]{3,2,1,0:T(8,128)(2,1)S(1)}, bf16[3,2,128,256]{3,2,1,0:T(8,128)(2,1)S(1)}, u32[]{:S(2)}, u32[]{:S(2)}) %collective-permute-start.1) | collective-permute-done | bytes 393248 | tf_op jit(solution)/shard_map/ppermute | solution.py:39
  28.3 5.3 %collective-permute-start.2 = (bf16[3,2,128,256]{3,2,1,0:T(8,128)(2,1)S(1)}, bf16[3,2,128,256]{3,2,1,0:T(8,128)(2,1)S(1)}, u32[]{:S(2)}, u32[]{:S(2)}) collective-permute-start(bf16[3,2,128,256]{3,2,1,0:T(8,128)(2,1)S(1)} %collective-permute-done.1), channel_id=1, source_target_pairs={{0,240},{16,0},{32,16},{48,32},{64,48},{80,64},{96,80},{112,96},{1... | collective-permute-start | bytes 1179656 | tf_op jit(solution)/shard_map/ppermute | solution.py:39
  36.7 2.9 %collective-permute-done.2 = bf16[3,2,128,256]{3,2,1,0:T(8,128)(2,1)S(1)} collective-permute-done((bf16[3,2,128,256]{3,2,1,0:T(8,128)(2,1)S(1)}, bf16[3,2,128,256]{3,2,1,0:T(8,128)(2,1)S(1)}, u32[]{:S(2)}, u32[]{:S(2)}) %collective-permute-start.2) | collective-permute-done | bytes 393248 | tf_op jit(solution)/shard_map/ppermute | solution.py:39
  39.5 5.3 %collective-permute-start.3 = (bf16[3,2,128,256]{3,2,1,0:T(8,128)(2,1)S(1)}, bf16[3,2,128,256]{3,2,1,0:T(8,128)(2,1)S(1)}, u32[]{:S(2)}, u32[]{:S(2)}) collective-permute-start(bf16[3,2,128,256]{3,2,1,0:T(8,128)(2,1)S(1)} %collective-permute-done.2), channel_id=1, source_target_pairs={{0,240},{16,0},{32,16},{48,32},{64,48},{80,64},{96,80},{112,96},{1... | collective-permute-start | bytes 1179656 | tf_op jit(solution)/shard_map/ppermute | solution.py:39
  48.3 2.6 %broadcast_in_dim.9 = bf16[16,32,4096]{2,1,0:T(8,128)(2,1)} broadcast(bf16[32,4096]{1,0:T(8,128)(2,1)S(1)} %bitcast.119), dimensions={1,2} | broadcast | bytes 4456448 | tf_op jit(solution)/shard_map/broadcast_in_dim | solution.py:68
  50.9 10.6 %all-to-all-start = ((bf16[16,32,4096]{2,1,0:T(8,128)(2,1)}), bf16[16,32,4096]{2,1,0:T(8,128)(2,1)}, u32[]{:S(2)}, u32[]{:S(2)}) async-start(bf16[16,32,4096]{2,1,0:T(8,128)(2,1)} %broadcast_in_dim.9), calls=%async_computation | async-start | bytes 8388608 | tf_op jit(solution)/shard_map/all_to_all | solution.py:69
  61.5 4.9 %collective-permute-start.4 = (bf16[3,2,128,256]{3,2,1,0:T(8,128)(2,1)S(1)}, bf16[3,2,128,256]{3,2,1,0:T(8,128)(2,1)}, u32[]{:S(2)}, u32[]{:S(2)}) collective-permute-start(bf16[3,2,128,256]{3,2,1,0:T(8,128)(2,1)S(1)} %collective-permute-done.3), channel_id=1, source_target_pairs={{0,240},{16,0},{32,16},{48,32},{64,48},{80,64},{96,80},{112,96},{1... | collective-permute-start | bytes 1179656 | tf_op jit(solution)/shard_map/ppermute | solution.py:39
  66.4 1.9 %collective-permute-start.11 = (bf16[3,2,128,256]{3,2,1,0:T(8,128)(2,1)S(1)}, bf16[3,2,128,256]{3,2,1,0:T(8,128)(2,1)S(1)}, u32[]{:S(2)}, u32[]{:S(2)}) collective-permute-start(bf16[3,2,128,256]{3,2,1,0:T(8,128)(2,1)S(1)} %collective-permute-done.10), channel_id=1, source_target_pairs={{0,16},{16,32},{32,48},{48,64},{64,80},{80,96},{96,112},{112,128},... | collective-permute-start | bytes 1179656 | tf_op jit(solution)/shard_map/ppermute | solution.py:38
  70.2 4.6 %collective-permute-done.4 = bf16[3,2,128,256]{3,2,1,0:T(8,128)(2,1)} collective-permute-done((bf16[3,2,128,256]{3,2,1,0:T(8,128)(2,1)S(1)}, bf16[3,2,128,256]{3,2,1,0:T(8,128)(2,1)}, u32[]{:S(2)}, u32[]{:S(2)}) %collective-permute-start.4) | collective-permute-done | bytes 393248 | tf_op jit(solution)/shard_map/ppermute | solution.py:39
  74.7 5.4 %collective-permute-start.5 = (bf16[3,2,128,256]{3,2,1,0:T(8,128)(2,1)}, bf16[3,2,128,256]{3,2,1,0:T(8,128)(2,1)S(1)}, u32[]{:S(2)}, u32[]{:S(2)}) collective-permute-start(bf16[3,2,128,256]{3,2,1,0:T(8,128)(2,1)} %collective-permute-done.4), channel_id=1, source_target_pairs={{0,240},{16,0},{32,16},{48,32},{64,48},{80,64},{96,80},{112,96},{1... | collective-permute-start | bytes 1179656 | tf_op jit(solution)/shard_map/ppermute | solution.py:39
  83.7 4.2 %collective-permute-done.5 = bf16[3,2,128,256]{3,2,1,0:T(8,128)(2,1)S(1)} collective-permute-done((bf16[3,2,128,256]{3,2,1,0:T(8,128)(2,1)}, bf16[3,2,128,256]{3,2,1,0:T(8,128)(2,1)S(1)}, u32[]{:S(2)}, u32[]{:S(2)}) %collective-permute-start.5) | collective-permute-done | bytes 393248 | tf_op jit(solution)/shard_map/ppermute | solution.py:39
  87.9 5.3 %collective-permute-start.6 = (bf16[3,2,128,256]{3,2,1,0:T(8,128)(2,1)S(1)}, bf16[3,2,128,256]{3,2,1,0:T(8,128)(2,1)S(1)}, u32[]{:S(2)}, u32[]{:S(2)}) collective-permute-start(bf16[3,2,128,256]{3,2,1,0:T(8,128)(2,1)S(1)} %collective-permute-done.5), channel_id=1, source_target_pairs={{0,240},{16,0},{32,16},{48,32},{64,48},{80,64},{96,80},{112,96},{1... | collective-permute-start | bytes 1179656 | tf_op jit(solution)/shard_map/ppermute | solution.py:39
  97.8 2.1 %collective-permute-done.6 = bf16[3,2,128,256]{3,2,1,0:T(8,128)(2,1)S(1)} collective-permute-done((bf16[3,2,128,256]{3,2,1,0:T(8,128)(2,1)S(1)}, bf16[3,2,128,256]{3,2,1,0:T(8,128)(2,1)S(1)}, u32[]{:S(2)}, u32[]{:S(2)}) %collective-permute-start.6) | collective-permute-done | bytes 393248 | tf_op jit(solution)/shard_map/ppermute | solution.py:39
  99.8 5.4 %collective-permute-start.7 = (bf16[3,2,128,256]{3,2,1,0:T(8,128)(2,1)S(1)}, bf16[3,2,128,256]{3,2,1,0:T(8,128)(2,1)S(1)}, u32[]{:S(2)}, u32[]{:S(2)}) collective-permute-start(bf16[3,2,128,256]{3,2,1,0:T(8,128)(2,1)S(1)} %collective-permute-done.6), channel_id=1, source_target_pairs={{0,240},{16,0},{32,16},{48,32},{64,48},{80,64},{96,80},{112,96},{1... | collective-permute-start | bytes 1179656 | tf_op jit(solution)/shard_map/ppermute | solution.py:39
  105.3 1.9 %collective-permute-start.14 = (bf16[3,2,128,256]{3,2,1,0:T(8,128)(2,1)S(1)}, bf16[3,2,128,256]{3,2,1,0:T(8,128)(2,1)S(1)}, u32[]{:S(2)}, u32[]{:S(2)}) collective-permute-start(bf16[3,2,128,256]{3,2,1,0:T(8,128)(2,1)S(1)} %collective-permute-done.13), channel_id=1, source_target_pairs={{0,16},{16,32},{32,48},{48,64},{64,80},{80,96},{96,112},{112,128},... | collective-permute-start | bytes 1179656 | tf_op jit(solution)/shard_map/ppermute | solution.py:38
  108.8 7.4 %collective-permute-done.14 = bf16[3,2,128,256]{3,2,1,0:T(8,128)(2,1)S(1)} collective-permute-done((bf16[3,2,128,256]{3,2,1,0:T(8,128)(2,1)S(1)}, bf16[3,2,128,256]{3,2,1,0:T(8,128)(2,1)S(1)}, u32[]{:S(2)}, u32[]{:S(2)}) %collective-permute-start.14) | collective-permute-done | bytes 393248 | tf_op jit(solution)/shard_map/ppermute | solution.py:38
  116.1 1.9 %collective-permute-start.15 = (bf16[3,1,128,256]{3,2,1,0:T(8,128)(2,1)S(1)}, bf16[3,1,128,256]{3,2,1,0:T(8,128)(2,1)S(1)}, u32[]{:S(2)}, u32[]{:S(2)}) collective-permute-start(bf16[3,1,128,256]{3,2,1,0:T(8,128)(2,1)S(1)} %slice.143), channel_id=1, source_target_pairs={{0,16},{16,32},{32,48},{48,64},{64,80},{80,96},{96,112},{112,128},... | collective-permute-start | bytes 589832 | tf_op jit(solution)/shard_map/ppermute | solution.py:42
  118.1 4.6 %collective-permute-start.16 = (bf16[3,1,128,256]{3,2,1,0:T(8,128)(2,1)S(1)}, bf16[3,1,128,256]{3,2,1,0:T(8,128)(2,1)S(1)}, u32[]{:S(2)}, u32[]{:S(2)}) collective-permute-start(bf16[3,1,128,256]{3,2,1,0:T(8,128)(2,1)S(1)} %slice.144), channel_id=1, source_target_pairs={{0,240},{16,0},{32,16},{48,32},{64,48},{80,64},{96,80},{112,96},{1... | collective-permute-start | bytes 589832 | tf_op jit(solution)/shard_map/ppermute | solution.py:43
  131.5 7.0 %convolution_bitcast_fusion = f32[3,512,256]{2,1,0:T(8,128)S(1)} fusion(bf16[512,4096,1]{1,0,2:T(8,128)(2,1)} %bitcast.36, bf16[3,4096,256]{2,1,0:T(8,128)(2,1)} %bitcast.34), kind=kOutput, calls=%fused_computation | convolution fusion | flops 3221225472 | bytes 12058624 | tf_op jit(solution)/shard_map/sk,ikc->isc/dot_general | solution.py:72
  140.1 20.5 %all_to_all.10 = bf16[16,48,256]{2,1,0:T(8,128)(2,1)S(1)} all-to-all(bf16[16,48,256]{2,1,0:T(8,128)(2,1)S(1)} %pad_maximum_fusion.1), channel_id=1, replica_groups=mesh['fsdp'=32,'tp'=16] {'tp'}, dimensions={0} | all-to-all | bytes 786432 | tf_op jit(solution)/shard_map/all_to_all | solution.py:96
  (65 shorter events, 30.4 us)
Async XLA Ops:
  0.6 7.2 %collective-permute-start = (bf16[3,128,256]{2,1,0:T(8,128)(2,1)}, bf16[3,128,256]{2,1,0:T(8,128)(2,1)S(1)}, u32[]{:S(2)}, u32[]{:S(2)}) collective-permute-start(bf16[3,128,256]{2,1,0:T(8,128)(2,1)} %param.13), channel_id=1, source_target_pairs={{0,256},{16,272},{32,288},{48,304},{64,320},{80,336},{96,352},{112... | collective-permute-start | bytes 589832 | tf_op jit(solution)/shard_map/ppermute | solution.py:29
  8.8 19.5 %collective-permute-start.1 = (bf16[3,2,128,256]{3,2,1,0:T(8,128)(2,1)S(1)}, bf16[3,2,128,256]{3,2,1,0:T(8,128)(2,1)S(1)}, u32[]{:S(2)}, u32[]{:S(2)}) collective-permute-start(bf16[3,2,128,256]{3,2,1,0:T(8,128)(2,1)S(1)} %pad_maximum_fusion), channel_id=1, source_target_pairs={{0,240},{16,0},{32,16},{48,32},{64,48},{80,64},{96,80},{112,96},{1... | collective-permute-start | bytes 1179656 | tf_op jit(solution)/shard_map/ppermute | solution.py:39
  21.5 12.2 %collective-permute-start.8 = (bf16[3,2,128,256]{3,2,1,0:T(8,128)(2,1)S(1)}, bf16[3,2,128,256]{3,2,1,0:T(8,128)(2,1)S(1)}, u32[]{:S(2)}, u32[]{:S(2)}) collective-permute-start(bf16[3,2,128,256]{3,2,1,0:T(8,128)(2,1)S(1)} %pad_maximum_fusion), channel_id=1, source_target_pairs={{0,16},{16,32},{32,48},{48,64},{64,80},{80,96},{96,112},{112,128},... | collective-permute-start | bytes 1179656 | tf_op jit(solution)/shard_map/ppermute | solution.py:38
  28.3 11.2 %collective-permute-start.2 = (bf16[3,2,128,256]{3,2,1,0:T(8,128)(2,1)S(1)}, bf16[3,2,128,256]{3,2,1,0:T(8,128)(2,1)S(1)}, u32[]{:S(2)}, u32[]{:S(2)}) collective-permute-start(bf16[3,2,128,256]{3,2,1,0:T(8,128)(2,1)S(1)} %collective-permute-done.1), channel_id=1, source_target_pairs={{0,240},{16,0},{32,16},{48,32},{64,48},{80,64},{96,80},{112,96},{1... | collective-permute-start | bytes 1179656 | tf_op jit(solution)/shard_map/ppermute | solution.py:39
  33.6 11.2 %collective-permute-start.9 = (bf16[3,2,128,256]{3,2,1,0:T(8,128)(2,1)S(1)}, bf16[3,2,128,256]{3,2,1,0:T(8,128)(2,1)S(1)}, u32[]{:S(2)}, u32[]{:S(2)}) collective-permute-start(bf16[3,2,128,256]{3,2,1,0:T(8,128)(2,1)S(1)} %collective-permute-done.8), channel_id=1, source_target_pairs={{0,16},{16,32},{32,48},{48,64},{64,80},{80,96},{96,112},{112,128},... | collective-permute-start | bytes 1179656 | tf_op jit(solution)/shard_map/ppermute | solution.py:38
  39.5 22.0 %collective-permute-start.3 = (bf16[3,2,128,256]{3,2,1,0:T(8,128)(2,1)S(1)}, bf16[3,2,128,256]{3,2,1,0:T(8,128)(2,1)S(1)}, u32[]{:S(2)}, u32[]{:S(2)}) collective-permute-start(bf16[3,2,128,256]{3,2,1,0:T(8,128)(2,1)S(1)} %collective-permute-done.2), channel_id=1, source_target_pairs={{0,240},{16,0},{32,16},{48,32},{64,48},{80,64},{96,80},{112,96},{1... | collective-permute-start | bytes 1179656 | tf_op jit(solution)/shard_map/ppermute | solution.py:39
  44.9 21.5 %collective-permute-start.10 = (bf16[3,2,128,256]{3,2,1,0:T(8,128)(2,1)S(1)}, bf16[3,2,128,256]{3,2,1,0:T(8,128)(2,1)S(1)}, u32[]{:S(2)}, u32[]{:S(2)}) collective-permute-start(bf16[3,2,128,256]{3,2,1,0:T(8,128)(2,1)S(1)} %collective-permute-done.9), channel_id=1, source_target_pairs={{0,16},{16,32},{32,48},{48,64},{64,80},{80,96},{96,112},{112,128},... | collective-permute-start | bytes 1179656 | tf_op jit(solution)/shard_map/ppermute | solution.py:38
  48.3 20.0 %copy-start.1 = (s32[1,512]{1,0:T(1,128)S(1)}, s32[1,512]{1,0:T(1,128)}, u32[]{:S(2)}) copy-start(s32[1,512]{1,0:T(1,128)} %param.15) | copy-start | bytes 6148
  48.3 20.1 %copy-start = (f32[16,7]{0,1:T(8,128)S(1)}, f32[16,7]{0,1:T(8,128)}, u32[]{:S(2)}) copy-start(f32[16,7]{0,1:T(8,128)} %param.14) | copy-start | bytes 1348
  50.9 80.6 %all-to-all-start = ((bf16[16,32,4096]{2,1,0:T(8,128)(2,1)}), bf16[16,32,4096]{2,1,0:T(8,128)(2,1)}, u32[]{:S(2)}, u32[]{:S(2)}) async-start(bf16[16,32,4096]{2,1,0:T(8,128)(2,1)} %broadcast_in_dim.9), calls=%async_computation | async-start | bytes 8388608 | tf_op jit(solution)/shard_map/all_to_all | solution.py:69
  61.5 13.2 %collective-permute-start.4 = (bf16[3,2,128,256]{3,2,1,0:T(8,128)(2,1)S(1)}, bf16[3,2,128,256]{3,2,1,0:T(8,128)(2,1)}, u32[]{:S(2)}, u32[]{:S(2)}) collective-permute-start(bf16[3,2,128,256]{3,2,1,0:T(8,128)(2,1)S(1)} %collective-permute-done.3), channel_id=1, source_target_pairs={{0,240},{16,0},{32,16},{48,32},{64,48},{80,64},{96,80},{112,96},{1... | collective-permute-start | bytes 1179656 | tf_op jit(solution)/shard_map/ppermute | solution.py:39
  66.4 13.8 %collective-permute-start.11 = (bf16[3,2,128,256]{3,2,1,0:T(8,128)(2,1)S(1)}, bf16[3,2,128,256]{3,2,1,0:T(8,128)(2,1)S(1)}, u32[]{:S(2)}, u32[]{:S(2)}) collective-permute-start(bf16[3,2,128,256]{3,2,1,0:T(8,128)(2,1)S(1)} %collective-permute-done.10), channel_id=1, source_target_pairs={{0,16},{16,32},{32,48},{48,64},{64,80},{80,96},{96,112},{112,128},... | collective-permute-start | bytes 1179656 | tf_op jit(solution)/shard_map/ppermute | solution.py:38
  74.7 13.2 %collective-permute-start.5 = (bf16[3,2,128,256]{3,2,1,0:T(8,128)(2,1)}, bf16[3,2,128,256]{3,2,1,0:T(8,128)(2,1)S(1)}, u32[]{:S(2)}, u32[]{:S(2)}) collective-permute-start(bf16[3,2,128,256]{3,2,1,0:T(8,128)(2,1)} %collective-permute-done.4), channel_id=1, source_target_pairs={{0,240},{16,0},{32,16},{48,32},{64,48},{80,64},{96,80},{112,96},{1... | collective-permute-start | bytes 1179656 | tf_op jit(solution)/shard_map/ppermute | solution.py:39
  80.2 13.1 %collective-permute-start.12 = (bf16[3,2,128,256]{3,2,1,0:T(8,128)(2,1)S(1)}, bf16[3,2,128,256]{3,2,1,0:T(8,128)(2,1)S(1)}, u32[]{:S(2)}, u32[]{:S(2)}) collective-permute-start(bf16[3,2,128,256]{3,2,1,0:T(8,128)(2,1)S(1)} %collective-permute-done.11), channel_id=1, source_target_pairs={{0,16},{16,32},{32,48},{48,64},{64,80},{80,96},{96,112},{112,128},... | collective-permute-start | bytes 1179656 | tf_op jit(solution)/shard_map/ppermute | solution.py:38
  87.9 11.9 %collective-permute-start.6 = (bf16[3,2,128,256]{3,2,1,0:T(8,128)(2,1)S(1)}, bf16[3,2,128,256]{3,2,1,0:T(8,128)(2,1)S(1)}, u32[]{:S(2)}, u32[]{:S(2)}) collective-permute-start(bf16[3,2,128,256]{3,2,1,0:T(8,128)(2,1)S(1)} %collective-permute-done.5), channel_id=1, source_target_pairs={{0,240},{16,0},{32,16},{48,32},{64,48},{80,64},{96,80},{112,96},{1... | collective-permute-start | bytes 1179656 | tf_op jit(solution)/shard_map/ppermute | solution.py:39
  93.2 12.0 %collective-permute-start.13 = (bf16[3,2,128,256]{3,2,1,0:T(8,128)(2,1)S(1)}, bf16[3,2,128,256]{3,2,1,0:T(8,128)(2,1)S(1)}, u32[]{:S(2)}, u32[]{:S(2)}) collective-permute-start(bf16[3,2,128,256]{3,2,1,0:T(8,128)(2,1)S(1)} %collective-permute-done.12), channel_id=1, source_target_pairs={{0,16},{16,32},{32,48},{48,64},{64,80},{80,96},{96,112},{112,128},... | collective-permute-start | bytes 1179656 | tf_op jit(solution)/shard_map/ppermute | solution.py:38
  99.8 18.2 %collective-permute-start.7 = (bf16[3,2,128,256]{3,2,1,0:T(8,128)(2,1)S(1)}, bf16[3,2,128,256]{3,2,1,0:T(8,128)(2,1)S(1)}, u32[]{:S(2)}, u32[]{:S(2)}) collective-permute-start(bf16[3,2,128,256]{3,2,1,0:T(8,128)(2,1)S(1)} %collective-permute-done.6), channel_id=1, source_target_pairs={{0,240},{16,0},{32,16},{48,32},{64,48},{80,64},{96,80},{112,96},{1... | collective-permute-start | bytes 1179656 | tf_op jit(solution)/shard_map/ppermute | solution.py:39
  105.3 10.8 %collective-permute-start.14 = (bf16[3,2,128,256]{3,2,1,0:T(8,128)(2,1)S(1)}, bf16[3,2,128,256]{3,2,1,0:T(8,128)(2,1)S(1)}, u32[]{:S(2)}, u32[]{:S(2)}) collective-permute-start(bf16[3,2,128,256]{3,2,1,0:T(8,128)(2,1)S(1)} %collective-permute-done.13), channel_id=1, source_target_pairs={{0,16},{16,32},{32,48},{48,64},{64,80},{80,96},{96,112},{112,128},... | collective-permute-start | bytes 1179656 | tf_op jit(solution)/shard_map/ppermute | solution.py:38
  116.1 7.6 %collective-permute-start.15 = (bf16[3,1,128,256]{3,2,1,0:T(8,128)(2,1)S(1)}, bf16[3,1,128,256]{3,2,1,0:T(8,128)(2,1)S(1)}, u32[]{:S(2)}, u32[]{:S(2)}) collective-permute-start(bf16[3,1,128,256]{3,2,1,0:T(8,128)(2,1)S(1)} %slice.143), channel_id=1, source_target_pairs={{0,16},{16,32},{32,48},{48,64},{64,80},{80,96},{96,112},{112,128},... | collective-permute-start | bytes 589832 | tf_op jit(solution)/shard_map/ppermute | solution.py:42
  118.1 7.2 %collective-permute-start.16 = (bf16[3,1,128,256]{3,2,1,0:T(8,128)(2,1)S(1)}, bf16[3,1,128,256]{3,2,1,0:T(8,128)(2,1)S(1)}, u32[]{:S(2)}, u32[]{:S(2)}) collective-permute-start(bf16[3,1,128,256]{3,2,1,0:T(8,128)(2,1)S(1)} %slice.144), channel_id=1, source_target_pairs={{0,240},{16,0},{32,16},{48,32},{64,48},{80,64},{96,80},{112,96},{1... | collective-permute-start | bytes 589832 | tf_op jit(solution)/shard_map/ppermute | solution.py:43
  131.5 8.0 %copy-start.2 = (s32[1,16]{1,0:T(1,128)S(1)}, s32[1,16]{1,0:T(1,128)}, u32[]{:S(2)}) copy-start(s32[1,16]{1,0:T(1,128)} %param.16) | copy-start | bytes 196

commit v4 on v3

--- a/solution.py
+++ b/solution.py
@@ -20,33 +20,38 @@
     return filtered
 
 
-def gather_weights(proj_weight, fsdp_size, z_size):
+def ring_gather(part, fsdp_size, z_size):
     fsdp = lax.axis_index("fsdp")
     x_lo = fsdp // z_size
+    z = fsdp % z_size
     x_swap = [(f, (f + z_size) % fsdp_size) for f in range(fsdp_size)]
     z_up = [(f, (f // z_size) * z_size + (f + 1) % z_size) for f in range(fsdp_size)]
     z_down = [(f, (f // z_size) * z_size + (f - 1) % z_size) for f in range(fsdp_size)]
-    other = lax.ppermute(proj_weight, "fsdp", x_swap)
-    first = jnp.where(x_lo == 0, proj_weight, other)
-    second = jnp.where(x_lo == 0, other, proj_weight)
+    other = lax.ppermute(part, "fsdp", x_swap)
+    first = jnp.where(x_lo == 0, part, other)
+    second = jnp.where(x_lo == 0, other, part)
     pair = jnp.stack([first, second], axis=1)
-    ahead = [pair]
-    behind = []
+    lead, halves, block, width = pair.shape
+    buffer = with_layout_constraint(
+        jnp.zeros((lead, halves, z_size, block, width), part.dtype), Layout((0, 1, 2, 3, 4))
+    )
+
+    def put(into, piece, at):
+        return lax.dynamic_update_slice(into, piece[:, :, None], (0, 0, at, 0, 0))
+
+    buffer = put(buffer, pair, z)
     right = pair
     left = pair
-    for _ in range(1, z_size // 2):
+    for step in range(1, z_size // 2):
         right = lax.ppermute(right, "fsdp", z_up)
         left = lax.ppermute(left, "fsdp", z_down)
-        behind.append(right)
-        ahead.append(left)
+        buffer = put(buffer, right, (z - step) % z_size)
+        buffer = put(buffer, left, (z + step) % z_size)
     last_a = lax.ppermute(right[:, :1], "fsdp", z_up)
     last_b = lax.ppermute(left[:, 1:], "fsdp", z_down)
-    ahead.append(jnp.concatenate([last_a, last_b], axis=1))
-    pieces = ahead + behind[::-1]
-    stacked = with_layout_constraint(jnp.stack(pieces, axis=2), Layout((0, 1, 2, 3, 4)))
-    return stacked.reshape(
-        proj_weight.shape[0], fsdp_size * proj_weight.shape[1], proj_weight.shape[2]
-    )
+    buffer = put(buffer, jnp.concatenate([last_a, last_b], axis=1), (z + z_size // 2) % z_size)
+    buffer = with_layout_constraint(buffer, Layout((0, 1, 2, 3, 4)))
+    return buffer.reshape(lead, fsdp_size * block, width)
 
 
 def local(activations, norm_gain, proj_weight, short_filter, segment_ids, needle_pos, readout):
@@ -56,21 +61,21 @@
     fsdp_size = lax.axis_size("fsdp")
     z_size = fsdp_size // 2
     channels = proj_weight.shape[2]
-    block = proj_weight.shape[1]
-    weights = gather_weights(proj_weight, fsdp_size, z_size)
+    query_weights = lax.all_gather(proj_weight[0], "fsdp", axis=0, tiled=True)
+    pair_weights = ring_gather(proj_weight[1:], fsdp_size, z_size)
     values = activations.astype(jnp.float32)
     scaled = lax.rsqrt(jnp.mean(values * values, axis=1, keepdims=True) + EPSILON)
     normed = (values * scaled * norm_gain[None, :]).astype(jnp.bfloat16)
-    z = lax.axis_index("fsdp") % z_size
-    grid = normed.reshape(local_rows, 2, z_size, block)
-    doubled = jnp.concatenate([grid, grid], axis=2)
-    rotated = lax.dynamic_slice_in_dim(doubled, z, z_size, axis=2).reshape(local_rows, model_width)
-    spread = jnp.broadcast_to(rotated[None], (tp_size,) + rotated.shape)
+    spread = jnp.broadcast_to(normed[None], (tp_size,) + normed.shape)
     slab_rows = lax.all_to_all(spread, "tp", 0, 0, tiled=False).reshape(
         tp_size * local_rows, model_width
     )
-    projected = jnp.einsum("sk,ikc->isc", slab_rows, weights, preferred_element_type=jnp.float32)
-    projected = with_layout_constraint(projected, Layout((0, 1, 2)))
+    key_value = jnp.einsum(
+        "sk,ikc->isc", slab_rows, pair_weights, preferred_element_type=jnp.float32
+    )
+    key_value = with_layout_constraint(key_value, Layout((0, 1, 2)))
+    query_part = jnp.dot(slab_rows, query_weights, preferred_element_type=jnp.float32)
+    projected = (query_part, key_value[0], key_value[1])
     gated_prod = projected[1] * projected[2]
     tap_table = jnp.repeat(short_filter, channels // short_filter.shape[0], axis=0)
     filtered = short_conv(gated_prod, tap_table, segment_ids[0])
@@ -84,8 +89,9 @@
     picked = jnp.dot(picker, mixed_local, preferred_element_type=jnp.float32)
     own_readout = lax.dynamic_slice_in_dim(readout, device_rank * channels, channels, 0)
     partial_sum = jnp.sum(picked * own_readout[None, :], axis=1)
-    high = partial_sum.astype(jnp.bfloat16)
-    low = (partial_sum - high.astype(jnp.float32)).astype(jnp.bfloat16)
+    rounded = lax.reduce_precision(partial_sum, exponent_bits=8, mantissa_bits=7)
+    high = rounded.astype(jnp.bfloat16)
+    low = (partial_sum - rounded).astype(jnp.bfloat16)
     extra_rows = 16
     extra = jnp.zeros((extra_rows, channels), jnp.bfloat16)
     extra = extra.at[0, : high.shape[0]].set(high).at[1, : low.shape[0]].set(low)

time: 163 us -> 198 us (1.21)
  blocking collectives: 20.5 us -> 35.8 us
  between operations: 1.05 us -> 14.8 us
  waiting for transfers between devices: 31.1 us -> 41.9 us
  starting transfers between devices: 78.7 us -> 71.7 us
  matrix products: 7.34 us -> 10.4 us
  other arithmetic: 6.53 us -> 4.44 us
    all_gather x0 -> x1, waiting for transfers between devices: none -> 28.1 us  [local(): query_weights = lax.all_gather(proj_weight[0], 'fsdp', axis=0, tiled=True)]
    ppermute x17, waiting for transfers between devices: 31.1 us -> 13.7 us  [the longest x7 12.9 us: ring_gather(): right = lax.ppermute(right, 'fsdp', z_up)]
    all_to_all x1, blocking collectives: 20.5 us -> 35.8 us  [local(): gathered = lax.all_to_all(payload, 'tp', 0, 0, tiled=False)]
    unnamed x22 -> x9, local copies, waits for them, and re-layouts: 11.4 us -> 0.03 us
    dynamic_update_slice x0 -> x14, local copies, waits for them, and re-layouts: none -> 10.1 us  [put(): return lax.dynamic_update_slice(into, piece[:, :, None], (0, 0, at, 0, 0))]
    ppermute x17, starting transfers between devices: 68.1 us -> 62.4 us  [the longest x7 38 us: ring_gather(): left = lax.ppermute(left, 'fsdp', z_down)]
    dot_general x1 -> x2, matrix products: 7.04 us -> 10.1 us  [the longest x1 5.8 us: local(): jnp.einsum('sk,ikc->isc', slab_rows, pair_weights, preferred_element_type...]
    unnamed x3 -> x0, other arithmetic: 2.66 us -> none
  transfers between devices with their start and end apart: 18 -> 19, of which waited for: 9 -> 9; matrix products, arithmetic and copies ran while one was open for 12% -> 13% of each run, Pallas kernels for 0% -> 0%
where the time goes in v4:
time: 198 us; the launch traced here: 197 us
  starting transfers between devices  71.7 us (36%)
  waiting for transfers between devices  41.9 us (21%)
  blocking collectives  35.8 us (18%)
  local copies, waits for them, and re-layouts  18.5 us (9%)
  between operations  14.8 us (7%)
  matrix products  10.4 us (5%)
  other arithmetic  4.44 us (2%)
    ppermute x7, starting transfers between devices, ring_gather(): left = lax.ppermute(left, 'fsdp', z_down)  38 us
    all_to_all x1, blocking collectives, local(): gathered = lax.all_to_all(payload, 'tp', 0, 0, tiled=False)  35.8 us
    all_gather x1, waiting for transfers between devices, local(): query_weights = lax.all_gather(proj_weight[0], 'fsdp', axis=0, tiled=True)  28.1 us
    ppermute x7, starting transfers between devices, ring_gather(): right = lax.ppermute(right, 'fsdp', z_up)  13.5 us
    ppermute x7, waiting for transfers between devices, ring_gather(): right = lax.ppermute(right, 'fsdp', z_up)  12.9 us
    dynamic_update_slice x14, local copies, waits for them, and re-layouts, put(): return lax.dynamic_update_slice(into, piece[:, :, None], (0, 0, at, 0, 0))  10.1 us
    all_to_all x1, starting transfers between devices, local(): lax.all_to_all(spread, 'tp', 0, 0, tiled=False)  9.24 us
    dot_general x1, matrix products, local(): jnp.einsum('sk,ikc->isc', slab_rows, pair_weights, preferred_element_type...  5.8 us
  transfers between devices with their start and end apart: 19, of which 9 were waited for; matrix products, arithmetic and copies ran while one was open for 13% of the time, Pallas kernels for 0%

profile of v4, /device:TPU:1, one launch (start us, length us, event | category | flops | bytes accessed | tf_op | source)
XLA Modules:
  0.0 197.4 jit_solution(9545895974344266782)
XLA Ops:
  8.1 3.9 %collective-permute-start = (bf16[2,128,256]{2,1,0:T(8,128)(2,1)S(1)}, bf16[2,128,256]{2,1,0:T(8,128)(2,1)S(1)}, u32[]{:S(2)}, u32[]{:S(2)}) collective-permute-start(bf16[2,128,256]{2,1,0:T(8,128)(2,1)S(1)} %slice.120), channel_id=1, source_target_pairs={{0,256},{16,272},{32,288},{48,304},{64,320},{80,336},{96,352},{112... | collective-permute-start | bytes 393224 | tf_op jit(solution)/shard_map/ppermute | solution.py:30
  14.3 2.5 %broadcast_in_dim.79 = bf16[16,32,4096]{2,1,0:T(8,128)(2,1)} broadcast(bf16[32,4096]{1,0:T(8,128)(2,1)S(1)} %fusion.29), dimensions={1,2} | broadcast | bytes 4456448 | tf_op jit(solution)/shard_map/broadcast_in_dim | solution.py:69
  16.8 9.2 %all-to-all-start = ((bf16[16,32,4096]{2,1,0:T(8,128)(2,1)}), bf16[16,32,4096]{2,1,0:T(8,128)(2,1)}, u32[]{:S(2)}, u32[]{:S(2)}) async-start(bf16[16,32,4096]{2,1,0:T(8,128)(2,1)} %broadcast_in_dim.79), calls=%async_computation | async-start | bytes 8388608 | tf_op jit(solution)/shard_map/all_to_all | solution.py:70
  28.2 2.0 %collective-permute-start.1 = (bf16[2,2,128,256]{3,2,1,0:T(8,128)(2,1)S(1)}, bf16[2,2,128,256]{3,2,1,0:T(8,128)(2,1)S(1)}, u32[]{:S(2)}, u32[]{:S(2)}) collective-permute-start(bf16[2,2,128,256]{3,2,1,0:T(8,128)(2,1)S(1)} %pad_maximum_fusion.1), channel_id=1, source_target_pairs={{0,16},{16,32},{32,48},{48,64},{64,80},{80,96},{96,112},{112,128},... | collective-permute-start | bytes 786440 | tf_op jit(solution)/shard_map/ppermute | solution.py:46
  30.2 9.5 %collective-permute-start.2 = (bf16[2,2,128,256]{3,2,1,0:T(8,128)(2,1)S(1)}, bf16[2,2,128,256]{3,2,1,0:T(8,128)(2,1)S(1)}, u32[]{:S(2)}, u32[]{:S(2)}) collective-permute-start(bf16[2,2,128,256]{3,2,1,0:T(8,128)(2,1)S(1)} %pad_maximum_fusion.1), channel_id=1, source_target_pairs={{0,240},{16,0},{32,16},{48,32},{64,48},{80,64},{96,80},{112,96},{1... | collective-permute-start | bytes 786440 | tf_op jit(solution)/shard_map/ppermute | solution.py:47
  39.8 2.5 %broadcast_in_dim.80 = bf16[2,2,16,128,256]{4,3,2,1,0:T(8,128)(2,1)} broadcast(bf16[]{:T(256)} %constant.173.clone.1), dimensions={} | broadcast | bytes 4194306 | tf_op jit(solution)/shard_map/broadcast_in_dim | solution.py:36
  44.4 1.9 collective-permute-start.3
  46.3 4.6 %collective-permute-start.4 = (bf16[2,2,128,256]{3,2,1,0:T(8,128)(2,1)S(1)}, bf16[2,2,128,256]{3,2,1,0:T(8,128)(2,1)S(1)}, u32[]{:S(2)}, u32[]{:S(2)}) collective-permute-start(bf16[2,2,128,256]{3,2,1,0:T(8,128)(2,1)S(1)} %collective-permute-done.2), channel_id=1, source_target_pairs={{0,240},{16,0},{32,16},{48,32},{64,48},{80,64},{96,80},{112,96},{1... | collective-permute-start | bytes 786440 | tf_op jit(solution)/shard_map/ppermute | solution.py:47
  52.4 3.2 %collective-permute-done.3 = bf16[2,2,128,256]{3,2,1,0:T(8,128)(2,1)S(1)} collective-permute-done((bf16[2,2,128,256]{3,2,1,0:T(8,128)(2,1)S(1)}, bf16[2,2,128,256]{3,2,1,0:T(8,128)(2,1)S(1)}, u32[]{:S(2)}, u32[]{:S(2)}) %collective-permute-start.3) | collective-permute-done | bytes 262176 | tf_op jit(solution)/shard_map/ppermute | solution.py:46
  57.5 4.6 %collective-permute-start.6 = (bf16[2,2,128,256]{3,2,1,0:T(8,128)(2,1)S(1)}, bf16[2,2,128,256]{3,2,1,0:T(8,128)(2,1)S(1)}, u32[]{:S(2)}, u32[]{:S(2)}) collective-permute-start(bf16[2,2,128,256]{3,2,1,0:T(8,128)(2,1)S(1)} %collective-permute-done.4), channel_id=1, source_target_pairs={{0,240},{16,0},{32,16},{48,32},{64,48},{80,64},{96,80},{112,96},{1... | collective-permute-start | bytes 786440 | tf_op jit(solution)/shard_map/ppermute | solution.py:47
  63.5 3.2 %collective-permute-done.5 = bf16[2,2,128,256]{3,2,1,0:T(8,128)(2,1)S(1)} collective-permute-done((bf16[2,2,128,256]{3,2,1,0:T(8,128)(2,1)S(1)}, bf16[2,2,128,256]{3,2,1,0:T(8,128)(2,1)S(1)}, u32[]{:S(2)}, u32[]{:S(2)}) %collective-permute-start.5) | collective-permute-done | bytes 262176 | tf_op jit(solution)/shard_map/ppermute | solution.py:46
  68.6 4.6 %collective-permute-start.8 = (bf16[2,2,128,256]{3,2,1,0:T(8,128)(2,1)S(1)}, bf16[2,2,128,256]{3,2,1,0:T(8,128)(2,1)S(1)}, u32[]{:S(2)}, u32[]{:S(2)}) collective-permute-start(bf16[2,2,128,256]{3,2,1,0:T(8,128)(2,1)S(1)} %collective-permute-done.6), channel_id=1, source_target_pairs={{0,240},{16,0},{32,16},{48,32},{64,48},{80,64},{96,80},{112,96},{1... | collective-permute-start | bytes 786440 | tf_op jit(solution)/shard_map/ppermute | solution.py:47
  74.6 2.4 %collective-permute-done.7 = bf16[2,2,128,256]{3,2,1,0:T(8,128)(2,1)S(1)} collective-permute-done((bf16[2,2,128,256]{3,2,1,0:T(8,128)(2,1)S(1)}, bf16[2,2,128,256]{3,2,1,0:T(8,128)(2,1)S(1)}, u32[]{:S(2)}, u32[]{:S(2)}) %collective-permute-start.7) | collective-permute-done | bytes 262176 | tf_op jit(solution)/shard_map/ppermute | solution.py:46
  79.0 4.6 %collective-permute-start.10 = (bf16[2,2,128,256]{3,2,1,0:T(8,128)(2,1)S(1)}, bf16[2,2,128,256]{3,2,1,0:T(8,128)(2,1)S(1)}, u32[]{:S(2)}, u32[]{:S(2)}) collective-permute-start(bf16[2,2,128,256]{3,2,1,0:T(8,128)(2,1)S(1)} %collective-permute-done.8), channel_id=1, source_target_pairs={{0,240},{16,0},{32,16},{48,32},{64,48},{80,64},{96,80},{112,96},{1... | collective-permute-start | bytes 786440 | tf_op jit(solution)/shard_map/ppermute | solution.py:47
  86.3 1.9 collective-permute-start.11
  88.2 5.1 %collective-permute-start.12 = (bf16[2,2,128,256]{3,2,1,0:T(8,128)(2,1)S(1)}, bf16[2,2,128,256]{3,2,1,0:T(8,128)(2,1)S(1)}, u32[]{:S(2)}, u32[]{:S(2)}) collective-permute-start(bf16[2,2,128,256]{3,2,1,0:T(8,128)(2,1)S(1)} %collective-permute-done.10), channel_id=1, source_target_pairs={{0,240},{16,0},{32,16},{48,32},{64,48},{80,64},{96,80},{112,96},{1... | collective-permute-start | bytes 786440 | tf_op jit(solution)/shard_map/ppermute | solution.py:47
  95.2 1.9 collective-permute-start.13
  97.2 5.1 %collective-permute-start.14 = (bf16[2,2,128,256]{3,2,1,0:T(8,128)(2,1)S(1)}, bf16[2,2,128,256]{3,2,1,0:T(8,128)(2,1)S(1)}, u32[]{:S(2)}, u32[]{:S(2)}) collective-permute-start(bf16[2,2,128,256]{3,2,1,0:T(8,128)(2,1)S(1)} %collective-permute-done.12), channel_id=1, source_target_pairs={{0,240},{16,0},{32,16},{48,32},{64,48},{80,64},{96,80},{112,96},{1... | collective-permute-start | bytes 786440 | tf_op jit(solution)/shard_map/ppermute | solution.py:47
  104.8 1.9 collective-permute-start.15
  106.7 5.0 %collective-permute-start.16 = (bf16[2,1,128,256]{3,2,1,0:T(8,128)(2,1)S(1)}, bf16[2,1,128,256]{3,2,1,0:T(8,128)(2,1)S(1)}, u32[]{:S(2)}, u32[]{:S(2)}) collective-permute-start(bf16[2,1,128,256]{3,2,1,0:T(8,128)(2,1)S(1)} %slice.148), channel_id=1, source_target_pairs={{0,240},{16,0},{32,16},{48,32},{64,48},{80,64},{96,80},{112,96},{1... | collective-permute-start | bytes 393224 | tf_op jit(solution)/shard_map/ppermute | solution.py:51
  114.7 5.8 %convolution_bitcast_fusion = f32[2,512,256]{2,1,0:T(8,128)S(1)} fusion(bf16[512,4096,1]{1,0,2:T(8,128)(2,1)} %bitcast.37, bf16[2,4096,256]{2,1,0:T(8,128)(2,1)} %bitcast.36), kind=kOutput, calls=%fused_computation.2 | convolution fusion | flops 2147483648 | bytes 9437184 | tf_op jit(solution)/shard_map/sk,ikc->isc/dot_general | solution.py:73
  120.5 28.1 %all-gather.3.cloned.1.call-done = bf16[1,4096,256]{2,1,0:T(8,128)(2,1)} async-done(((bf16[1,128,256]{2,1,0:T(8,128)(2,1)}), bf16[1,4096,256]{2,1,0:T(8,128)(2,1)}) %all-gather.3.cloned.1.call-update) | async-done | bytes 2097168 | tf_op jit(solution)/shard_map/all_gather | solution.py:64
  148.6 4.3 %fusion.5 = bf16[512,256]{1,0:T(8,128)(2,1)S(1)} fusion(bf16[512,4096]{1,0:T(8,128)(2,1)} %bitcast, bf16[1,4096,256]{2,1,0:T(8,128)(2,1)} %all-gather.3.cloned.1.call-done, f32[512,256]{1,0:T(8,128)S(1)} %fusion.30, f32[256]{0:T(256)S(1)} %bitcast.114, f32[512]{0:T(512)S(1)} %get-tuple-element.40, f32[256]{0:T(256)S(1)} %bitcast.115, ...), kind=kOutput, calls=%fused_computation.4 | convolution fusion | flops 1076494336 | bytes 7097344 | tf_op jit(solution)/shard_map/dot_general | solution.py:77
  153.5 35.8 %all_to_all.10 = bf16[16,48,256]{2,1,0:T(8,128)(2,1)S(1)} all-to-all(bf16[16,48,256]{2,1,0:T(8,128)(2,1)S(1)} %pad_maximum_fusion), channel_id=1, replica_groups=mesh['fsdp'=32,'tp'=16] {'tp'}, dimensions={0} | all-to-all | bytes 786432 | tf_op jit(solution)/shard_map/all_to_all | solution.py:102
  (69 shorter events, 29.1 us)
Async XLA Ops:
  8.1 20.0 %collective-permute-start = (bf16[2,128,256]{2,1,0:T(8,128)(2,1)S(1)}, bf16[2,128,256]{2,1,0:T(8,128)(2,1)S(1)}, u32[]{:S(2)}, u32[]{:S(2)}) collective-permute-start(bf16[2,128,256]{2,1,0:T(8,128)(2,1)S(1)} %slice.120), channel_id=1, source_target_pairs={{0,256},{16,272},{32,288},{48,304},{64,320},{80,336},{96,352},{112... | collective-permute-start | bytes 393224 | tf_op jit(solution)/shard_map/ppermute | solution.py:30
  16.8 9.3 %copy-start = (bf16[3,128,256]{2,1,0:T(8,128)(2,1)S(1)}, bf16[3,128,256]{2,1,0:T(8,128)(2,1)}, u32[]{:S(2)}) copy-start(bf16[3,128,256]{2,1,0:T(8,128)(2,1)} %param.13) | copy-start | bytes 589828
  16.8 10.3 %copy-start.1 = (f32[16,7]{0,1:T(8,128)S(1)}, f32[16,7]{0,1:T(8,128)}, u32[]{:S(2)}) copy-start(f32[16,7]{0,1:T(8,128)} %param.14) | copy-start | bytes 1348
  16.8 23.0 %copy-start.2 = (s32[1,512]{1,0:T(1,128)S(1)}, s32[1,512]{1,0:T(1,128)}, u32[]{:S(2)}) copy-start(s32[1,512]{1,0:T(1,128)} %param.15) | copy-start | bytes 6148
  16.8 97.9 %all-to-all-start = ((bf16[16,32,4096]{2,1,0:T(8,128)(2,1)}), bf16[16,32,4096]{2,1,0:T(8,128)(2,1)}, u32[]{:S(2)}, u32[]{:S(2)}) async-start(bf16[16,32,4096]{2,1,0:T(8,128)(2,1)} %broadcast_in_dim.79), calls=%async_computation | async-start | bytes 8388608 | tf_op jit(solution)/shard_map/all_to_all | solution.py:70
  26.0 122.6 %all-gather.3.cloned.1.call-start = ((), (), s32[]{:S(2)}) async-start(), calls=%async_computation.2 | async-start | bytes 2162688 | tf_op jit(solution)/shard_map/all_gather | solution.py:64
  28.2 16.2 %collective-permute-start.1 = (bf16[2,2,128,256]{3,2,1,0:T(8,128)(2,1)S(1)}, bf16[2,2,128,256]{3,2,1,0:T(8,128)(2,1)S(1)}, u32[]{:S(2)}, u32[]{:S(2)}) collective-permute-start(bf16[2,2,128,256]{3,2,1,0:T(8,128)(2,1)S(1)} %pad_maximum_fusion.1), channel_id=1, source_target_pairs={{0,16},{16,32},{32,48},{48,64},{64,80},{80,96},{96,112},{112,128},... | collective-permute-start | bytes 786440 | tf_op jit(solution)/shard_map/ppermute | solution.py:46
  30.2 16.1 %collective-permute-start.2 = (bf16[2,2,128,256]{3,2,1,0:T(8,128)(2,1)S(1)}, bf16[2,2,128,256]{3,2,1,0:T(8,128)(2,1)S(1)}, u32[]{:S(2)}, u32[]{:S(2)}) collective-permute-start(bf16[2,2,128,256]{3,2,1,0:T(8,128)(2,1)S(1)} %pad_maximum_fusion.1), channel_id=1, source_target_pairs={{0,240},{16,0},{32,16},{48,32},{64,48},{80,64},{96,80},{112,96},{1... | collective-permute-start | bytes 786440 | tf_op jit(solution)/shard_map/ppermute | solution.py:47
  44.4 11.1 %collective-permute-start.3 = (bf16[2,2,128,256]{3,2,1,0:T(8,128)(2,1)S(1)}, bf16[2,2,128,256]{3,2,1,0:T(8,128)(2,1)S(1)}, u32[]{:S(2)}, u32[]{:S(2)}) collective-permute-start(bf16[2,2,128,256]{3,2,1,0:T(8,128)(2,1)S(1)} %collective-permute-done.1), channel_id=1, source_target_pairs={{0,16},{16,32},{32,48},{48,64},{64,80},{80,96},{96,112},{112,128},... | collective-permute-start | bytes 786440 | tf_op jit(solution)/shard_map/ppermute | solution.py:46
  46.3 11.1 %collective-permute-start.4 = (bf16[2,2,128,256]{3,2,1,0:T(8,128)(2,1)S(1)}, bf16[2,2,128,256]{3,2,1,0:T(8,128)(2,1)S(1)}, u32[]{:S(2)}, u32[]{:S(2)}) collective-permute-start(bf16[2,2,128,256]{3,2,1,0:T(8,128)(2,1)S(1)} %collective-permute-done.2), channel_id=1, source_target_pairs={{0,240},{16,0},{32,16},{48,32},{64,48},{80,64},{96,80},{112,96},{1... | collective-permute-start | bytes 786440 | tf_op jit(solution)/shard_map/ppermute | solution.py:47
  55.5 11.2 %collective-permute-start.5 = (bf16[2,2,128,256]{3,2,1,0:T(8,128)(2,1)S(1)}, bf16[2,2,128,256]{3,2,1,0:T(8,128)(2,1)S(1)}, u32[]{:S(2)}, u32[]{:S(2)}) collective-permute-start(bf16[2,2,128,256]{3,2,1,0:T(8,128)(2,1)S(1)} %collective-permute-done.3), channel_id=1, source_target_pairs={{0,16},{16,32},{32,48},{48,64},{64,80},{80,96},{96,112},{112,128},... | collective-permute-start | bytes 786440 | tf_op jit(solution)/shard_map/ppermute | solution.py:46
  57.5 11.1 %collective-permute-start.6 = (bf16[2,2,128,256]{3,2,1,0:T(8,128)(2,1)S(1)}, bf16[2,2,128,256]{3,2,1,0:T(8,128)(2,1)S(1)}, u32[]{:S(2)}, u32[]{:S(2)}) collective-permute-start(bf16[2,2,128,256]{3,2,1,0:T(8,128)(2,1)S(1)} %collective-permute-done.4), channel_id=1, source_target_pairs={{0,240},{16,0},{32,16},{48,32},{64,48},{80,64},{96,80},{112,96},{1... | collective-permute-start | bytes 786440 | tf_op jit(solution)/shard_map/ppermute | solution.py:47
  66.7 10.3 %collective-permute-start.7 = (bf16[2,2,128,256]{3,2,1,0:T(8,128)(2,1)S(1)}, bf16[2,2,128,256]{3,2,1,0:T(8,128)(2,1)S(1)}, u32[]{:S(2)}, u32[]{:S(2)}) collective-permute-start(bf16[2,2,128,256]{3,2,1,0:T(8,128)(2,1)S(1)} %collective-permute-done.5), channel_id=1, source_target_pairs={{0,16},{16,32},{32,48},{48,64},{64,80},{80,96},{96,112},{112,128},... | collective-permute-start | bytes 786440 | tf_op jit(solution)/shard_map/ppermute | solution.py:46
  68.6 10.3 %collective-permute-start.8 = (bf16[2,2,128,256]{3,2,1,0:T(8,128)(2,1)S(1)}, bf16[2,2,128,256]{3,2,1,0:T(8,128)(2,1)S(1)}, u32[]{:S(2)}, u32[]{:S(2)}) collective-permute-start(bf16[2,2,128,256]{3,2,1,0:T(8,128)(2,1)S(1)} %collective-permute-done.6), channel_id=1, source_target_pairs={{0,240},{16,0},{32,16},{48,32},{64,48},{80,64},{96,80},{112,96},{1... | collective-permute-start | bytes 786440 | tf_op jit(solution)/shard_map/ppermute | solution.py:47
  77.0 9.2 %collective-permute-start.9 = (bf16[2,2,128,256]{3,2,1,0:T(8,128)(2,1)S(1)}, bf16[2,2,128,256]{3,2,1,0:T(8,128)(2,1)S(1)}, u32[]{:S(2)}, u32[]{:S(2)}) collective-permute-start(bf16[2,2,128,256]{3,2,1,0:T(8,128)(2,1)S(1)} %collective-permute-done.7), channel_id=1, source_target_pairs={{0,16},{16,32},{32,48},{48,64},{64,80},{80,96},{96,112},{112,128},... | collective-permute-start | bytes 786440 | tf_op jit(solution)/shard_map/ppermute | solution.py:46
  79.0 9.2 %collective-permute-start.10 = (bf16[2,2,128,256]{3,2,1,0:T(8,128)(2,1)S(1)}, bf16[2,2,128,256]{3,2,1,0:T(8,128)(2,1)S(1)}, u32[]{:S(2)}, u32[]{:S(2)}) collective-permute-start(bf16[2,2,128,256]{3,2,1,0:T(8,128)(2,1)S(1)} %collective-permute-done.8), channel_id=1, source_target_pairs={{0,240},{16,0},{32,16},{48,32},{64,48},{80,64},{96,80},{112,96},{1... | collective-permute-start | bytes 786440 | tf_op jit(solution)/shard_map/ppermute | solution.py:47
  86.3 8.9 %collective-permute-start.11 = (bf16[2,2,128,256]{3,2,1,0:T(8,128)(2,1)S(1)}, bf16[2,2,128,256]{3,2,1,0:T(8,128)(2,1)S(1)}, u32[]{:S(2)}, u32[]{:S(2)}) collective-permute-start(bf16[2,2,128,256]{3,2,1,0:T(8,128)(2,1)S(1)} %collective-permute-done.9), channel_id=1, source_target_pairs={{0,16},{16,32},{32,48},{48,64},{64,80},{80,96},{96,112},{112,128},... | collective-permute-start | bytes 786440 | tf_op jit(solution)/shard_map/ppermute | solution.py:46
  88.2 9.0 %collective-permute-start.12 = (bf16[2,2,128,256]{3,2,1,0:T(8,128)(2,1)S(1)}, bf16[2,2,128,256]{3,2,1,0:T(8,128)(2,1)S(1)}, u32[]{:S(2)}, u32[]{:S(2)}) collective-permute-start(bf16[2,2,128,256]{3,2,1,0:T(8,128)(2,1)S(1)} %collective-permute-done.10), channel_id=1, source_target_pairs={{0,240},{16,0},{32,16},{48,32},{64,48},{80,64},{96,80},{112,96},{1... | collective-permute-start | bytes 786440 | tf_op jit(solution)/shard_map/ppermute | solution.py:47
  95.2 9.5 %collective-permute-start.13 = (bf16[2,2,128,256]{3,2,1,0:T(8,128)(2,1)S(1)}, bf16[2,2,128,256]{3,2,1,0:T(8,128)(2,1)S(1)}, u32[]{:S(2)}, u32[]{:S(2)}) collective-permute-start(bf16[2,2,128,256]{3,2,1,0:T(8,128)(2,1)S(1)} %collective-permute-done.11), channel_id=1, source_target_pairs={{0,16},{16,32},{32,48},{48,64},{64,80},{80,96},{96,112},{112,128},... | collective-permute-start | bytes 786440 | tf_op jit(solution)/shard_map/ppermute | solution.py:46
  97.2 9.5 %collective-permute-start.14 = (bf16[2,2,128,256]{3,2,1,0:T(8,128)(2,1)S(1)}, bf16[2,2,128,256]{3,2,1,0:T(8,128)(2,1)S(1)}, u32[]{:S(2)}, u32[]{:S(2)}) collective-permute-start(bf16[2,2,128,256]{3,2,1,0:T(8,128)(2,1)S(1)} %collective-permute-done.12), channel_id=1, source_target_pairs={{0,240},{16,0},{32,16},{48,32},{64,48},{80,64},{96,80},{112,96},{1... | collective-permute-start | bytes 786440 | tf_op jit(solution)/shard_map/ppermute | solution.py:47
  104.8 8.4 %collective-permute-start.15 = (bf16[2,1,128,256]{3,2,1,0:T(8,128)(2,1)S(1)}, bf16[2,1,128,256]{3,2,1,0:T(8,128)(2,1)S(1)}, u32[]{:S(2)}, u32[]{:S(2)}) collective-permute-start(bf16[2,1,128,256]{3,2,1,0:T(8,128)(2,1)S(1)} %slice.147), channel_id=1, source_target_pairs={{0,16},{16,32},{32,48},{48,64},{64,80},{80,96},{96,112},{112,128},... | collective-permute-start | bytes 393224 | tf_op jit(solution)/shard_map/ppermute | solution.py:50
  106.7 7.2 %collective-permute-start.16 = (bf16[2,1,128,256]{3,2,1,0:T(8,128)(2,1)S(1)}, bf16[2,1,128,256]{3,2,1,0:T(8,128)(2,1)S(1)}, u32[]{:S(2)}, u32[]{:S(2)}) collective-permute-start(bf16[2,1,128,256]{3,2,1,0:T(8,128)(2,1)S(1)} %slice.148), channel_id=1, source_target_pairs={{0,240},{16,0},{32,16},{48,32},{64,48},{80,64},{96,80},{112,96},{1... | collective-permute-start | bytes 393224 | tf_op jit(solution)/shard_map/ppermute | solution.py:51
  148.6 4.3 %copy-start.3 = (s32[1,16]{1,0:T(1,128)S(1)}, s32[1,16]{1,0:T(1,128)}, u32[]{:S(2)}) copy-start(s32[1,16]{1,0:T(1,128)} %param.16) | copy-start | bytes 196
Sparse Core Ops, SparseCore 0:
  29.5 119.0 all-gather.2

commit v5 on v3

--- a/solution.py
+++ b/solution.py
@@ -84,8 +84,9 @@
     picked = jnp.dot(picker, mixed_local, preferred_element_type=jnp.float32)
     own_readout = lax.dynamic_slice_in_dim(readout, device_rank * channels, channels, 0)
     partial_sum = jnp.sum(picked * own_readout[None, :], axis=1)
-    high = partial_sum.astype(jnp.bfloat16)
-    low = (partial_sum - high.astype(jnp.float32)).astype(jnp.bfloat16)
+    rounded = lax.reduce_precision(partial_sum, exponent_bits=8, mantissa_bits=7)
+    high = rounded.astype(jnp.bfloat16)
+    low = (partial_sum - rounded).astype(jnp.bfloat16)
     extra_rows = 16
     extra = jnp.zeros((extra_rows, channels), jnp.bfloat16)
     extra = extra.at[0, : high.shape[0]].set(high).at[1, : low.shape[0]].set(low)

time: 163 us -> 163 us (level)
  no operation moved by 1% of the time
where the time goes in v5:
time: 163 us; the launch traced here: 162 us
  starting transfers between devices  78.7 us (48%)
  waiting for transfers between devices  31.2 us (19%)
  blocking collectives  20.5 us (13%)
  local copies, waits for them, and re-layouts  16.4 us (10%)
  matrix products  7.34 us (5%)
  other arithmetic  6.5 us (4%)
    ppermute x7, starting transfers between devices, gather_weights(): left = lax.ppermute(left, 'fsdp', z_down)  44.2 us
    all_to_all x1, blocking collectives, local(): gathered = lax.all_to_all(payload, 'tp', 0, 0, tiled=False)  20.5 us
    ppermute x7, waiting for transfers between devices, gather_weights(): left = lax.ppermute(left, 'fsdp', z_down)  18.8 us
    ppermute x7, starting transfers between devices, gather_weights(): right = lax.ppermute(right, 'fsdp', z_up)  13.4 us
    unnamed x22, local copies, waits for them, and re-layouts  11.2 us
    all_to_all x1, starting transfers between devices, local(): lax.all_to_all(spread, 'tp', 0, 0, tiled=False)  10.6 us
    ppermute x7, waiting for transfers between devices, gather_weights(): right = lax.ppermute(right, 'fsdp', z_up)  7.39 us
    dot_general x1, matrix products, local(): jnp.einsum('sk,ikc->isc', slab_rows, weights, preferred_element_type=jnp....  7.05 us
  transfers between devices with their start and end apart: 18, of which 9 were waited for; matrix products, arithmetic and copies ran while one was open for 12% of the time, Pallas kernels for 0%

profile of v5, /device:TPU:1, one launch (start us, length us, event | category | flops | bytes accessed | tf_op | source)
XLA Modules:
  0.0 161.7 jit_solution(987484318704540527)
XLA Ops:
  0.6 3.9 %collective-permute-start = (bf16[3,128,256]{2,1,0:T(8,128)(2,1)}, bf16[3,128,256]{2,1,0:T(8,128)(2,1)S(1)}, u32[]{:S(2)}, u32[]{:S(2)}) collective-permute-start(bf16[3,128,256]{2,1,0:T(8,128)(2,1)} %param.13), channel_id=1, source_target_pairs={{0,256},{16,272},{32,288},{48,304},{64,320},{80,336},{96,352},{112... | collective-permute-start | bytes 589832 | tf_op jit(solution)/shard_map/ppermute | solution.py:29
  4.6 3.2 %collective-permute-done = bf16[3,128,256]{2,1,0:T(8,128)(2,1)S(1)} collective-permute-done((bf16[3,128,256]{2,1,0:T(8,128)(2,1)}, bf16[3,128,256]{2,1,0:T(8,128)(2,1)S(1)}, u32[]{:S(2)}, u32[]{:S(2)}) %collective-permute-start) | collective-permute-done | bytes 196640 | tf_op jit(solution)/shard_map/ppermute | solution.py:29
  8.8 12.6 %collective-permute-start.1 = (bf16[3,2,128,256]{3,2,1,0:T(8,128)(2,1)S(1)}, bf16[3,2,128,256]{3,2,1,0:T(8,128)(2,1)S(1)}, u32[]{:S(2)}, u32[]{:S(2)}) collective-permute-start(bf16[3,2,128,256]{3,2,1,0:T(8,128)(2,1)S(1)} %pad_maximum_fusion), channel_id=1, source_target_pairs={{0,240},{16,0},{32,16},{48,32},{64,48},{80,64},{96,80},{112,96},{1... | collective-permute-start | bytes 1179656 | tf_op jit(solution)/shard_map/ppermute | solution.py:39
  21.5 1.9 %collective-permute-start.8 = (bf16[3,2,128,256]{3,2,1,0:T(8,128)(2,1)S(1)}, bf16[3,2,128,256]{3,2,1,0:T(8,128)(2,1)S(1)}, u32[]{:S(2)}, u32[]{:S(2)}) collective-permute-start(bf16[3,2,128,256]{3,2,1,0:T(8,128)(2,1)S(1)} %pad_maximum_fusion), channel_id=1, source_target_pairs={{0,16},{16,32},{32,48},{48,64},{64,80},{80,96},{96,112},{112,128},... | collective-permute-start | bytes 1179656 | tf_op jit(solution)/shard_map/ppermute | solution.py:38
  23.4 4.9 %collective-permute-done.1 = bf16[3,2,128,256]{3,2,1,0:T(8,128)(2,1)S(1)} collective-permute-done((bf16[3,2,128,256]{3,2,1,0:T(8,128)(2,1)S(1)}, bf16[3,2,128,256]{3,2,1,0:T(8,128)(2,1)S(1)}, u32[]{:S(2)}, u32[]{:S(2)}) %collective-permute-start.1) | collective-permute-done | bytes 393248 | tf_op jit(solution)/shard_map/ppermute | solution.py:39
  28.3 5.3 %collective-permute-start.2 = (bf16[3,2,128,256]{3,2,1,0:T(8,128)(2,1)S(1)}, bf16[3,2,128,256]{3,2,1,0:T(8,128)(2,1)S(1)}, u32[]{:S(2)}, u32[]{:S(2)}) collective-permute-start(bf16[3,2,128,256]{3,2,1,0:T(8,128)(2,1)S(1)} %collective-permute-done.1), channel_id=1, source_target_pairs={{0,240},{16,0},{32,16},{48,32},{64,48},{80,64},{96,80},{112,96},{1... | collective-permute-start | bytes 1179656 | tf_op jit(solution)/shard_map/ppermute | solution.py:39
  33.6 1.9 %collective-permute-start.9 = (bf16[3,2,128,256]{3,2,1,0:T(8,128)(2,1)S(1)}, bf16[3,2,128,256]{3,2,1,0:T(8,128)(2,1)S(1)}, u32[]{:S(2)}, u32[]{:S(2)}) collective-permute-start(bf16[3,2,128,256]{3,2,1,0:T(8,128)(2,1)S(1)} %collective-permute-done.8), channel_id=1, source_target_pairs={{0,16},{16,32},{32,48},{48,64},{64,80},{80,96},{96,112},{112,128},... | collective-permute-start | bytes 1179656 | tf_op jit(solution)/shard_map/ppermute | solution.py:38
  36.7 2.9 %collective-permute-done.2 = bf16[3,2,128,256]{3,2,1,0:T(8,128)(2,1)S(1)} collective-permute-done((bf16[3,2,128,256]{3,2,1,0:T(8,128)(2,1)S(1)}, bf16[3,2,128,256]{3,2,1,0:T(8,128)(2,1)S(1)}, u32[]{:S(2)}, u32[]{:S(2)}) %collective-permute-start.2) | collective-permute-done | bytes 393248 | tf_op jit(solution)/shard_map/ppermute | solution.py:39
  39.5 5.3 %collective-permute-start.3 = (bf16[3,2,128,256]{3,2,1,0:T(8,128)(2,1)S(1)}, bf16[3,2,128,256]{3,2,1,0:T(8,128)(2,1)S(1)}, u32[]{:S(2)}, u32[]{:S(2)}) collective-permute-start(bf16[3,2,128,256]{3,2,1,0:T(8,128)(2,1)S(1)} %collective-permute-done.2), channel_id=1, source_target_pairs={{0,240},{16,0},{32,16},{48,32},{64,48},{80,64},{96,80},{112,96},{1... | collective-permute-start | bytes 1179656 | tf_op jit(solution)/shard_map/ppermute | solution.py:39
  48.3 2.6 %broadcast_in_dim.9 = bf16[16,32,4096]{2,1,0:T(8,128)(2,1)} broadcast(bf16[32,4096]{1,0:T(8,128)(2,1)S(1)} %bitcast.115), dimensions={1,2} | broadcast | bytes 4456448 | tf_op jit(solution)/shard_map/broadcast_in_dim | solution.py:68
  50.9 10.6 %all-to-all-start = ((bf16[16,32,4096]{2,1,0:T(8,128)(2,1)}), bf16[16,32,4096]{2,1,0:T(8,128)(2,1)}, u32[]{:S(2)}, u32[]{:S(2)}) async-start(bf16[16,32,4096]{2,1,0:T(8,128)(2,1)} %broadcast_in_dim.9), calls=%async_computation | async-start | bytes 8388608 | tf_op jit(solution)/shard_map/all_to_all | solution.py:69
  61.5 4.9 %collective-permute-start.4 = (bf16[3,2,128,256]{3,2,1,0:T(8,128)(2,1)S(1)}, bf16[3,2,128,256]{3,2,1,0:T(8,128)(2,1)}, u32[]{:S(2)}, u32[]{:S(2)}) collective-permute-start(bf16[3,2,128,256]{3,2,1,0:T(8,128)(2,1)S(1)} %collective-permute-done.3), channel_id=1, source_target_pairs={{0,240},{16,0},{32,16},{48,32},{64,48},{80,64},{96,80},{112,96},{1... | collective-permute-start | bytes 1179656 | tf_op jit(solution)/shard_map/ppermute | solution.py:39
  66.4 1.9 %collective-permute-start.11 = (bf16[3,2,128,256]{3,2,1,0:T(8,128)(2,1)S(1)}, bf16[3,2,128,256]{3,2,1,0:T(8,128)(2,1)S(1)}, u32[]{:S(2)}, u32[]{:S(2)}) collective-permute-start(bf16[3,2,128,256]{3,2,1,0:T(8,128)(2,1)S(1)} %collective-permute-done.10), channel_id=1, source_target_pairs={{0,16},{16,32},{32,48},{48,64},{64,80},{80,96},{96,112},{112,128},... | collective-permute-start | bytes 1179656 | tf_op jit(solution)/shard_map/ppermute | solution.py:38
  70.1 4.6 %collective-permute-done.4 = bf16[3,2,128,256]{3,2,1,0:T(8,128)(2,1)} collective-permute-done((bf16[3,2,128,256]{3,2,1,0:T(8,128)(2,1)S(1)}, bf16[3,2,128,256]{3,2,1,0:T(8,128)(2,1)}, u32[]{:S(2)}, u32[]{:S(2)}) %collective-permute-start.4) | collective-permute-done | bytes 393248 | tf_op jit(solution)/shard_map/ppermute | solution.py:39
  74.7 5.4 %collective-permute-start.5 = (bf16[3,2,128,256]{3,2,1,0:T(8,128)(2,1)}, bf16[3,2,128,256]{3,2,1,0:T(8,128)(2,1)S(1)}, u32[]{:S(2)}, u32[]{:S(2)}) collective-permute-start(bf16[3,2,128,256]{3,2,1,0:T(8,128)(2,1)} %collective-permute-done.4), channel_id=1, source_target_pairs={{0,240},{16,0},{32,16},{48,32},{64,48},{80,64},{96,80},{112,96},{1... | collective-permute-start | bytes 1179656 | tf_op jit(solution)/shard_map/ppermute | solution.py:39
  83.6 4.3 %collective-permute-done.5 = bf16[3,2,128,256]{3,2,1,0:T(8,128)(2,1)S(1)} collective-permute-done((bf16[3,2,128,256]{3,2,1,0:T(8,128)(2,1)}, bf16[3,2,128,256]{3,2,1,0:T(8,128)(2,1)S(1)}, u32[]{:S(2)}, u32[]{:S(2)}) %collective-permute-start.5) | collective-permute-done | bytes 393248 | tf_op jit(solution)/shard_map/ppermute | solution.py:39
  87.9 5.3 %collective-permute-start.6 = (bf16[3,2,128,256]{3,2,1,0:T(8,128)(2,1)S(1)}, bf16[3,2,128,256]{3,2,1,0:T(8,128)(2,1)S(1)}, u32[]{:S(2)}, u32[]{:S(2)}) collective-permute-start(bf16[3,2,128,256]{3,2,1,0:T(8,128)(2,1)S(1)} %collective-permute-done.5), channel_id=1, source_target_pairs={{0,240},{16,0},{32,16},{48,32},{64,48},{80,64},{96,80},{112,96},{1... | collective-permute-start | bytes 1179656 | tf_op jit(solution)/shard_map/ppermute | solution.py:39
  93.2 1.9 %collective-permute-start.13 = (bf16[3,2,128,256]{3,2,1,0:T(8,128)(2,1)S(1)}, bf16[3,2,128,256]{3,2,1,0:T(8,128)(2,1)S(1)}, u32[]{:S(2)}, u32[]{:S(2)}) collective-permute-start(bf16[3,2,128,256]{3,2,1,0:T(8,128)(2,1)S(1)} %collective-permute-done.12), channel_id=1, source_target_pairs={{0,16},{16,32},{32,48},{48,64},{64,80},{80,96},{96,112},{112,128},... | collective-permute-start | bytes 1179656 | tf_op jit(solution)/shard_map/ppermute | solution.py:38
  97.7 2.2 %collective-permute-done.6 = bf16[3,2,128,256]{3,2,1,0:T(8,128)(2,1)S(1)} collective-permute-done((bf16[3,2,128,256]{3,2,1,0:T(8,128)(2,1)S(1)}, bf16[3,2,128,256]{3,2,1,0:T(8,128)(2,1)S(1)}, u32[]{:S(2)}, u32[]{:S(2)}) %collective-permute-start.6) | collective-permute-done | bytes 393248 | tf_op jit(solution)/shard_map/ppermute | solution.py:39
  99.8 5.4 %collective-permute-start.7 = (bf16[3,2,128,256]{3,2,1,0:T(8,128)(2,1)S(1)}, bf16[3,2,128,256]{3,2,1,0:T(8,128)(2,1)S(1)}, u32[]{:S(2)}, u32[]{:S(2)}) collective-permute-start(bf16[3,2,128,256]{3,2,1,0:T(8,128)(2,1)S(1)} %collective-permute-done.6), channel_id=1, source_target_pairs={{0,240},{16,0},{32,16},{48,32},{64,48},{80,64},{96,80},{112,96},{1... | collective-permute-start | bytes 1179656 | tf_op jit(solution)/shard_map/ppermute | solution.py:39
  108.7 7.4 %collective-permute-done.14 = bf16[3,2,128,256]{3,2,1,0:T(8,128)(2,1)S(1)} collective-permute-done((bf16[3,2,128,256]{3,2,1,0:T(8,128)(2,1)S(1)}, bf16[3,2,128,256]{3,2,1,0:T(8,128)(2,1)S(1)}, u32[]{:S(2)}, u32[]{:S(2)}) %collective-permute-start.14) | collective-permute-done | bytes 393248 | tf_op jit(solution)/shard_map/ppermute | solution.py:38
  118.1 4.6 %collective-permute-start.16 = (bf16[3,1,128,256]{3,2,1,0:T(8,128)(2,1)S(1)}, bf16[3,1,128,256]{3,2,1,0:T(8,128)(2,1)S(1)}, u32[]{:S(2)}, u32[]{:S(2)}) collective-permute-start(bf16[3,1,128,256]{3,2,1,0:T(8,128)(2,1)S(1)} %slice.144), channel_id=1, source_target_pairs={{0,240},{16,0},{32,16},{48,32},{64,48},{80,64},{96,80},{112,96},{1... | collective-permute-start | bytes 589832 | tf_op jit(solution)/shard_map/ppermute | solution.py:43
  131.4 7.0 %convolution_bitcast_fusion = f32[3,512,256]{2,1,0:T(8,128)S(1)} fusion(bf16[512,4096,1]{1,0,2:T(8,128)(2,1)} %bitcast.36, bf16[3,4096,256]{2,1,0:T(8,128)(2,1)} %bitcast.34), kind=kOutput, calls=%fused_computation | convolution fusion | flops 3221225472 | bytes 12058624 | tf_op jit(solution)/shard_map/sk,ikc->isc/dot_general | solution.py:72
  139.9 20.5 %all_to_all.10 = bf16[16,48,256]{2,1,0:T(8,128)(2,1)S(1)} all-to-all(bf16[16,48,256]{2,1,0:T(8,128)(2,1)S(1)} %pad_maximum_fusion.1), channel_id=1, replica_groups=mesh['fsdp'=32,'tp'=16] {'tp'}, dimensions={0} | all-to-all | bytes 786432 | tf_op jit(solution)/shard_map/all_to_all | solution.py:97
  (64 shorter events, 30.2 us)
Async XLA Ops:
  0.6 7.2 %collective-permute-start = (bf16[3,128,256]{2,1,0:T(8,128)(2,1)}, bf16[3,128,256]{2,1,0:T(8,128)(2,1)S(1)}, u32[]{:S(2)}, u32[]{:S(2)}) collective-permute-start(bf16[3,128,256]{2,1,0:T(8,128)(2,1)} %param.13), channel_id=1, source_target_pairs={{0,256},{16,272},{32,288},{48,304},{64,320},{80,336},{96,352},{112... | collective-permute-start | bytes 589832 | tf_op jit(solution)/shard_map/ppermute | solution.py:29
  8.8 19.5 %collective-permute-start.1 = (bf16[3,2,128,256]{3,2,1,0:T(8,128)(2,1)S(1)}, bf16[3,2,128,256]{3,2,1,0:T(8,128)(2,1)S(1)}, u32[]{:S(2)}, u32[]{:S(2)}) collective-permute-start(bf16[3,2,128,256]{3,2,1,0:T(8,128)(2,1)S(1)} %pad_maximum_fusion), channel_id=1, source_target_pairs={{0,240},{16,0},{32,16},{48,32},{64,48},{80,64},{96,80},{112,96},{1... | collective-permute-start | bytes 1179656 | tf_op jit(solution)/shard_map/ppermute | solution.py:39
  21.5 12.2 %collective-permute-start.8 = (bf16[3,2,128,256]{3,2,1,0:T(8,128)(2,1)S(1)}, bf16[3,2,128,256]{3,2,1,0:T(8,128)(2,1)S(1)}, u32[]{:S(2)}, u32[]{:S(2)}) collective-permute-start(bf16[3,2,128,256]{3,2,1,0:T(8,128)(2,1)S(1)} %pad_maximum_fusion), channel_id=1, source_target_pairs={{0,16},{16,32},{32,48},{48,64},{64,80},{80,96},{96,112},{112,128},... | collective-permute-start | bytes 1179656 | tf_op jit(solution)/shard_map/ppermute | solution.py:38
  28.3 11.2 %collective-permute-start.2 = (bf16[3,2,128,256]{3,2,1,0:T(8,128)(2,1)S(1)}, bf16[3,2,128,256]{3,2,1,0:T(8,128)(2,1)S(1)}, u32[]{:S(2)}, u32[]{:S(2)}) collective-permute-start(bf16[3,2,128,256]{3,2,1,0:T(8,128)(2,1)S(1)} %collective-permute-done.1), channel_id=1, source_target_pairs={{0,240},{16,0},{32,16},{48,32},{64,48},{80,64},{96,80},{112,96},{1... | collective-permute-start | bytes 1179656 | tf_op jit(solution)/shard_map/ppermute | solution.py:39
  33.6 11.2 %collective-permute-start.9 = (bf16[3,2,128,256]{3,2,1,0:T(8,128)(2,1)S(1)}, bf16[3,2,128,256]{3,2,1,0:T(8,128)(2,1)S(1)}, u32[]{:S(2)}, u32[]{:S(2)}) collective-permute-start(bf16[3,2,128,256]{3,2,1,0:T(8,128)(2,1)S(1)} %collective-permute-done.8), channel_id=1, source_target_pairs={{0,16},{16,32},{32,48},{48,64},{64,80},{80,96},{96,112},{112,128},... | collective-permute-start | bytes 1179656 | tf_op jit(solution)/shard_map/ppermute | solution.py:38
  39.5 22.0 %collective-permute-start.3 = (bf16[3,2,128,256]{3,2,1,0:T(8,128)(2,1)S(1)}, bf16[3,2,128,256]{3,2,1,0:T(8,128)(2,1)S(1)}, u32[]{:S(2)}, u32[]{:S(2)}) collective-permute-start(bf16[3,2,128,256]{3,2,1,0:T(8,128)(2,1)S(1)} %collective-permute-done.2), channel_id=1, source_target_pairs={{0,240},{16,0},{32,16},{48,32},{64,48},{80,64},{96,80},{112,96},{1... | collective-permute-start | bytes 1179656 | tf_op jit(solution)/shard_map/ppermute | solution.py:39
  44.9 21.5 %collective-permute-start.10 = (bf16[3,2,128,256]{3,2,1,0:T(8,128)(2,1)S(1)}, bf16[3,2,128,256]{3,2,1,0:T(8,128)(2,1)S(1)}, u32[]{:S(2)}, u32[]{:S(2)}) collective-permute-start(bf16[3,2,128,256]{3,2,1,0:T(8,128)(2,1)S(1)} %collective-permute-done.9), channel_id=1, source_target_pairs={{0,16},{16,32},{32,48},{48,64},{64,80},{80,96},{96,112},{112,128},... | collective-permute-start | bytes 1179656 | tf_op jit(solution)/shard_map/ppermute | solution.py:38
  48.3 20.0 %copy-start.1 = (s32[1,512]{1,0:T(1,128)S(1)}, s32[1,512]{1,0:T(1,128)}, u32[]{:S(2)}) copy-start(s32[1,512]{1,0:T(1,128)} %param.15) | copy-start | bytes 6148
  48.3 20.1 %copy-start = (f32[16,7]{0,1:T(8,128)S(1)}, f32[16,7]{0,1:T(8,128)}, u32[]{:S(2)}) copy-start(f32[16,7]{0,1:T(8,128)} %param.14) | copy-start | bytes 1348
  50.9 80.5 %all-to-all-start = ((bf16[16,32,4096]{2,1,0:T(8,128)(2,1)}), bf16[16,32,4096]{2,1,0:T(8,128)(2,1)}, u32[]{:S(2)}, u32[]{:S(2)}) async-start(bf16[16,32,4096]{2,1,0:T(8,128)(2,1)} %broadcast_in_dim.9), calls=%async_computation | async-start | bytes 8388608 | tf_op jit(solution)/shard_map/all_to_all | solution.py:69
  61.5 13.2 %collective-permute-start.4 = (bf16[3,2,128,256]{3,2,1,0:T(8,128)(2,1)S(1)}, bf16[3,2,128,256]{3,2,1,0:T(8,128)(2,1)}, u32[]{:S(2)}, u32[]{:S(2)}) collective-permute-start(bf16[3,2,128,256]{3,2,1,0:T(8,128)(2,1)S(1)} %collective-permute-done.3), channel_id=1, source_target_pairs={{0,240},{16,0},{32,16},{48,32},{64,48},{80,64},{96,80},{112,96},{1... | collective-permute-start | bytes 1179656 | tf_op jit(solution)/shard_map/ppermute | solution.py:39
  66.4 13.8 %collective-permute-start.11 = (bf16[3,2,128,256]{3,2,1,0:T(8,128)(2,1)S(1)}, bf16[3,2,128,256]{3,2,1,0:T(8,128)(2,1)S(1)}, u32[]{:S(2)}, u32[]{:S(2)}) collective-permute-start(bf16[3,2,128,256]{3,2,1,0:T(8,128)(2,1)S(1)} %collective-permute-done.10), channel_id=1, source_target_pairs={{0,16},{16,32},{32,48},{48,64},{64,80},{80,96},{96,112},{112,128},... | collective-permute-start | bytes 1179656 | tf_op jit(solution)/shard_map/ppermute | solution.py:38
  74.7 13.2 %collective-permute-start.5 = (bf16[3,2,128,256]{3,2,1,0:T(8,128)(2,1)}, bf16[3,2,128,256]{3,2,1,0:T(8,128)(2,1)S(1)}, u32[]{:S(2)}, u32[]{:S(2)}) collective-permute-start(bf16[3,2,128,256]{3,2,1,0:T(8,128)(2,1)} %collective-permute-done.4), channel_id=1, source_target_pairs={{0,240},{16,0},{32,16},{48,32},{64,48},{80,64},{96,80},{112,96},{1... | collective-permute-start | bytes 1179656 | tf_op jit(solution)/shard_map/ppermute | solution.py:39
  80.2 13.1 %collective-permute-start.12 = (bf16[3,2,128,256]{3,2,1,0:T(8,128)(2,1)S(1)}, bf16[3,2,128,256]{3,2,1,0:T(8,128)(2,1)S(1)}, u32[]{:S(2)}, u32[]{:S(2)}) collective-permute-start(bf16[3,2,128,256]{3,2,1,0:T(8,128)(2,1)S(1)} %collective-permute-done.11), channel_id=1, source_target_pairs={{0,16},{16,32},{32,48},{48,64},{64,80},{80,96},{96,112},{112,128},... | collective-permute-start | bytes 1179656 | tf_op jit(solution)/shard_map/ppermute | solution.py:38
  87.9 11.9 %collective-permute-start.6 = (bf16[3,2,128,256]{3,2,1,0:T(8,128)(2,1)S(1)}, bf16[3,2,128,256]{3,2,1,0:T(8,128)(2,1)S(1)}, u32[]{:S(2)}, u32[]{:S(2)}) collective-permute-start(bf16[3,2,128,256]{3,2,1,0:T(8,128)(2,1)S(1)} %collective-permute-done.5), channel_id=1, source_target_pairs={{0,240},{16,0},{32,16},{48,32},{64,48},{80,64},{96,80},{112,96},{1... | collective-permute-start | bytes 1179656 | tf_op jit(solution)/shard_map/ppermute | solution.py:39
  93.2 12.0 %collective-permute-start.13 = (bf16[3,2,128,256]{3,2,1,0:T(8,128)(2,1)S(1)}, bf16[3,2,128,256]{3,2,1,0:T(8,128)(2,1)S(1)}, u32[]{:S(2)}, u32[]{:S(2)}) collective-permute-start(bf16[3,2,128,256]{3,2,1,0:T(8,128)(2,1)S(1)} %collective-permute-done.12), channel_id=1, source_target_pairs={{0,16},{16,32},{32,48},{48,64},{64,80},{80,96},{96,112},{112,128},... | collective-permute-start | bytes 1179656 | tf_op jit(solution)/shard_map/ppermute | solution.py:38
  99.8 18.2 %collective-permute-start.7 = (bf16[3,2,128,256]{3,2,1,0:T(8,128)(2,1)S(1)}, bf16[3,2,128,256]{3,2,1,0:T(8,128)(2,1)S(1)}, u32[]{:S(2)}, u32[]{:S(2)}) collective-permute-start(bf16[3,2,128,256]{3,2,1,0:T(8,128)(2,1)S(1)} %collective-permute-done.6), channel_id=1, source_target_pairs={{0,240},{16,0},{32,16},{48,32},{64,48},{80,64},{96,80},{112,96},{1... | collective-permute-start | bytes 1179656 | tf_op jit(solution)/shard_map/ppermute | solution.py:39
  105.3 10.8 %collective-permute-start.14 = (bf16[3,2,128,256]{3,2,1,0:T(8,128)(2,1)S(1)}, bf16[3,2,128,256]{3,2,1,0:T(8,128)(2,1)S(1)}, u32[]{:S(2)}, u32[]{:S(2)}) collective-permute-start(bf16[3,2,128,256]{3,2,1,0:T(8,128)(2,1)S(1)} %collective-permute-done.13), channel_id=1, source_target_pairs={{0,16},{16,32},{32,48},{48,64},{64,80},{80,96},{96,112},{112,128},... | collective-permute-start | bytes 1179656 | tf_op jit(solution)/shard_map/ppermute | solution.py:38
  116.1 7.6 %collective-permute-start.15 = (bf16[3,1,128,256]{3,2,1,0:T(8,128)(2,1)S(1)}, bf16[3,1,128,256]{3,2,1,0:T(8,128)(2,1)S(1)}, u32[]{:S(2)}, u32[]{:S(2)}) collective-permute-start(bf16[3,1,128,256]{3,2,1,0:T(8,128)(2,1)S(1)} %slice.143), channel_id=1, source_target_pairs={{0,16},{16,32},{32,48},{48,64},{64,80},{80,96},{96,112},{112,128},... | collective-permute-start | bytes 589832 | tf_op jit(solution)/shard_map/ppermute | solution.py:42
  118.1 7.2 %collective-permute-start.16 = (bf16[3,1,128,256]{3,2,1,0:T(8,128)(2,1)S(1)}, bf16[3,1,128,256]{3,2,1,0:T(8,128)(2,1)S(1)}, u32[]{:S(2)}, u32[]{:S(2)}) collective-permute-start(bf16[3,1,128,256]{3,2,1,0:T(8,128)(2,1)S(1)} %slice.144), channel_id=1, source_target_pairs={{0,240},{16,0},{32,16},{48,32},{64,48},{80,64},{96,80},{112,96},{1... | collective-permute-start | bytes 589832 | tf_op jit(solution)/shard_map/ppermute | solution.py:43
  131.4 8.0 %copy-start.2 = (s32[1,16]{1,0:T(1,128)S(1)}, s32[1,16]{1,0:T(1,128)}, u32[]{:S(2)}) copy-start(s32[1,16]{1,0:T(1,128)} %param.16) | copy-start | bytes 196

commit v6 on v5

--- a/solution.py
+++ b/solution.py
@@ -20,7 +20,7 @@
     return filtered
 
 
-def gather_weights(proj_weight, fsdp_size, z_size):
+def gather_weights(proj_weight, fsdp_size, z_size, companion):
     fsdp = lax.axis_index("fsdp")
     x_lo = fsdp // z_size
     x_swap = [(f, (f + z_size) % fsdp_size) for f in range(fsdp_size)]
@@ -39,14 +39,16 @@
         left = lax.ppermute(left, "fsdp", z_down)
         behind.append(right)
         ahead.append(left)
-    last_a = lax.ppermute(right[:, :1], "fsdp", z_up)
-    last_b = lax.ppermute(left[:, 1:], "fsdp", z_down)
-    ahead.append(jnp.concatenate([last_a, last_b], axis=1))
-    pieces = ahead + behind[::-1]
-    stacked = with_layout_constraint(jnp.stack(pieces, axis=2), Layout((0, 1, 2, 3, 4)))
-    return stacked.reshape(
-        proj_weight.shape[0], fsdp_size * proj_weight.shape[1], proj_weight.shape[2]
+    sent_a, sent_b, companion = lax.optimization_barrier((right[:, :1], left[:, 1:], companion))
+    last_a = lax.ppermute(sent_a, "fsdp", z_up)
+    last_b = lax.ppermute(sent_b, "fsdp", z_down)
+    last = jnp.concatenate([last_a, last_b], axis=1)
+    stacked = with_layout_constraint(
+        jnp.stack(ahead + behind[::-1], axis=1), Layout((0, 1, 2, 3, 4))
     )
+    lead, count, halves, block, width = stacked.shape
+    early = stacked.reshape(lead, count * halves * block, width)
+    return early, last.reshape(lead, halves * block, width), companion
 
 
 def local(activations, norm_gain, proj_weight, short_filter, segment_ids, needle_pos, readout):
@@ -57,19 +59,34 @@
     z_size = fsdp_size // 2
     channels = proj_weight.shape[2]
     block = proj_weight.shape[1]
-    weights = gather_weights(proj_weight, fsdp_size, z_size)
     values = activations.astype(jnp.float32)
     scaled = lax.rsqrt(jnp.mean(values * values, axis=1, keepdims=True) + EPSILON)
     normed = (values * scaled * norm_gain[None, :]).astype(jnp.bfloat16)
     z = lax.axis_index("fsdp") % z_size
-    grid = normed.reshape(local_rows, 2, z_size, block)
-    doubled = jnp.concatenate([grid, grid], axis=2)
-    rotated = lax.dynamic_slice_in_dim(doubled, z, z_size, axis=2).reshape(local_rows, model_width)
-    spread = jnp.broadcast_to(rotated[None], (tp_size,) + rotated.shape)
+    half = z_size // 2
+    grid = jnp.transpose(normed.reshape(local_rows, 2, z_size, block), (0, 2, 1, 3))
+    doubled = jnp.concatenate([grid, grid], axis=1)
+    ordered = jnp.concatenate(
+        [
+            lax.dynamic_slice_in_dim(doubled, z, half, axis=1),
+            lax.dynamic_slice_in_dim(doubled, z + half + 1, half - 1, axis=1),
+            lax.dynamic_slice_in_dim(doubled, z + half, 1, axis=1),
+        ],
+        axis=1,
+    ).reshape(local_rows, model_width)
+    spread = jnp.broadcast_to(ordered[None], (tp_size,) + ordered.shape)
     slab_rows = lax.all_to_all(spread, "tp", 0, 0, tiled=False).reshape(
         tp_size * local_rows, model_width
     )
-    projected = jnp.einsum("sk,ikc->isc", slab_rows, weights, preferred_element_type=jnp.float32)
+    early_weights, last_weights, slab_rows = gather_weights(
+        proj_weight, fsdp_size, z_size, slab_rows
+    )
+    split = early_weights.shape[1]
+    projected = jnp.einsum(
+        "sk,ikc->isc", slab_rows[:, :split], early_weights, preferred_element_type=jnp.float32
+    ) + jnp.einsum(
+        "sk,ikc->isc", slab_rows[:, split:], last_weights, preferred_element_type=jnp.float32
+    )
     projected = with_layout_constraint(projected, Layout((0, 1, 2)))
     gated_prod = projected[1] * projected[2]
     tap_table = jnp.repeat(short_filter, channels // short_filter.shape[0], axis=0)

time: 163 us -> 163 us (level)
  waiting for transfers between devices: 31.2 us -> 28.4 us
    ppermute x7, waiting for transfers between devices: 18.8 us -> 16 us  [gather_weights(): left = lax.ppermute(left, 'fsdp', z_down)]
    dot_general x1 -> x2, matrix products: 7.05 us -> 8.4 us  [the longest x1 7.08 us: local(): jnp.einsum('sk,ikc->isc', slab_rows[:, :split], early_weights, preferred_...]
    unnamed x22 -> x21, local copies, waits for them, and re-layouts: 11.2 us -> 12.3 us
  transfers between devices with their start and end apart: 18 -> 18, of which waited for: 9 -> 9; matrix products, arithmetic and copies ran while one was open for 12% -> 13% of each run, Pallas kernels for 0% -> 0%
where the time goes in v6:
time: 163 us; the launch traced here: 162 us
  starting transfers between devices  78.6 us (48%)
  waiting for transfers between devices  28.4 us (17%)
  blocking collectives  20.5 us (13%)
  local copies, waits for them, and re-layouts  17.9 us (11%)
  matrix products  8.69 us (5%)
  other arithmetic  6.65 us (4%)
    ppermute x7, starting transfers between devices, gather_weights(): left = lax.ppermute(left, 'fsdp', z_down)  44.1 us
    all_to_all x1, blocking collectives, local(): gathered = lax.all_to_all(payload, 'tp', 0, 0, tiled=False)  20.5 us
    ppermute x7, waiting for transfers between devices, gather_weights(): left = lax.ppermute(left, 'fsdp', z_down)  16 us
    ppermute x7, starting transfers between devices, gather_weights(): right = lax.ppermute(right, 'fsdp', z_up)  13.4 us
    unnamed x21, local copies, waits for them, and re-layouts  12.3 us
    all_to_all x1, starting transfers between devices, local(): lax.all_to_all(spread, 'tp', 0, 0, tiled=False)  10.6 us
    ppermute x7, waiting for transfers between devices, gather_weights(): right = lax.ppermute(right, 'fsdp', z_up)  7.35 us
    dot_general x1, matrix products, local(): jnp.einsum('sk,ikc->isc', slab_rows[:, :split], early_weights, preferred_...  7.08 us
  transfers between devices with their start and end apart: 18, of which 9 were waited for; matrix products, arithmetic and copies ran while one was open for 13% of the time, Pallas kernels for 0%

profile of v6, /device:TPU:1, one launch (start us, length us, event | category | flops | bytes accessed | tf_op | source)
XLA Modules:
  0.0 161.8 jit_solution(6404207795840338799)
XLA Ops:
  0.6 3.9 %collective-permute-start = (bf16[3,128,256]{2,1,0:T(8,128)(2,1)}, bf16[3,128,256]{2,1,0:T(8,128)(2,1)S(1)}, u32[]{:S(2)}, u32[]{:S(2)}) collective-permute-start(bf16[3,128,256]{2,1,0:T(8,128)(2,1)} %param.13), channel_id=1, source_target_pairs={{0,256},{16,272},{32,288},{48,304},{64,320},{80,336},{96,352},{112... | collective-permute-start | bytes 589832 | tf_op jit(solution)/shard_map/ppermute | solution.py:29
  4.6 3.2 %collective-permute-done = bf16[3,128,256]{2,1,0:T(8,128)(2,1)S(1)} collective-permute-done((bf16[3,128,256]{2,1,0:T(8,128)(2,1)}, bf16[3,128,256]{2,1,0:T(8,128)(2,1)S(1)}, u32[]{:S(2)}, u32[]{:S(2)}) %collective-permute-start) | collective-permute-done | bytes 196640 | tf_op jit(solution)/shard_map/ppermute | solution.py:29
  8.8 12.6 %collective-permute-start.1 = (bf16[3,2,128,256]{3,2,1,0:T(8,128)(2,1)S(1)}, bf16[3,2,128,256]{3,2,1,0:T(8,128)(2,1)S(1)}, u32[]{:S(2)}, u32[]{:S(2)}) collective-permute-start(bf16[3,2,128,256]{3,2,1,0:T(8,128)(2,1)S(1)} %pad_maximum_fusion), channel_id=1, source_target_pairs={{0,240},{16,0},{32,16},{48,32},{64,48},{80,64},{96,80},{112,96},{1... | collective-permute-start | bytes 1179656 | tf_op jit(solution)/shard_map/ppermute | solution.py:39
  21.5 1.9 %collective-permute-start.8 = (bf16[3,2,128,256]{3,2,1,0:T(8,128)(2,1)S(1)}, bf16[3,2,128,256]{3,2,1,0:T(8,128)(2,1)S(1)}, u32[]{:S(2)}, u32[]{:S(2)}) collective-permute-start(bf16[3,2,128,256]{3,2,1,0:T(8,128)(2,1)S(1)} %pad_maximum_fusion), channel_id=1, source_target_pairs={{0,16},{16,32},{32,48},{48,64},{64,80},{80,96},{96,112},{112,128},... | collective-permute-start | bytes 1179656 | tf_op jit(solution)/shard_map/ppermute | solution.py:38
  24.5 3.8 %collective-permute-done.1 = bf16[3,2,128,256]{3,2,1,0:T(8,128)(2,1)S(1)} collective-permute-done((bf16[3,2,128,256]{3,2,1,0:T(8,128)(2,1)S(1)}, bf16[3,2,128,256]{3,2,1,0:T(8,128)(2,1)S(1)}, u32[]{:S(2)}, u32[]{:S(2)}) %collective-permute-start.1) | collective-permute-done | bytes 393248 | tf_op jit(solution)/shard_map/ppermute | solution.py:39
  28.3 5.3 %collective-permute-start.2 = (bf16[3,2,128,256]{3,2,1,0:T(8,128)(2,1)S(1)}, bf16[3,2,128,256]{3,2,1,0:T(8,128)(2,1)S(1)}, u32[]{:S(2)}, u32[]{:S(2)}) collective-permute-start(bf16[3,2,128,256]{3,2,1,0:T(8,128)(2,1)S(1)} %collective-permute-done.1), channel_id=1, source_target_pairs={{0,240},{16,0},{32,16},{48,32},{64,48},{80,64},{96,80},{112,96},{1... | collective-permute-start | bytes 1179656 | tf_op jit(solution)/shard_map/ppermute | solution.py:39
  33.6 1.9 %collective-permute-start.9 = (bf16[3,2,128,256]{3,2,1,0:T(8,128)(2,1)S(1)}, bf16[3,2,128,256]{3,2,1,0:T(8,128)(2,1)S(1)}, u32[]{:S(2)}, u32[]{:S(2)}) collective-permute-start(bf16[3,2,128,256]{3,2,1,0:T(8,128)(2,1)S(1)} %collective-permute-done.8), channel_id=1, source_target_pairs={{0,16},{16,32},{32,48},{48,64},{64,80},{80,96},{96,112},{112,128},... | collective-permute-start | bytes 1179656 | tf_op jit(solution)/shard_map/ppermute | solution.py:38
  37.6 1.9 %collective-permute-done.2 = bf16[3,2,128,256]{3,2,1,0:T(8,128)(2,1)S(1)} collective-permute-done((bf16[3,2,128,256]{3,2,1,0:T(8,128)(2,1)S(1)}, bf16[3,2,128,256]{3,2,1,0:T(8,128)(2,1)S(1)}, u32[]{:S(2)}, u32[]{:S(2)}) %collective-permute-start.2) | collective-permute-done | bytes 393248 | tf_op jit(solution)/shard_map/ppermute | solution.py:39
  39.5 5.3 %collective-permute-start.3 = (bf16[3,2,128,256]{3,2,1,0:T(8,128)(2,1)S(1)}, bf16[3,2,128,256]{3,2,1,0:T(8,128)(2,1)}, u32[]{:S(2)}, u32[]{:S(2)}) collective-permute-start(bf16[3,2,128,256]{3,2,1,0:T(8,128)(2,1)S(1)} %collective-permute-done.2), channel_id=1, source_target_pairs={{0,240},{16,0},{32,16},{48,32},{64,48},{80,64},{96,80},{112,96},{1... | collective-permute-start | bytes 1179656 | tf_op jit(solution)/shard_map/ppermute | solution.py:39
  44.9 1.9 %collective-permute-start.10 = (bf16[3,2,128,256]{3,2,1,0:T(8,128)(2,1)S(1)}, bf16[3,2,128,256]{3,2,1,0:T(8,128)(2,1)S(1)}, u32[]{:S(2)}, u32[]{:S(2)}) collective-permute-start(bf16[3,2,128,256]{3,2,1,0:T(8,128)(2,1)S(1)} %collective-permute-done.9), channel_id=1, source_target_pairs={{0,16},{16,32},{32,48},{48,64},{64,80},{80,96},{96,112},{112,128},... | collective-permute-start | bytes 1179656 | tf_op jit(solution)/shard_map/ppermute | solution.py:38
  47.5 2.6 %broadcast_in_dim.9 = bf16[16,32,4096]{2,1,0:T(8,128)(2,1)} broadcast(bf16[32,4096]{1,0:T(8,128)(2,1)S(1)} %broadcast_in_dim.8), dimensions={1,2} | broadcast | bytes 4456448 | tf_op jit(solution)/shard_map/broadcast_in_dim | solution.py:77
  50.0 10.6 %all-to-all-start = ((bf16[16,32,4096]{2,1,0:T(8,128)(2,1)}), bf16[16,32,4096]{2,1,0:T(8,128)(2,1)}, u32[]{:S(2)}, u32[]{:S(2)}) async-start(bf16[16,32,4096]{2,1,0:T(8,128)(2,1)} %broadcast_in_dim.9), calls=%async_computation | async-start | bytes 8388608 | tf_op jit(solution)/shard_map/all_to_all | solution.py:78
  60.6 4.9 %collective-permute-start.4 = (bf16[3,2,128,256]{3,2,1,0:T(8,128)(2,1)}, bf16[3,2,128,256]{3,2,1,0:T(8,128)(2,1)}, u32[]{:S(2)}, u32[]{:S(2)}) collective-permute-start(bf16[3,2,128,256]{3,2,1,0:T(8,128)(2,1)} %collective-permute-done.3), channel_id=1, source_target_pairs={{0,240},{16,0},{32,16},{48,32},{64,48},{80,64},{96,80},{112,96},{1... | collective-permute-start | bytes 1179656 | tf_op jit(solution)/shard_map/ppermute | solution.py:39
  65.5 1.9 %collective-permute-start.11 = (bf16[3,2,128,256]{3,2,1,0:T(8,128)(2,1)S(1)}, bf16[3,2,128,256]{3,2,1,0:T(8,128)(2,1)S(1)}, u32[]{:S(2)}, u32[]{:S(2)}) collective-permute-start(bf16[3,2,128,256]{3,2,1,0:T(8,128)(2,1)S(1)} %collective-permute-done.10), channel_id=1, source_target_pairs={{0,16},{16,32},{32,48},{48,64},{64,80},{80,96},{96,112},{112,128},... | collective-permute-start | bytes 1179656 | tf_op jit(solution)/shard_map/ppermute | solution.py:38
  69.3 4.9 %collective-permute-done.4 = bf16[3,2,128,256]{3,2,1,0:T(8,128)(2,1)} collective-permute-done((bf16[3,2,128,256]{3,2,1,0:T(8,128)(2,1)}, bf16[3,2,128,256]{3,2,1,0:T(8,128)(2,1)}, u32[]{:S(2)}, u32[]{:S(2)}) %collective-permute-start.4) | collective-permute-done | bytes 393248 | tf_op jit(solution)/shard_map/ppermute | solution.py:39
  74.2 5.3 %collective-permute-start.5 = (bf16[3,2,128,256]{3,2,1,0:T(8,128)(2,1)}, bf16[3,2,128,256]{3,2,1,0:T(8,128)(2,1)S(1)}, u32[]{:S(2)}, u32[]{:S(2)}) collective-permute-start(bf16[3,2,128,256]{3,2,1,0:T(8,128)(2,1)} %collective-permute-done.4), channel_id=1, source_target_pairs={{0,240},{16,0},{32,16},{48,32},{64,48},{80,64},{96,80},{112,96},{1... | collective-permute-start | bytes 1179656 | tf_op jit(solution)/shard_map/ppermute | solution.py:39
  79.5 1.9 %collective-permute-start.12 = (bf16[3,2,128,256]{3,2,1,0:T(8,128)(2,1)S(1)}, bf16[3,2,128,256]{3,2,1,0:T(8,128)(2,1)S(1)}, u32[]{:S(2)}, u32[]{:S(2)}) collective-permute-start(bf16[3,2,128,256]{3,2,1,0:T(8,128)(2,1)S(1)} %collective-permute-done.11), channel_id=1, source_target_pairs={{0,16},{16,32},{32,48},{48,64},{64,80},{80,96},{96,112},{112,128},... | collective-permute-start | bytes 1179656 | tf_op jit(solution)/shard_map/ppermute | solution.py:38
  83.0 4.3 %collective-permute-done.5 = bf16[3,2,128,256]{3,2,1,0:T(8,128)(2,1)S(1)} collective-permute-done((bf16[3,2,128,256]{3,2,1,0:T(8,128)(2,1)}, bf16[3,2,128,256]{3,2,1,0:T(8,128)(2,1)S(1)}, u32[]{:S(2)}, u32[]{:S(2)}) %collective-permute-start.5) | collective-permute-done | bytes 393248 | tf_op jit(solution)/shard_map/ppermute | solution.py:39
  87.2 5.3 %collective-permute-start.6 = (bf16[3,2,128,256]{3,2,1,0:T(8,128)(2,1)S(1)}, bf16[3,2,128,256]{3,2,1,0:T(8,128)(2,1)S(1)}, u32[]{:S(2)}, u32[]{:S(2)}) collective-permute-start(bf16[3,2,128,256]{3,2,1,0:T(8,128)(2,1)S(1)} %collective-permute-done.5), channel_id=1, source_target_pairs={{0,240},{16,0},{32,16},{48,32},{64,48},{80,64},{96,80},{112,96},{1... | collective-permute-start | bytes 1179656 | tf_op jit(solution)/shard_map/ppermute | solution.py:39
  99.2 5.4 %collective-permute-start.7 = (bf16[3,2,128,256]{3,2,1,0:T(8,128)(2,1)S(1)}, bf16[3,2,128,256]{3,2,1,0:T(8,128)(2,1)S(1)}, u32[]{:S(2)}, u32[]{:S(2)}) collective-permute-start(bf16[3,2,128,256]{3,2,1,0:T(8,128)(2,1)S(1)} %collective-permute-done.6), channel_id=1, source_target_pairs={{0,240},{16,0},{32,16},{48,32},{64,48},{80,64},{96,80},{112,96},{1... | collective-permute-start | bytes 1179656 | tf_op jit(solution)/shard_map/ppermute | solution.py:39
  108.1 7.3 %collective-permute-done.14 = bf16[3,2,128,256]{3,2,1,0:T(8,128)(2,1)S(1)} collective-permute-done((bf16[3,2,128,256]{3,2,1,0:T(8,128)(2,1)S(1)}, bf16[3,2,128,256]{3,2,1,0:T(8,128)(2,1)S(1)}, u32[]{:S(2)}, u32[]{:S(2)}) %collective-permute-start.14) | collective-permute-done | bytes 393248 | tf_op jit(solution)/shard_map/ppermute | solution.py:38
  122.9 4.6 %collective-permute-start.16 = (bf16[3,1,128,256]{3,2,1,0:T(8,128)(2,1)S(1)}, bf16[3,1,128,256]{3,2,1,0:T(8,128)(2,1)S(1)}, u32[]{:S(2)}, u32[]{:S(2)}) collective-permute-start(bf16[3,1,128,256]{3,2,1,0:T(8,128)(2,1)S(1)} %slice.152), channel_id=1, source_target_pairs={{0,240},{16,0},{32,16},{48,32},{64,48},{80,64},{96,80},{112,96},{1... | collective-permute-start | bytes 589832 | tf_op jit(solution)/shard_map/ppermute | solution.py:44
  131.5 7.1 %add_bitcast_fusion = f32[3,512,256]{2,1,0:T(8,128)S(1)} fusion(f32[3,256,512]{1,2,0:T(8,128)S(1)} %fusion.31, bf16[3,3840,256]{2,1,0:T(8,128)(2,1)} %bitcast.32, bf16[512,4096]{1,0:T(8,128)(2,1)} %bitcast.34), kind=kOutput, calls=%fused_computation.3 | convolution fusion | flops 3020292096 | bytes 12976128 | tf_op jit(solution)/shard_map/sk,ikc->isc/dot_general | solution.py:85
  140.0 20.5 %all_to_all.10 = bf16[16,48,256]{2,1,0:T(8,128)(2,1)S(1)} all-to-all(bf16[16,48,256]{2,1,0:T(8,128)(2,1)S(1)} %pad_maximum_fusion.2), channel_id=1, replica_groups=mesh['fsdp'=32,'tp'=16] {'tp'}, dimensions={0} | all-to-all | bytes 786432 | tf_op jit(solution)/shard_map/all_to_all | solution.py:114
  (69 shorter events, 32.3 us)
Async XLA Ops:
  0.6 7.2 %collective-permute-start = (bf16[3,128,256]{2,1,0:T(8,128)(2,1)}, bf16[3,128,256]{2,1,0:T(8,128)(2,1)S(1)}, u32[]{:S(2)}, u32[]{:S(2)}) collective-permute-start(bf16[3,128,256]{2,1,0:T(8,128)(2,1)} %param.13), channel_id=1, source_target_pairs={{0,256},{16,272},{32,288},{48,304},{64,320},{80,336},{96,352},{112... | collective-permute-start | bytes 589832 | tf_op jit(solution)/shard_map/ppermute | solution.py:29
  8.8 19.5 %collective-permute-start.1 = (bf16[3,2,128,256]{3,2,1,0:T(8,128)(2,1)S(1)}, bf16[3,2,128,256]{3,2,1,0:T(8,128)(2,1)S(1)}, u32[]{:S(2)}, u32[]{:S(2)}) collective-permute-start(bf16[3,2,128,256]{3,2,1,0:T(8,128)(2,1)S(1)} %pad_maximum_fusion), channel_id=1, source_target_pairs={{0,240},{16,0},{32,16},{48,32},{64,48},{80,64},{96,80},{112,96},{1... | collective-permute-start | bytes 1179656 | tf_op jit(solution)/shard_map/ppermute | solution.py:39
  21.5 12.2 %collective-permute-start.8 = (bf16[3,2,128,256]{3,2,1,0:T(8,128)(2,1)S(1)}, bf16[3,2,128,256]{3,2,1,0:T(8,128)(2,1)S(1)}, u32[]{:S(2)}, u32[]{:S(2)}) collective-permute-start(bf16[3,2,128,256]{3,2,1,0:T(8,128)(2,1)S(1)} %pad_maximum_fusion), channel_id=1, source_target_pairs={{0,16},{16,32},{32,48},{48,64},{64,80},{80,96},{96,112},{112,128},... | collective-permute-start | bytes 1179656 | tf_op jit(solution)/shard_map/ppermute | solution.py:38
  28.3 11.2 %collective-permute-start.2 = (bf16[3,2,128,256]{3,2,1,0:T(8,128)(2,1)S(1)}, bf16[3,2,128,256]{3,2,1,0:T(8,128)(2,1)S(1)}, u32[]{:S(2)}, u32[]{:S(2)}) collective-permute-start(bf16[3,2,128,256]{3,2,1,0:T(8,128)(2,1)S(1)} %collective-permute-done.1), channel_id=1, source_target_pairs={{0,240},{16,0},{32,16},{48,32},{64,48},{80,64},{96,80},{112,96},{1... | collective-permute-start | bytes 1179656 | tf_op jit(solution)/shard_map/ppermute | solution.py:39
  33.6 11.2 %collective-permute-start.9 = (bf16[3,2,128,256]{3,2,1,0:T(8,128)(2,1)S(1)}, bf16[3,2,128,256]{3,2,1,0:T(8,128)(2,1)S(1)}, u32[]{:S(2)}, u32[]{:S(2)}) collective-permute-start(bf16[3,2,128,256]{3,2,1,0:T(8,128)(2,1)S(1)} %collective-permute-done.8), channel_id=1, source_target_pairs={{0,16},{16,32},{32,48},{48,64},{64,80},{80,96},{96,112},{112,128},... | collective-permute-start | bytes 1179656 | tf_op jit(solution)/shard_map/ppermute | solution.py:38
  39.5 21.1 %collective-permute-start.3 = (bf16[3,2,128,256]{3,2,1,0:T(8,128)(2,1)S(1)}, bf16[3,2,128,256]{3,2,1,0:T(8,128)(2,1)}, u32[]{:S(2)}, u32[]{:S(2)}) collective-permute-start(bf16[3,2,128,256]{3,2,1,0:T(8,128)(2,1)S(1)} %collective-permute-done.2), channel_id=1, source_target_pairs={{0,240},{16,0},{32,16},{48,32},{64,48},{80,64},{96,80},{112,96},{1... | collective-permute-start | bytes 1179656 | tf_op jit(solution)/shard_map/ppermute | solution.py:39
  44.9 20.6 %collective-permute-start.10 = (bf16[3,2,128,256]{3,2,1,0:T(8,128)(2,1)S(1)}, bf16[3,2,128,256]{3,2,1,0:T(8,128)(2,1)S(1)}, u32[]{:S(2)}, u32[]{:S(2)}) collective-permute-start(bf16[3,2,128,256]{3,2,1,0:T(8,128)(2,1)S(1)} %collective-permute-done.9), channel_id=1, source_target_pairs={{0,16},{16,32},{32,48},{48,64},{64,80},{80,96},{96,112},{112,128},... | collective-permute-start | bytes 1179656 | tf_op jit(solution)/shard_map/ppermute | solution.py:38
  47.4 20.0 %copy-start.1 = (s32[1,512]{1,0:T(1,128)S(1)}, s32[1,512]{1,0:T(1,128)}, u32[]{:S(2)}) copy-start(s32[1,512]{1,0:T(1,128)} %param.15) | copy-start | bytes 6148
  47.4 20.1 %copy-start = (f32[16,7]{0,1:T(8,128)S(1)}, f32[16,7]{0,1:T(8,128)}, u32[]{:S(2)}) copy-start(f32[16,7]{0,1:T(8,128)} %param.14) | copy-start | bytes 1348
  50.0 71.0 %all-to-all-start = ((bf16[16,32,4096]{2,1,0:T(8,128)(2,1)}), bf16[16,32,4096]{2,1,0:T(8,128)(2,1)}, u32[]{:S(2)}, u32[]{:S(2)}) async-start(bf16[16,32,4096]{2,1,0:T(8,128)(2,1)} %broadcast_in_dim.9), calls=%async_computation | async-start | bytes 8388608 | tf_op jit(solution)/shard_map/all_to_all | solution.py:78
  60.6 13.5 %collective-permute-start.4 = (bf16[3,2,128,256]{3,2,1,0:T(8,128)(2,1)}, bf16[3,2,128,256]{3,2,1,0:T(8,128)(2,1)}, u32[]{:S(2)}, u32[]{:S(2)}) collective-permute-start(bf16[3,2,128,256]{3,2,1,0:T(8,128)(2,1)} %collective-permute-done.3), channel_id=1, source_target_pairs={{0,240},{16,0},{32,16},{48,32},{64,48},{80,64},{96,80},{112,96},{1... | collective-permute-start | bytes 1179656 | tf_op jit(solution)/shard_map/ppermute | solution.py:39
  65.5 14.0 %collective-permute-start.11 = (bf16[3,2,128,256]{3,2,1,0:T(8,128)(2,1)S(1)}, bf16[3,2,128,256]{3,2,1,0:T(8,128)(2,1)S(1)}, u32[]{:S(2)}, u32[]{:S(2)}) collective-permute-start(bf16[3,2,128,256]{3,2,1,0:T(8,128)(2,1)S(1)} %collective-permute-done.10), channel_id=1, source_target_pairs={{0,16},{16,32},{32,48},{48,64},{64,80},{80,96},{96,112},{112,128},... | collective-permute-start | bytes 1179656 | tf_op jit(solution)/shard_map/ppermute | solution.py:38
  74.2 13.1 %collective-permute-start.5 = (bf16[3,2,128,256]{3,2,1,0:T(8,128)(2,1)}, bf16[3,2,128,256]{3,2,1,0:T(8,128)(2,1)S(1)}, u32[]{:S(2)}, u32[]{:S(2)}) collective-permute-start(bf16[3,2,128,256]{3,2,1,0:T(8,128)(2,1)} %collective-permute-done.4), channel_id=1, source_target_pairs={{0,240},{16,0},{32,16},{48,32},{64,48},{80,64},{96,80},{112,96},{1... | collective-permute-start | bytes 1179656 | tf_op jit(solution)/shard_map/ppermute | solution.py:39
  79.5 13.1 %collective-permute-start.12 = (bf16[3,2,128,256]{3,2,1,0:T(8,128)(2,1)S(1)}, bf16[3,2,128,256]{3,2,1,0:T(8,128)(2,1)S(1)}, u32[]{:S(2)}, u32[]{:S(2)}) collective-permute-start(bf16[3,2,128,256]{3,2,1,0:T(8,128)(2,1)S(1)} %collective-permute-done.11), channel_id=1, source_target_pairs={{0,16},{16,32},{32,48},{48,64},{64,80},{80,96},{96,112},{112,128},... | collective-permute-start | bytes 1179656 | tf_op jit(solution)/shard_map/ppermute | solution.py:38
  87.2 11.9 %collective-permute-start.6 = (bf16[3,2,128,256]{3,2,1,0:T(8,128)(2,1)S(1)}, bf16[3,2,128,256]{3,2,1,0:T(8,128)(2,1)S(1)}, u32[]{:S(2)}, u32[]{:S(2)}) collective-permute-start(bf16[3,2,128,256]{3,2,1,0:T(8,128)(2,1)S(1)} %collective-permute-done.5), channel_id=1, source_target_pairs={{0,240},{16,0},{32,16},{48,32},{64,48},{80,64},{96,80},{112,96},{1... | collective-permute-start | bytes 1179656 | tf_op jit(solution)/shard_map/ppermute | solution.py:39
  92.6 12.0 %collective-permute-start.13 = (bf16[3,2,128,256]{3,2,1,0:T(8,128)(2,1)S(1)}, bf16[3,2,128,256]{3,2,1,0:T(8,128)(2,1)S(1)}, u32[]{:S(2)}, u32[]{:S(2)}) collective-permute-start(bf16[3,2,128,256]{3,2,1,0:T(8,128)(2,1)S(1)} %collective-permute-done.12), channel_id=1, source_target_pairs={{0,16},{16,32},{32,48},{48,64},{64,80},{80,96},{96,112},{112,128},... | collective-permute-start | bytes 1179656 | tf_op jit(solution)/shard_map/ppermute | solution.py:38
  99.2 16.3 %collective-permute-start.7 = (bf16[3,2,128,256]{3,2,1,0:T(8,128)(2,1)S(1)}, bf16[3,2,128,256]{3,2,1,0:T(8,128)(2,1)S(1)}, u32[]{:S(2)}, u32[]{:S(2)}) collective-permute-start(bf16[3,2,128,256]{3,2,1,0:T(8,128)(2,1)S(1)} %collective-permute-done.6), channel_id=1, source_target_pairs={{0,240},{16,0},{32,16},{48,32},{64,48},{80,64},{96,80},{112,96},{1... | collective-permute-start | bytes 1179656 | tf_op jit(solution)/shard_map/ppermute | solution.py:39
  104.6 10.8 %collective-permute-start.14 = (bf16[3,2,128,256]{3,2,1,0:T(8,128)(2,1)S(1)}, bf16[3,2,128,256]{3,2,1,0:T(8,128)(2,1)S(1)}, u32[]{:S(2)}, u32[]{:S(2)}) collective-permute-start(bf16[3,2,128,256]{3,2,1,0:T(8,128)(2,1)S(1)} %collective-permute-done.13), channel_id=1, source_target_pairs={{0,16},{16,32},{32,48},{48,64},{64,80},{80,96},{96,112},{112,128},... | collective-permute-start | bytes 1179656 | tf_op jit(solution)/shard_map/ppermute | solution.py:38
  121.0 7.6 %collective-permute-start.15 = (bf16[3,1,128,256]{3,2,1,0:T(8,128)(2,1)S(1)}, bf16[3,1,128,256]{3,2,1,0:T(8,128)(2,1)S(1)}, u32[]{:S(2)}, u32[]{:S(2)}) collective-permute-start(bf16[3,1,128,256]{3,2,1,0:T(8,128)(2,1)S(1)} %slice.151), channel_id=1, source_target_pairs={{0,16},{16,32},{32,48},{48,64},{64,80},{80,96},{96,112},{112,128},... | collective-permute-start | bytes 589832 | tf_op jit(solution)/shard_map/ppermute | solution.py:43
  122.9 7.2 %collective-permute-start.16 = (bf16[3,1,128,256]{3,2,1,0:T(8,128)(2,1)S(1)}, bf16[3,1,128,256]{3,2,1,0:T(8,128)(2,1)S(1)}, u32[]{:S(2)}, u32[]{:S(2)}) collective-permute-start(bf16[3,1,128,256]{3,2,1,0:T(8,128)(2,1)S(1)} %slice.152), channel_id=1, source_target_pairs={{0,240},{16,0},{32,16},{48,32},{64,48},{80,64},{96,80},{112,96},{1... | collective-permute-start | bytes 589832 | tf_op jit(solution)/shard_map/ppermute | solution.py:44
  131.5 8.0 %copy-start.2 = (s32[1,16]{1,0:T(1,128)S(1)}, s32[1,16]{1,0:T(1,128)}, u32[]{:S(2)}) copy-start(s32[1,16]{1,0:T(1,128)} %param.16) | copy-start | bytes 196

commit v7 on v5

--- a/solution.py
+++ b/solution.py
@@ -4,9 +4,10 @@
 import jax.numpy as jnp
 from jax import lax
 from jax.experimental.layout import Layout, with_layout_constraint
-from jax.sharding import PartitionSpec as P
+from jax.sharding import Mesh, PartitionSpec as P
 
 EPSILON = 1e-06
+TP = ("chip", "core")
 
 
 def short_conv(gated_prod, tap_table, segments):
@@ -52,7 +53,7 @@
 def local(activations, norm_gain, proj_weight, short_filter, segment_ids, needle_pos, readout):
     model_width = activations.shape[1]
     local_rows = activations.shape[0]
-    tp_size = lax.axis_size("tp")
+    tp_size = lax.axis_size(TP)
     fsdp_size = lax.axis_size("fsdp")
     z_size = fsdp_size // 2
     channels = proj_weight.shape[2]
@@ -66,7 +67,7 @@
     doubled = jnp.concatenate([grid, grid], axis=2)
     rotated = lax.dynamic_slice_in_dim(doubled, z, z_size, axis=2).reshape(local_rows, model_width)
     spread = jnp.broadcast_to(rotated[None], (tp_size,) + rotated.shape)
-    slab_rows = lax.all_to_all(spread, "tp", 0, 0, tiled=False).reshape(
+    slab_rows = lax.all_to_all(spread, TP, 0, 0, tiled=False).reshape(
         tp_size * local_rows, model_width
     )
     projected = jnp.einsum("sk,ikc->isc", slab_rows, weights, preferred_element_type=jnp.float32)
@@ -75,7 +76,7 @@
     tap_table = jnp.repeat(short_filter, channels // short_filter.shape[0], axis=0)
     filtered = short_conv(gated_prod, tap_table, segment_ids[0])
     mixed_local = (projected[0] * filtered).astype(jnp.bfloat16)
-    device_rank = lax.axis_index("tp")
+    device_rank = lax.axis_index(TP)
     positions = needle_pos[0]
     slab_len = tp_size * local_rows
     picker = (positions[:, None] == jnp.arange(slab_len, dtype=jnp.int32)[None, :]).astype(
@@ -94,7 +95,9 @@
     payload = jnp.concatenate(
         [blocks, jnp.broadcast_to(extra[None], (tp_size, extra_rows, channels))], axis=1
     )
-    gathered = lax.all_to_all(payload, "tp", 0, 0, tiled=False)
+    per_chip = payload.reshape((tp_size // 2, 2) + payload.shape[1:])
+    paired = lax.all_to_all(per_chip, "core", 1, 1, tiled=False)
+    gathered = lax.all_to_all(paired, "chip", 0, 0, tiled=False).reshape(payload.shape)
     own_rows = jnp.transpose(gathered[:, :local_rows], (1, 0, 2)).reshape(
         local_rows, tp_size * channels
     )
@@ -107,14 +110,18 @@
 
 
 def solution(mesh):
+    fsdp_size, tp_size = mesh.devices.shape
+    split_mesh = Mesh(mesh.devices.reshape(fsdp_size, tp_size // 2, 2), ("fsdp",) + TP)
     in_specs = (
-        P(("fsdp", "tp"), None),
+        P(("fsdp",) + TP, None),
         P(),
-        P(None, "fsdp", "tp"),
-        P("tp", None),
+        P(None, "fsdp", TP),
+        P(TP, None),
         P("fsdp", None),
         P("fsdp", None),
         P(),
     )
-    out_specs = (P(("fsdp", "tp"), None), P("fsdp", None))
-    return jax.shard_map(local, mesh=mesh, in_specs=in_specs, out_specs=out_specs, check_vma=False)
+    out_specs = (P(("fsdp",) + TP, None), P("fsdp", None))
+    return jax.shard_map(
+        local, mesh=split_mesh, in_specs=in_specs, out_specs=out_specs, check_vma=False
+    )

time: 163 us -> 165 us (1.012)
  blocking collectives: 20.5 us -> 23.2 us
    all_to_all x1 -> x2, blocking collectives: 20.5 us -> 23.2 us  [the longest x1 14.6 us: local(): lax.all_to_all(paired, 'chip', 0, 0, tiled=False).reshape(payload.shape)]
where the time goes in v7:
time: 165 us; the launch traced here: 164 us
  starting transfers between devices  78.7 us (48%)
  waiting for transfers between devices  31.2 us (19%)
  blocking collectives  23.2 us (14%)
  local copies, waits for them, and re-layouts  16.4 us (10%)
  matrix products  7.34 us (4%)
  other arithmetic  6.5 us (4%)
    ppermute x7, starting transfers between devices, gather_weights(): left = lax.ppermute(left, 'fsdp', z_down)  44.2 us
    ppermute x7, waiting for transfers between devices, gather_weights(): left = lax.ppermute(left, 'fsdp', z_down)  18.8 us
    all_to_all x1, blocking collectives, local(): lax.all_to_all(paired, 'chip', 0, 0, tiled=False).reshape(payload.shape)  14.6 us
    ppermute x7, starting transfers between devices, gather_weights(): right = lax.ppermute(right, 'fsdp', z_up)  13.4 us
    unnamed x22, local copies, waits for them, and re-layouts  11.2 us
    all_to_all x1, starting transfers between devices, local(): lax.all_to_all(spread, TP, 0, 0, tiled=False)  10.6 us
    all_to_all x1, blocking collectives, local(): paired = lax.all_to_all(per_chip, 'core', 1, 1, tiled=False)  8.6 us
    ppermute x7, waiting for transfers between devices, gather_weights(): right = lax.ppermute(right, 'fsdp', z_up)  7.39 us
  transfers between devices with their start and end apart: 18, of which 9 were waited for; matrix products, arithmetic and copies ran while one was open for 12% of the time, Pallas kernels for 0%

profile of v7, /device:TPU:1, one launch (start us, length us, event | category | flops | bytes accessed | tf_op | source)
XLA Modules:
  0.0 164.5 jit_solution(1809296523692466932)
XLA Ops:
  0.6 3.9 %collective-permute-start = (bf16[3,128,256]{2,1,0:T(8,128)(2,1)}, bf16[3,128,256]{2,1,0:T(8,128)(2,1)S(1)}, u32[]{:S(2)}, u32[]{:S(2)}) collective-permute-start(bf16[3,128,256]{2,1,0:T(8,128)(2,1)} %param.13), channel_id=1, source_target_pairs={{0,256},{16,272},{32,288},{48,304},{64,320},{80,336},{96,352},{112... | collective-permute-start | bytes 589832 | tf_op jit(solution)/shard_map/ppermute | solution.py:30
  4.6 3.2 %collective-permute-done = bf16[3,128,256]{2,1,0:T(8,128)(2,1)S(1)} collective-permute-done((bf16[3,128,256]{2,1,0:T(8,128)(2,1)}, bf16[3,128,256]{2,1,0:T(8,128)(2,1)S(1)}, u32[]{:S(2)}, u32[]{:S(2)}) %collective-permute-start) | collective-permute-done | bytes 196640 | tf_op jit(solution)/shard_map/ppermute | solution.py:30
  8.8 12.6 %collective-permute-start.1 = (bf16[3,2,128,256]{3,2,1,0:T(8,128)(2,1)S(1)}, bf16[3,2,128,256]{3,2,1,0:T(8,128)(2,1)S(1)}, u32[]{:S(2)}, u32[]{:S(2)}) collective-permute-start(bf16[3,2,128,256]{3,2,1,0:T(8,128)(2,1)S(1)} %pad_maximum_fusion), channel_id=1, source_target_pairs={{0,240},{16,0},{32,16},{48,32},{64,48},{80,64},{96,80},{112,96},{1... | collective-permute-start | bytes 1179656 | tf_op jit(solution)/shard_map/ppermute | solution.py:40
  21.5 1.9 %collective-permute-start.8 = (bf16[3,2,128,256]{3,2,1,0:T(8,128)(2,1)S(1)}, bf16[3,2,128,256]{3,2,1,0:T(8,128)(2,1)S(1)}, u32[]{:S(2)}, u32[]{:S(2)}) collective-permute-start(bf16[3,2,128,256]{3,2,1,0:T(8,128)(2,1)S(1)} %pad_maximum_fusion), channel_id=1, source_target_pairs={{0,16},{16,32},{32,48},{48,64},{64,80},{80,96},{96,112},{112,128},... | collective-permute-start | bytes 1179656 | tf_op jit(solution)/shard_map/ppermute | solution.py:39
  23.4 4.9 %collective-permute-done.1 = bf16[3,2,128,256]{3,2,1,0:T(8,128)(2,1)S(1)} collective-permute-done((bf16[3,2,128,256]{3,2,1,0:T(8,128)(2,1)S(1)}, bf16[3,2,128,256]{3,2,1,0:T(8,128)(2,1)S(1)}, u32[]{:S(2)}, u32[]{:S(2)}) %collective-permute-start.1) | collective-permute-done | bytes 393248 | tf_op jit(solution)/shard_map/ppermute | solution.py:40
  28.3 5.3 %collective-permute-start.2 = (bf16[3,2,128,256]{3,2,1,0:T(8,128)(2,1)S(1)}, bf16[3,2,128,256]{3,2,1,0:T(8,128)(2,1)S(1)}, u32[]{:S(2)}, u32[]{:S(2)}) collective-permute-start(bf16[3,2,128,256]{3,2,1,0:T(8,128)(2,1)S(1)} %collective-permute-done.1), channel_id=1, source_target_pairs={{0,240},{16,0},{32,16},{48,32},{64,48},{80,64},{96,80},{112,96},{1... | collective-permute-start | bytes 1179656 | tf_op jit(solution)/shard_map/ppermute | solution.py:40
  36.7 2.9 %collective-permute-done.2 = bf16[3,2,128,256]{3,2,1,0:T(8,128)(2,1)S(1)} collective-permute-done((bf16[3,2,128,256]{3,2,1,0:T(8,128)(2,1)S(1)}, bf16[3,2,128,256]{3,2,1,0:T(8,128)(2,1)S(1)}, u32[]{:S(2)}, u32[]{:S(2)}) %collective-permute-start.2) | collective-permute-done | bytes 393248 | tf_op jit(solution)/shard_map/ppermute | solution.py:40
  39.5 5.3 %collective-permute-start.3 = (bf16[3,2,128,256]{3,2,1,0:T(8,128)(2,1)S(1)}, bf16[3,2,128,256]{3,2,1,0:T(8,128)(2,1)S(1)}, u32[]{:S(2)}, u32[]{:S(2)}) collective-permute-start(bf16[3,2,128,256]{3,2,1,0:T(8,128)(2,1)S(1)} %collective-permute-done.2), channel_id=1, source_target_pairs={{0,240},{16,0},{32,16},{48,32},{64,48},{80,64},{96,80},{112,96},{1... | collective-permute-start | bytes 1179656 | tf_op jit(solution)/shard_map/ppermute | solution.py:40
  48.3 2.6 %broadcast_in_dim.9 = bf16[16,32,4096]{2,1,0:T(8,128)(2,1)} broadcast(bf16[32,4096]{1,0:T(8,128)(2,1)S(1)} %bitcast.118), dimensions={1,2} | broadcast | bytes 4456448 | tf_op jit(solution)/shard_map/broadcast_in_dim | solution.py:69
  50.9 10.6 %all-to-all-start = ((bf16[16,32,4096]{2,1,0:T(8,128)(2,1)}), bf16[16,32,4096]{2,1,0:T(8,128)(2,1)}, u32[]{:S(2)}, u32[]{:S(2)}) async-start(bf16[16,32,4096]{2,1,0:T(8,128)(2,1)} %broadcast_in_dim.9), calls=%async_computation | async-start | bytes 8388608 | tf_op jit(solution)/shard_map/all_to_all | solution.py:70
  61.5 4.9 %collective-permute-start.4 = (bf16[3,2,128,256]{3,2,1,0:T(8,128)(2,1)S(1)}, bf16[3,2,128,256]{3,2,1,0:T(8,128)(2,1)}, u32[]{:S(2)}, u32[]{:S(2)}) collective-permute-start(bf16[3,2,128,256]{3,2,1,0:T(8,128)(2,1)S(1)} %collective-permute-done.3), channel_id=1, source_target_pairs={{0,240},{16,0},{32,16},{48,32},{64,48},{80,64},{96,80},{112,96},{1... | collective-permute-start | bytes 1179656 | tf_op jit(solution)/shard_map/ppermute | solution.py:40
  66.4 1.9 %collective-permute-start.11 = (bf16[3,2,128,256]{3,2,1,0:T(8,128)(2,1)S(1)}, bf16[3,2,128,256]{3,2,1,0:T(8,128)(2,1)S(1)}, u32[]{:S(2)}, u32[]{:S(2)}) collective-permute-start(bf16[3,2,128,256]{3,2,1,0:T(8,128)(2,1)S(1)} %collective-permute-done.10), channel_id=1, source_target_pairs={{0,16},{16,32},{32,48},{48,64},{64,80},{80,96},{96,112},{112,128},... | collective-permute-start | bytes 1179656 | tf_op jit(solution)/shard_map/ppermute | solution.py:39
  70.1 4.6 %collective-permute-done.4 = bf16[3,2,128,256]{3,2,1,0:T(8,128)(2,1)} collective-permute-done((bf16[3,2,128,256]{3,2,1,0:T(8,128)(2,1)S(1)}, bf16[3,2,128,256]{3,2,1,0:T(8,128)(2,1)}, u32[]{:S(2)}, u32[]{:S(2)}) %collective-permute-start.4) | collective-permute-done | bytes 393248 | tf_op jit(solution)/shard_map/ppermute | solution.py:40
  74.7 5.4 %collective-permute-start.5 = (bf16[3,2,128,256]{3,2,1,0:T(8,128)(2,1)}, bf16[3,2,128,256]{3,2,1,0:T(8,128)(2,1)S(1)}, u32[]{:S(2)}, u32[]{:S(2)}) collective-permute-start(bf16[3,2,128,256]{3,2,1,0:T(8,128)(2,1)} %collective-permute-done.4), channel_id=1, source_target_pairs={{0,240},{16,0},{32,16},{48,32},{64,48},{80,64},{96,80},{112,96},{1... | collective-permute-start | bytes 1179656 | tf_op jit(solution)/shard_map/ppermute | solution.py:40
  83.6 4.3 %collective-permute-done.5 = bf16[3,2,128,256]{3,2,1,0:T(8,128)(2,1)S(1)} collective-permute-done((bf16[3,2,128,256]{3,2,1,0:T(8,128)(2,1)}, bf16[3,2,128,256]{3,2,1,0:T(8,128)(2,1)S(1)}, u32[]{:S(2)}, u32[]{:S(2)}) %collective-permute-start.5) | collective-permute-done | bytes 393248 | tf_op jit(solution)/shard_map/ppermute | solution.py:40
  87.9 5.3 %collective-permute-start.6 = (bf16[3,2,128,256]{3,2,1,0:T(8,128)(2,1)S(1)}, bf16[3,2,128,256]{3,2,1,0:T(8,128)(2,1)S(1)}, u32[]{:S(2)}, u32[]{:S(2)}) collective-permute-start(bf16[3,2,128,256]{3,2,1,0:T(8,128)(2,1)S(1)} %collective-permute-done.5), channel_id=1, source_target_pairs={{0,240},{16,0},{32,16},{48,32},{64,48},{80,64},{96,80},{112,96},{1... | collective-permute-start | bytes 1179656 | tf_op jit(solution)/shard_map/ppermute | solution.py:40
  93.2 1.9 %collective-permute-start.13 = (bf16[3,2,128,256]{3,2,1,0:T(8,128)(2,1)S(1)}, bf16[3,2,128,256]{3,2,1,0:T(8,128)(2,1)S(1)}, u32[]{:S(2)}, u32[]{:S(2)}) collective-permute-start(bf16[3,2,128,256]{3,2,1,0:T(8,128)(2,1)S(1)} %collective-permute-done.12), channel_id=1, source_target_pairs={{0,16},{16,32},{32,48},{48,64},{64,80},{80,96},{96,112},{112,128},... | collective-permute-start | bytes 1179656 | tf_op jit(solution)/shard_map/ppermute | solution.py:39
  97.7 2.2 %collective-permute-done.6 = bf16[3,2,128,256]{3,2,1,0:T(8,128)(2,1)S(1)} collective-permute-done((bf16[3,2,128,256]{3,2,1,0:T(8,128)(2,1)S(1)}, bf16[3,2,128,256]{3,2,1,0:T(8,128)(2,1)S(1)}, u32[]{:S(2)}, u32[]{:S(2)}) %collective-permute-start.6) | collective-permute-done | bytes 393248 | tf_op jit(solution)/shard_map/ppermute | solution.py:40
  99.8 5.4 %collective-permute-start.7 = (bf16[3,2,128,256]{3,2,1,0:T(8,128)(2,1)S(1)}, bf16[3,2,128,256]{3,2,1,0:T(8,128)(2,1)S(1)}, u32[]{:S(2)}, u32[]{:S(2)}) collective-permute-start(bf16[3,2,128,256]{3,2,1,0:T(8,128)(2,1)S(1)} %collective-permute-done.6), channel_id=1, source_target_pairs={{0,240},{16,0},{32,16},{48,32},{64,48},{80,64},{96,80},{112,96},{1... | collective-permute-start | bytes 1179656 | tf_op jit(solution)/shard_map/ppermute | solution.py:40
  108.7 7.4 %collective-permute-done.14 = bf16[3,2,128,256]{3,2,1,0:T(8,128)(2,1)S(1)} collective-permute-done((bf16[3,2,128,256]{3,2,1,0:T(8,128)(2,1)S(1)}, bf16[3,2,128,256]{3,2,1,0:T(8,128)(2,1)S(1)}, u32[]{:S(2)}, u32[]{:S(2)}) %collective-permute-start.14) | collective-permute-done | bytes 393248 | tf_op jit(solution)/shard_map/ppermute | solution.py:39
  118.1 4.6 %collective-permute-start.16 = (bf16[3,1,128,256]{3,2,1,0:T(8,128)(2,1)S(1)}, bf16[3,1,128,256]{3,2,1,0:T(8,128)(2,1)S(1)}, u32[]{:S(2)}, u32[]{:S(2)}) collective-permute-start(bf16[3,1,128,256]{3,2,1,0:T(8,128)(2,1)S(1)} %slice.144), channel_id=1, source_target_pairs={{0,240},{16,0},{32,16},{48,32},{64,48},{80,64},{96,80},{112,96},{1... | collective-permute-start | bytes 589832 | tf_op jit(solution)/shard_map/ppermute | solution.py:44
  131.4 7.0 %convolution_bitcast_fusion = f32[3,512,256]{2,1,0:T(8,128)S(1)} fusion(bf16[512,4096,1]{1,0,2:T(8,128)(2,1)} %bitcast.36, bf16[3,4096,256]{2,1,0:T(8,128)(2,1)} %bitcast.34), kind=kOutput, calls=%fused_computation | convolution fusion | flops 3221225472 | bytes 12058624 | tf_op jit(solution)/shard_map/sk,ikc->isc/dot_general | solution.py:73
  139.9 8.6 %all_to_all.15 = bf16[8,2,48,256]{3,2,0,1:T(8,128)(2,1)S(1)} all-to-all(bf16[8,2,48,256]{3,2,0,1:T(8,128)(2,1)S(1)} %pad_maximum_fusion.1), channel_id=1, replica_groups=mesh['fsdp'=32,'chip'=8,'core'=2] {'core'}, dimensions={1} | all-to-all | bytes 786432 | tf_op jit(solution)/shard_map/all_to_all | solution.py:99
  148.6 14.6 %all_to_all.16 = bf16[8,2,48,256]{3,2,1,0:T(8,128)(2,1)S(1)} all-to-all(bf16[8,2,48,256]{3,2,1,0:T(8,128)(2,1)S(1)} %copy.96), channel_id=1, replica_groups=mesh['fsdp'=32,'chip'=8,'core'=2] {'chip'}, dimensions={0} | all-to-all | bytes 786432 | tf_op jit(solution)/shard_map/all_to_all | solution.py:100
  (66 shorter events, 32.1 us)
Async XLA Ops:
  0.6 7.2 %collective-permute-start = (bf16[3,128,256]{2,1,0:T(8,128)(2,1)}, bf16[3,128,256]{2,1,0:T(8,128)(2,1)S(1)}, u32[]{:S(2)}, u32[]{:S(2)}) collective-permute-start(bf16[3,128,256]{2,1,0:T(8,128)(2,1)} %param.13), channel_id=1, source_target_pairs={{0,256},{16,272},{32,288},{48,304},{64,320},{80,336},{96,352},{112... | collective-permute-start | bytes 589832 | tf_op jit(solution)/shard_map/ppermute | solution.py:30
  8.8 19.5 %collective-permute-start.1 = (bf16[3,2,128,256]{3,2,1,0:T(8,128)(2,1)S(1)}, bf16[3,2,128,256]{3,2,1,0:T(8,128)(2,1)S(1)}, u32[]{:S(2)}, u32[]{:S(2)}) collective-permute-start(bf16[3,2,128,256]{3,2,1,0:T(8,128)(2,1)S(1)} %pad_maximum_fusion), channel_id=1, source_target_pairs={{0,240},{16,0},{32,16},{48,32},{64,48},{80,64},{96,80},{112,96},{1... | collective-permute-start | bytes 1179656 | tf_op jit(solution)/shard_map/ppermute | solution.py:40
  21.5 12.2 %collective-permute-start.8 = (bf16[3,2,128,256]{3,2,1,0:T(8,128)(2,1)S(1)}, bf16[3,2,128,256]{3,2,1,0:T(8,128)(2,1)S(1)}, u32[]{:S(2)}, u32[]{:S(2)}) collective-permute-start(bf16[3,2,128,256]{3,2,1,0:T(8,128)(2,1)S(1)} %pad_maximum_fusion), channel_id=1, source_target_pairs={{0,16},{16,32},{32,48},{48,64},{64,80},{80,96},{96,112},{112,128},... | collective-permute-start | bytes 1179656 | tf_op jit(solution)/shard_map/ppermute | solution.py:39
  28.3 11.2 %collective-permute-start.2 = (bf16[3,2,128,256]{3,2,1,0:T(8,128)(2,1)S(1)}, bf16[3,2,128,256]{3,2,1,0:T(8,128)(2,1)S(1)}, u32[]{:S(2)}, u32[]{:S(2)}) collective-permute-start(bf16[3,2,128,256]{3,2,1,0:T(8,128)(2,1)S(1)} %collective-permute-done.1), channel_id=1, source_target_pairs={{0,240},{16,0},{32,16},{48,32},{64,48},{80,64},{96,80},{112,96},{1... | collective-permute-start | bytes 1179656 | tf_op jit(solution)/shard_map/ppermute | solution.py:40
  33.6 11.2 %collective-permute-start.9 = (bf16[3,2,128,256]{3,2,1,0:T(8,128)(2,1)S(1)}, bf16[3,2,128,256]{3,2,1,0:T(8,128)(2,1)S(1)}, u32[]{:S(2)}, u32[]{:S(2)}) collective-permute-start(bf16[3,2,128,256]{3,2,1,0:T(8,128)(2,1)S(1)} %collective-permute-done.8), channel_id=1, source_target_pairs={{0,16},{16,32},{32,48},{48,64},{64,80},{80,96},{96,112},{112,128},... | collective-permute-start | bytes 1179656 | tf_op jit(solution)/shard_map/ppermute | solution.py:39
  39.5 22.0 %collective-permute-start.3 = (bf16[3,2,128,256]{3,2,1,0:T(8,128)(2,1)S(1)}, bf16[3,2,128,256]{3,2,1,0:T(8,128)(2,1)S(1)}, u32[]{:S(2)}, u32[]{:S(2)}) collective-permute-start(bf16[3,2,128,256]{3,2,1,0:T(8,128)(2,1)S(1)} %collective-permute-done.2), channel_id=1, source_target_pairs={{0,240},{16,0},{32,16},{48,32},{64,48},{80,64},{96,80},{112,96},{1... | collective-permute-start | bytes 1179656 | tf_op jit(solution)/shard_map/ppermute | solution.py:40
  44.9 21.5 %collective-permute-start.10 = (bf16[3,2,128,256]{3,2,1,0:T(8,128)(2,1)S(1)}, bf16[3,2,128,256]{3,2,1,0:T(8,128)(2,1)S(1)}, u32[]{:S(2)}, u32[]{:S(2)}) collective-permute-start(bf16[3,2,128,256]{3,2,1,0:T(8,128)(2,1)S(1)} %collective-permute-done.9), channel_id=1, source_target_pairs={{0,16},{16,32},{32,48},{48,64},{64,80},{80,96},{96,112},{112,128},... | collective-permute-start | bytes 1179656 | tf_op jit(solution)/shard_map/ppermute | solution.py:39
  48.3 20.0 %copy-start.1 = (s32[1,512]{1,0:T(1,128)S(1)}, s32[1,512]{1,0:T(1,128)}, u32[]{:S(2)}) copy-start(s32[1,512]{1,0:T(1,128)} %param.15) | copy-start | bytes 6148
  48.3 20.1 %copy-start = (f32[16,7]{0,1:T(8,128)S(1)}, f32[16,7]{0,1:T(8,128)}, u32[]{:S(2)}) copy-start(f32[16,7]{0,1:T(8,128)} %param.14) | copy-start | bytes 1348
  50.9 80.5 %all-to-all-start = ((bf16[16,32,4096]{2,1,0:T(8,128)(2,1)}), bf16[16,32,4096]{2,1,0:T(8,128)(2,1)}, u32[]{:S(2)}, u32[]{:S(2)}) async-start(bf16[16,32,4096]{2,1,0:T(8,128)(2,1)} %broadcast_in_dim.9), calls=%async_computation | async-start | bytes 8388608 | tf_op jit(solution)/shard_map/all_to_all | solution.py:70
  61.5 13.2 %collective-permute-start.4 = (bf16[3,2,128,256]{3,2,1,0:T(8,128)(2,1)S(1)}, bf16[3,2,128,256]{3,2,1,0:T(8,128)(2,1)}, u32[]{:S(2)}, u32[]{:S(2)}) collective-permute-start(bf16[3,2,128,256]{3,2,1,0:T(8,128)(2,1)S(1)} %collective-permute-done.3), channel_id=1, source_target_pairs={{0,240},{16,0},{32,16},{48,32},{64,48},{80,64},{96,80},{112,96},{1... | collective-permute-start | bytes 1179656 | tf_op jit(solution)/shard_map/ppermute | solution.py:40
  66.4 13.8 %collective-permute-start.11 = (bf16[3,2,128,256]{3,2,1,0:T(8,128)(2,1)S(1)}, bf16[3,2,128,256]{3,2,1,0:T(8,128)(2,1)S(1)}, u32[]{:S(2)}, u32[]{:S(2)}) collective-permute-start(bf16[3,2,128,256]{3,2,1,0:T(8,128)(2,1)S(1)} %collective-permute-done.10), channel_id=1, source_target_pairs={{0,16},{16,32},{32,48},{48,64},{64,80},{80,96},{96,112},{112,128},... | collective-permute-start | bytes 1179656 | tf_op jit(solution)/shard_map/ppermute | solution.py:39
  74.7 13.2 %collective-permute-start.5 = (bf16[3,2,128,256]{3,2,1,0:T(8,128)(2,1)}, bf16[3,2,128,256]{3,2,1,0:T(8,128)(2,1)S(1)}, u32[]{:S(2)}, u32[]{:S(2)}) collective-permute-start(bf16[3,2,128,256]{3,2,1,0:T(8,128)(2,1)} %collective-permute-done.4), channel_id=1, source_target_pairs={{0,240},{16,0},{32,16},{48,32},{64,48},{80,64},{96,80},{112,96},{1... | collective-permute-start | bytes 1179656 | tf_op jit(solution)/shard_map/ppermute | solution.py:40
  80.2 13.1 %collective-permute-start.12 = (bf16[3,2,128,256]{3,2,1,0:T(8,128)(2,1)S(1)}, bf16[3,2,128,256]{3,2,1,0:T(8,128)(2,1)S(1)}, u32[]{:S(2)}, u32[]{:S(2)}) collective-permute-start(bf16[3,2,128,256]{3,2,1,0:T(8,128)(2,1)S(1)} %collective-permute-done.11), channel_id=1, source_target_pairs={{0,16},{16,32},{32,48},{48,64},{64,80},{80,96},{96,112},{112,128},... | collective-permute-start | bytes 1179656 | tf_op jit(solution)/shard_map/ppermute | solution.py:39
  87.9 11.9 %collective-permute-start.6 = (bf16[3,2,128,256]{3,2,1,0:T(8,128)(2,1)S(1)}, bf16[3,2,128,256]{3,2,1,0:T(8,128)(2,1)S(1)}, u32[]{:S(2)}, u32[]{:S(2)}) collective-permute-start(bf16[3,2,128,256]{3,2,1,0:T(8,128)(2,1)S(1)} %collective-permute-done.5), channel_id=1, source_target_pairs={{0,240},{16,0},{32,16},{48,32},{64,48},{80,64},{96,80},{112,96},{1... | collective-permute-start | bytes 1179656 | tf_op jit(solution)/shard_map/ppermute | solution.py:40
  93.2 12.0 %collective-permute-start.13 = (bf16[3,2,128,256]{3,2,1,0:T(8,128)(2,1)S(1)}, bf16[3,2,128,256]{3,2,1,0:T(8,128)(2,1)S(1)}, u32[]{:S(2)}, u32[]{:S(2)}) collective-permute-start(bf16[3,2,128,256]{3,2,1,0:T(8,128)(2,1)S(1)} %collective-permute-done.12), channel_id=1, source_target_pairs={{0,16},{16,32},{32,48},{48,64},{64,80},{80,96},{96,112},{112,128},... | collective-permute-start | bytes 1179656 | tf_op jit(solution)/shard_map/ppermute | solution.py:39
  99.8 18.2 %collective-permute-start.7 = (bf16[3,2,128,256]{3,2,1,0:T(8,128)(2,1)S(1)}, bf16[3,2,128,256]{3,2,1,0:T(8,128)(2,1)S(1)}, u32[]{:S(2)}, u32[]{:S(2)}) collective-permute-start(bf16[3,2,128,256]{3,2,1,0:T(8,128)(2,1)S(1)} %collective-permute-done.6), channel_id=1, source_target_pairs={{0,240},{16,0},{32,16},{48,32},{64,48},{80,64},{96,80},{112,96},{1... | collective-permute-start | bytes 1179656 | tf_op jit(solution)/shard_map/ppermute | solution.py:40
  105.3 10.8 %collective-permute-start.14 = (bf16[3,2,128,256]{3,2,1,0:T(8,128)(2,1)S(1)}, bf16[3,2,128,256]{3,2,1,0:T(8,128)(2,1)S(1)}, u32[]{:S(2)}, u32[]{:S(2)}) collective-permute-start(bf16[3,2,128,256]{3,2,1,0:T(8,128)(2,1)S(1)} %collective-permute-done.13), channel_id=1, source_target_pairs={{0,16},{16,32},{32,48},{48,64},{64,80},{80,96},{96,112},{112,128},... | collective-permute-start | bytes 1179656 | tf_op jit(solution)/shard_map/ppermute | solution.py:39
  116.1 7.6 %collective-permute-start.15 = (bf16[3,1,128,256]{3,2,1,0:T(8,128)(2,1)S(1)}, bf16[3,1,128,256]{3,2,1,0:T(8,128)(2,1)S(1)}, u32[]{:S(2)}, u32[]{:S(2)}) collective-permute-start(bf16[3,1,128,256]{3,2,1,0:T(8,128)(2,1)S(1)} %slice.143), channel_id=1, source_target_pairs={{0,16},{16,32},{32,48},{48,64},{64,80},{80,96},{96,112},{112,128},... | collective-permute-start | bytes 589832 | tf_op jit(solution)/shard_map/ppermute | solution.py:43
  118.1 7.2 %collective-permute-start.16 = (bf16[3,1,128,256]{3,2,1,0:T(8,128)(2,1)S(1)}, bf16[3,1,128,256]{3,2,1,0:T(8,128)(2,1)S(1)}, u32[]{:S(2)}, u32[]{:S(2)}) collective-permute-start(bf16[3,1,128,256]{3,2,1,0:T(8,128)(2,1)S(1)} %slice.144), channel_id=1, source_target_pairs={{0,240},{16,0},{32,16},{48,32},{64,48},{80,64},{96,80},{112,96},{1... | collective-permute-start | bytes 589832 | tf_op jit(solution)/shard_map/ppermute | solution.py:44
  131.4 8.0 %copy-start.2 = (s32[1,16]{1,0:T(1,128)S(1)}, s32[1,16]{1,0:T(1,128)}, u32[]{:S(2)}) copy-start(s32[1,16]{1,0:T(1,128)} %param.16) | copy-start | bytes 196

commit v8 on v5

--- a/solution.py
+++ b/solution.py
@@ -30,23 +30,34 @@
     first = jnp.where(x_lo == 0, proj_weight, other)
     second = jnp.where(x_lo == 0, other, proj_weight)
     pair = jnp.stack([first, second], axis=1)
-    ahead = [pair]
-    behind = []
+    lead, halves, block, width = pair.shape
+    buffer = with_layout_constraint(
+        jnp.zeros((lead, halves, z_size, block, width), pair.dtype), Layout((0, 1, 2, 3, 4))
+    )
+
+    def place(into, arrived):
+        for at, piece in arrived:
+            into = lax.dynamic_update_slice(into, piece[:, :, None], (0, 0, at, 0, 0))
+        return into
+
+    arrivals = [[(0, pair)]]
     right = pair
     left = pair
-    for _ in range(1, z_size // 2):
+    for step in range(1, z_size // 2):
+        if step >= 2:
+            buffer = place(buffer, arrivals[step - 2])
+            right, left, buffer = lax.optimization_barrier((right, left, buffer))
         right = lax.ppermute(right, "fsdp", z_up)
         left = lax.ppermute(left, "fsdp", z_down)
-        behind.append(right)
-        ahead.append(left)
-    last_a = lax.ppermute(right[:, :1], "fsdp", z_up)
-    last_b = lax.ppermute(left[:, 1:], "fsdp", z_down)
-    ahead.append(jnp.concatenate([last_a, last_b], axis=1))
-    pieces = ahead + behind[::-1]
-    stacked = with_layout_constraint(jnp.stack(pieces, axis=2), Layout((0, 1, 2, 3, 4)))
-    return stacked.reshape(
-        proj_weight.shape[0], fsdp_size * proj_weight.shape[1], proj_weight.shape[2]
-    )
+        arrivals.append([(step, left), (z_size - step, right)])
+    buffer = place(buffer, arrivals[-2])
+    sent_a, sent_b, buffer = lax.optimization_barrier((right[:, :1], left[:, 1:], buffer))
+    last_a = lax.ppermute(sent_a, "fsdp", z_up)
+    last_b = lax.ppermute(sent_b, "fsdp", z_down)
+    last = jnp.concatenate([last_a, last_b], axis=1)
+    buffer = place(buffer, arrivals[-1] + [(z_size // 2, last)])
+    buffer = with_layout_constraint(buffer, Layout((0, 1, 2, 3, 4)))
+    return buffer.reshape(lead, fsdp_size * block, width)
 
 
 def local(activations, norm_gain, proj_weight, short_filter, segment_ids, needle_pos, readout):

time: 163 us -> 167 us (1.025)
  blocking collectives: 20.5 us -> 25.9 us
  starting transfers between devices: 78.7 us -> 74.2 us
  waiting for transfers between devices: 31.2 us -> 33.8 us
  local copies, waits for them, and re-layouts: 16.4 us -> 18.9 us
  other arithmetic: 6.5 us -> 4.83 us
    ppermute x7, waiting for transfers between devices: 7.39 us -> 25.4 us  [gather_weights(): right = lax.ppermute(right, 'fsdp', z_up)]
    dynamic_update_slice x0 -> x15, local copies, waits for them, and re-layouts: none -> 14.2 us  [place(): into = lax.dynamic_update_slice(into, piece[:, :, None], (0, 0, at, 0, 0))]
    ppermute x7, waiting for transfers between devices: 18.8 us -> 7.39 us  [gather_weights(): left = lax.ppermute(left, 'fsdp', z_down)]
    unnamed x22 -> x11, local copies, waits for them, and re-layouts: 11.2 us -> 0.19 us
    all_to_all x1, blocking collectives: 20.5 us -> 25.9 us  [local(): gathered = lax.all_to_all(payload, 'tp', 0, 0, tiled=False)]
    ppermute x7, starting transfers between devices: 44.2 us -> 40.6 us  [gather_weights(): left = lax.ppermute(left, 'fsdp', z_down)]
    ppermute x1, waiting for transfers between devices: 3.24 us -> 0.01 us  [gather_weights(): other = lax.ppermute(proj_weight, 'fsdp', x_swap)]
  transfers between devices with their start and end apart: 18 -> 18, of which waited for: 9 -> 15; matrix products, arithmetic and copies ran while one was open for 12% -> 13% of each run, Pallas kernels for 0% -> 0%
where the time goes in v8:
time: 167 us; the launch traced here: 166 us
  starting transfers between devices  74.2 us (44%)
  waiting for transfers between devices  33.8 us (20%)
  blocking collectives  25.9 us (16%)
  local copies, waits for them, and re-layouts  18.9 us (11%)
  matrix products  7.34 us (4%)
  other arithmetic  4.83 us (3%)
    ppermute x7, starting transfers between devices, gather_weights(): left = lax.ppermute(left, 'fsdp', z_down)  40.6 us
    all_to_all x1, blocking collectives, local(): gathered = lax.all_to_all(payload, 'tp', 0, 0, tiled=False)  25.9 us
    ppermute x7, waiting for transfers between devices, gather_weights(): right = lax.ppermute(right, 'fsdp', z_up)  25.4 us
    dynamic_update_slice x15, local copies, waits for them, and re-layouts, place(): into = lax.dynamic_update_slice(into, piece[:, :, None], (0, 0, at, 0, 0))  14.2 us
    ppermute x7, starting transfers between devices, gather_weights(): right = lax.ppermute(right, 'fsdp', z_up)  13.5 us
    all_to_all x1, starting transfers between devices, local(): lax.all_to_all(spread, 'tp', 0, 0, tiled=False)  9.26 us
    ppermute x7, waiting for transfers between devices, gather_weights(): left = lax.ppermute(left, 'fsdp', z_down)  7.39 us
    dot_general x1, matrix products, local(): jnp.einsum('sk,ikc->isc', slab_rows, weights, preferred_element_type=jnp....  7.04 us
  transfers between devices with their start and end apart: 18, of which 15 were waited for; matrix products, arithmetic and copies ran while one was open for 13% of the time, Pallas kernels for 0%

profile of v8, /device:TPU:1, one launch (start us, length us, event | category | flops | bytes accessed | tf_op | source)
XLA Modules:
  0.0 165.9 jit_solution(17632707607183157068)
XLA Ops:
  0.6 4.0 %collective-permute-start = (bf16[3,128,256]{2,1,0:T(8,128)(2,1)}, bf16[3,128,256]{2,1,0:T(8,128)(2,1)S(1)}, u32[]{:S(2)}, u32[]{:S(2)}) collective-permute-start(bf16[3,128,256]{2,1,0:T(8,128)(2,1)} %param.13), channel_id=1, source_target_pairs={{0,256},{16,272},{32,288},{48,304},{64,320},{80,336},{96,352},{112... | collective-permute-start | bytes 589832 | tf_op jit(solution)/shard_map/ppermute | solution.py:29
  7.2 2.6 %broadcast_in_dim.98 = bf16[16,32,4096]{2,1,0:T(8,128)(2,1)} broadcast(bf16[32,4096]{1,0:T(8,128)(2,1)S(1)} %bitcast.115), dimensions={1,2} | broadcast | bytes 4456448 | tf_op jit(solution)/shard_map/broadcast_in_dim | solution.py:79
  9.8 9.3 %all-to-all-start = ((bf16[16,32,4096]{2,1,0:T(8,128)(2,1)}), bf16[16,32,4096]{2,1,0:T(8,128)(2,1)}, u32[]{:S(2)}, u32[]{:S(2)}) async-start(bf16[16,32,4096]{2,1,0:T(8,128)(2,1)} %broadcast_in_dim.98), calls=%async_computation | async-start | bytes 8388608 | tf_op jit(solution)/shard_map/all_to_all | solution.py:80
  20.1 2.0 %collective-permute-start.1 = (bf16[3,2,128,256]{3,2,1,0:T(8,128)(2,1)S(1)}, bf16[3,2,128,256]{3,2,1,0:T(8,128)(2,1)S(1)}, u32[]{:S(2)}, u32[]{:S(2)}) collective-permute-start(bf16[3,2,128,256]{3,2,1,0:T(8,128)(2,1)S(1)} %get-tuple-element.69), channel_id=1, source_target_pairs={{0,16},{16,32},{32,48},{48,64},{64,80},{80,96},{96,112},{112,128},... | collective-permute-start | bytes 1179656 | tf_op jit(solution)/shard_map/ppermute | solution.py:50
  22.2 9.5 %collective-permute-start.2 = (bf16[3,2,128,256]{3,2,1,0:T(8,128)(2,1)S(1)}, bf16[3,2,128,256]{3,2,1,0:T(8,128)(2,1)S(1)}, u32[]{:S(2)}, u32[]{:S(2)}) collective-permute-start(bf16[3,2,128,256]{3,2,1,0:T(8,128)(2,1)S(1)} %get-tuple-element.69), channel_id=1, source_target_pairs={{0,240},{16,0},{32,16},{48,32},{64,48},{80,64},{96,80},{112,96},{1... | collective-permute-start | bytes 1179656 | tf_op jit(solution)/shard_map/ppermute | solution.py:51
  31.8 3.4 %pad.68 = bf16[3,2,16,128,256]{4,3,2,1,0:T(8,128)(2,1)} pad(bf16[3,2,1,128,256]{4,3,2,1,0:T(8,128)(2,1)S(1)} %get-tuple-element.68, bf16[]{:T(256)} %constant.118.clone.1), padding=0_0x0_0x0_15x0_0x0_0 | pad | bytes 6684674 | tf_op jit(solution)/shard_map/dynamic_update_slice | solution.py:40
  35.2 4.0 %collective-permute-done.1 = bf16[3,2,128,256]{3,2,1,0:T(8,128)(2,1)S(1)} collective-permute-done((bf16[3,2,128,256]{3,2,1,0:T(8,128)(2,1)S(1)}, bf16[3,2,128,256]{3,2,1,0:T(8,128)(2,1)S(1)}, u32[]{:S(2)}, u32[]{:S(2)}) %collective-permute-start.1) | collective-permute-done | bytes 393248 | tf_op jit(solution)/shard_map/ppermute | solution.py:50
  40.0 1.9 %collective-permute-start.3 = (bf16[3,2,128,256]{3,2,1,0:T(8,128)(2,1)S(1)}, bf16[3,2,128,256]{3,2,1,0:T(8,128)(2,1)S(1)}, u32[]{:S(2)}, u32[]{:S(2)}) collective-permute-start(bf16[3,2,128,256]{3,2,1,0:T(8,128)(2,1)S(1)} %collective-permute-done.1), channel_id=1, source_target_pairs={{0,16},{16,32},{32,48},{48,64},{64,80},{80,96},{96,112},{112,128},... | collective-permute-start | bytes 1179656 | tf_op jit(solution)/shard_map/ppermute | solution.py:50
  41.9 5.4 %collective-permute-start.4 = (bf16[3,2,128,256]{3,2,1,0:T(8,128)(2,1)S(1)}, bf16[3,2,128,256]{3,2,1,0:T(8,128)(2,1)S(1)}, u32[]{:S(2)}, u32[]{:S(2)}) collective-permute-start(bf16[3,2,128,256]{3,2,1,0:T(8,128)(2,1)S(1)} %collective-permute-done.2), channel_id=1, source_target_pairs={{0,240},{16,0},{32,16},{48,32},{64,48},{80,64},{96,80},{112,96},{1... | collective-permute-start | bytes 1179656 | tf_op jit(solution)/shard_map/ppermute | solution.py:51
  48.9 5.2 %collective-permute-done.3 = bf16[3,2,128,256]{3,2,1,0:T(8,128)(2,1)S(1)} collective-permute-done((bf16[3,2,128,256]{3,2,1,0:T(8,128)(2,1)S(1)}, bf16[3,2,128,256]{3,2,1,0:T(8,128)(2,1)S(1)}, u32[]{:S(2)}, u32[]{:S(2)}) %collective-permute-start.3) | collective-permute-done | bytes 393248 | tf_op jit(solution)/shard_map/ppermute | solution.py:50
  56.8 5.4 %collective-permute-start.6 = (bf16[3,2,128,256]{3,2,1,0:T(8,128)(2,1)S(1)}, bf16[3,2,128,256]{3,2,1,0:T(8,128)(2,1)S(1)}, u32[]{:S(2)}, u32[]{:S(2)}) collective-permute-start(bf16[3,2,128,256]{3,2,1,0:T(8,128)(2,1)S(1)} %collective-permute-done.4), channel_id=1, source_target_pairs={{0,240},{16,0},{32,16},{48,32},{64,48},{80,64},{96,80},{112,96},{1... | collective-permute-start | bytes 1179656 | tf_op jit(solution)/shard_map/ppermute | solution.py:51
  63.8 4.4 %collective-permute-done.5 = bf16[3,2,128,256]{3,2,1,0:T(8,128)(2,1)S(1)} collective-permute-done((bf16[3,2,128,256]{3,2,1,0:T(8,128)(2,1)S(1)}, bf16[3,2,128,256]{3,2,1,0:T(8,128)(2,1)S(1)}, u32[]{:S(2)}, u32[]{:S(2)}) %collective-permute-start.5) | collective-permute-done | bytes 393248 | tf_op jit(solution)/shard_map/ppermute | solution.py:50
  70.9 5.3 %collective-permute-start.8 = (bf16[3,2,128,256]{3,2,1,0:T(8,128)(2,1)S(1)}, bf16[3,2,128,256]{3,2,1,0:T(8,128)(2,1)S(1)}, u32[]{:S(2)}, u32[]{:S(2)}) collective-permute-start(bf16[3,2,128,256]{3,2,1,0:T(8,128)(2,1)S(1)} %collective-permute-done.6), channel_id=1, source_target_pairs={{0,240},{16,0},{32,16},{48,32},{64,48},{80,64},{96,80},{112,96},{1... | collective-permute-start | bytes 1179656 | tf_op jit(solution)/shard_map/ppermute | solution.py:51
  77.7 3.3 %collective-permute-done.7 = bf16[3,2,128,256]{3,2,1,0:T(8,128)(2,1)S(1)} collective-permute-done((bf16[3,2,128,256]{3,2,1,0:T(8,128)(2,1)S(1)}, bf16[3,2,128,256]{3,2,1,0:T(8,128)(2,1)S(1)}, u32[]{:S(2)}, u32[]{:S(2)}) %collective-permute-start.7) | collective-permute-done | bytes 393248 | tf_op jit(solution)/shard_map/ppermute | solution.py:50
  82.0 5.3 %collective-permute-start.10 = (bf16[3,2,128,256]{3,2,1,0:T(8,128)(2,1)S(1)}, bf16[3,2,128,256]{3,2,1,0:T(8,128)(2,1)S(1)}, u32[]{:S(2)}, u32[]{:S(2)}) collective-permute-start(bf16[3,2,128,256]{3,2,1,0:T(8,128)(2,1)S(1)} %collective-permute-done.8), channel_id=1, source_target_pairs={{0,240},{16,0},{32,16},{48,32},{64,48},{80,64},{96,80},{112,96},{1... | collective-permute-start | bytes 1179656 | tf_op jit(solution)/shard_map/ppermute | solution.py:51
  87.3 1.9 %collective-permute-start.9 = (bf16[3,2,128,256]{3,2,1,0:T(8,128)(2,1)S(1)}, bf16[3,2,128,256]{3,2,1,0:T(8,128)(2,1)S(1)}, u32[]{:S(2)}, u32[]{:S(2)}) collective-permute-start(bf16[3,2,128,256]{3,2,1,0:T(8,128)(2,1)S(1)} %collective-permute-done.7), channel_id=1, source_target_pairs={{0,16},{16,32},{32,48},{48,64},{64,80},{80,96},{96,112},{112,128},... | collective-permute-start | bytes 1179656 | tf_op jit(solution)/shard_map/ppermute | solution.py:50
  92.0 5.0 %collective-permute-done.9 = bf16[3,2,128,256]{3,2,1,0:T(8,128)(2,1)S(1)} collective-permute-done((bf16[3,2,128,256]{3,2,1,0:T(8,128)(2,1)S(1)}, bf16[3,2,128,256]{3,2,1,0:T(8,128)(2,1)S(1)}, u32[]{:S(2)}, u32[]{:S(2)}) %collective-permute-start.9) | collective-permute-done | bytes 393248 | tf_op jit(solution)/shard_map/ppermute | solution.py:50
  97.0 1.9 %collective-permute-start.11 = (bf16[3,2,128,256]{3,2,1,0:T(8,128)(2,1)S(1)}, bf16[3,2,128,256]{3,2,1,0:T(8,128)(2,1)S(1)}, u32[]{:S(2)}, u32[]{:S(2)}) collective-permute-start(bf16[3,2,128,256]{3,2,1,0:T(8,128)(2,1)S(1)} %collective-permute-done.9), channel_id=1, source_target_pairs={{0,16},{16,32},{32,48},{48,64},{64,80},{80,96},{96,112},{112,128},... | collective-permute-start | bytes 1179656 | tf_op jit(solution)/shard_map/ppermute | solution.py:50
  98.9 4.6 %collective-permute-start.12 = (bf16[3,2,128,256]{3,2,1,0:T(8,128)(2,1)S(1)}, bf16[3,2,128,256]{3,2,1,0:T(8,128)(2,1)S(1)}, u32[]{:S(2)}, u32[]{:S(2)}) collective-permute-start(bf16[3,2,128,256]{3,2,1,0:T(8,128)(2,1)S(1)} %collective-permute-done.10), channel_id=1, source_target_pairs={{0,240},{16,0},{32,16},{48,32},{64,48},{80,64},{96,80},{112,96},{1... | collective-permute-start | bytes 1179656 | tf_op jit(solution)/shard_map/ppermute | solution.py:51
  110.1 5.0 %collective-permute-start.14 = (bf16[3,2,128,256]{3,2,1,0:T(8,128)(2,1)S(1)}, bf16[3,2,128,256]{3,2,1,0:T(8,128)(2,1)S(1)}, u32[]{:S(2)}, u32[]{:S(2)}) collective-permute-start(bf16[3,2,128,256]{3,2,1,0:T(8,128)(2,1)S(1)} %collective-permute-done.12), channel_id=1, source_target_pairs={{0,240},{16,0},{32,16},{48,32},{64,48},{80,64},{96,80},{112,96},{1... | collective-permute-start | bytes 1179656 | tf_op jit(solution)/shard_map/ppermute | solution.py:51
  119.9 3.1 %collective-permute-start.15 = (bf16[3,1,128,256]{3,2,1,0:T(8,128)(2,1)S(1)}, bf16[3,1,128,256]{3,2,1,0:T(8,128)(2,1)S(1)}, u32[]{:S(2)}, u32[]{:S(2)}) collective-permute-start(bf16[3,1,128,256]{3,2,1,0:T(8,128)(2,1)S(1)} %slice.143), channel_id=1, source_target_pairs={{0,16},{16,32},{32,48},{48,64},{64,80},{80,96},{96,112},{112,128},... | collective-permute-start | bytes 589832 | tf_op jit(solution)/shard_map/ppermute | solution.py:55
  123.0 3.9 %collective-permute-start.16 = (bf16[3,1,128,256]{3,2,1,0:T(8,128)(2,1)S(1)}, bf16[3,1,128,256]{3,2,1,0:T(8,128)(2,1)S(1)}, u32[]{:S(2)}, u32[]{:S(2)}) collective-permute-start(bf16[3,1,128,256]{3,2,1,0:T(8,128)(2,1)S(1)} %slice.144), channel_id=1, source_target_pairs={{0,240},{16,0},{32,16},{48,32},{64,48},{80,64},{96,80},{112,96},{1... | collective-permute-start | bytes 589832 | tf_op jit(solution)/shard_map/ppermute | solution.py:56
  130.2 7.0 %convolution_bitcast_fusion = f32[3,512,256]{2,1,0:T(8,128)S(1)} fusion(bf16[512,4096,1]{1,0,2:T(8,128)(2,1)} %bitcast.36, bf16[3,4096,256]{2,1,0:T(8,128)(2,1)} %bitcast.34), kind=kOutput, calls=%fused_computation | convolution fusion | flops 3221225472 | bytes 12058624 | tf_op jit(solution)/shard_map/sk,ikc->isc/dot_general | solution.py:83
  138.7 25.9 %all_to_all.10 = bf16[16,48,256]{2,1,0:T(8,128)(2,1)S(1)} all-to-all(bf16[16,48,256]{2,1,0:T(8,128)(2,1)S(1)} %pad_maximum_fusion.1), channel_id=1, replica_groups=mesh['fsdp'=32,'tp'=16] {'tp'}, dimensions={0} | all-to-all | bytes 786432 | tf_op jit(solution)/shard_map/all_to_all | solution.py:108
  (66 shorter events, 35.5 us)
Async XLA Ops:
  0.6 19.4 %collective-permute-start = (bf16[3,128,256]{2,1,0:T(8,128)(2,1)}, bf16[3,128,256]{2,1,0:T(8,128)(2,1)S(1)}, u32[]{:S(2)}, u32[]{:S(2)}) collective-permute-start(bf16[3,128,256]{2,1,0:T(8,128)(2,1)} %param.13), channel_id=1, source_target_pairs={{0,256},{16,272},{32,288},{48,304},{64,320},{80,336},{96,352},{112... | collective-permute-start | bytes 589832 | tf_op jit(solution)/shard_map/ppermute | solution.py:29
  7.2 11.9 %copy-start.1 = (f32[16,7]{0,1:T(8,128)S(1)}, f32[16,7]{0,1:T(8,128)}, u32[]{:S(2)}) copy-start(f32[16,7]{0,1:T(8,128)} %param.14) | copy-start | bytes 1348
  7.2 12.8 %copy-start = (bf16[3,128,256]{2,1,0:T(8,128)(2,1)S(1)}, bf16[3,128,256]{2,1,0:T(8,128)(2,1)}, u32[]{:S(2)}) copy-start(bf16[3,128,256]{2,1,0:T(8,128)(2,1)} %param.13) | copy-start | bytes 589828
  9.8 21.8 %copy-start.2 = (s32[1,512]{1,0:T(1,128)S(1)}, s32[1,512]{1,0:T(1,128)}, u32[]{:S(2)}) copy-start(s32[1,512]{1,0:T(1,128)} %param.15) | copy-start | bytes 6148
  9.8 120.4 %all-to-all-start = ((bf16[16,32,4096]{2,1,0:T(8,128)(2,1)}), bf16[16,32,4096]{2,1,0:T(8,128)(2,1)}, u32[]{:S(2)}, u32[]{:S(2)}) async-start(bf16[16,32,4096]{2,1,0:T(8,128)(2,1)} %broadcast_in_dim.98), calls=%async_computation | async-start | bytes 8388608 | tf_op jit(solution)/shard_map/all_to_all | solution.py:80
  20.1 19.1 %collective-permute-start.1 = (bf16[3,2,128,256]{3,2,1,0:T(8,128)(2,1)S(1)}, bf16[3,2,128,256]{3,2,1,0:T(8,128)(2,1)S(1)}, u32[]{:S(2)}, u32[]{:S(2)}) collective-permute-start(bf16[3,2,128,256]{3,2,1,0:T(8,128)(2,1)S(1)} %get-tuple-element.69), channel_id=1, source_target_pairs={{0,16},{16,32},{32,48},{48,64},{64,80},{80,96},{96,112},{112,128},... | collective-permute-start | bytes 1179656 | tf_op jit(solution)/shard_map/ppermute | solution.py:50
  22.2 17.8 %collective-permute-start.2 = (bf16[3,2,128,256]{3,2,1,0:T(8,128)(2,1)S(1)}, bf16[3,2,128,256]{3,2,1,0:T(8,128)(2,1)S(1)}, u32[]{:S(2)}, u32[]{:S(2)}) collective-permute-start(bf16[3,2,128,256]{3,2,1,0:T(8,128)(2,1)S(1)} %get-tuple-element.69), channel_id=1, source_target_pairs={{0,240},{16,0},{32,16},{48,32},{64,48},{80,64},{96,80},{112,96},{1... | collective-permute-start | bytes 1179656 | tf_op jit(solution)/shard_map/ppermute | solution.py:51
  40.0 14.1 %collective-permute-start.3 = (bf16[3,2,128,256]{3,2,1,0:T(8,128)(2,1)S(1)}, bf16[3,2,128,256]{3,2,1,0:T(8,128)(2,1)S(1)}, u32[]{:S(2)}, u32[]{:S(2)}) collective-permute-start(bf16[3,2,128,256]{3,2,1,0:T(8,128)(2,1)S(1)} %collective-permute-done.1), channel_id=1, source_target_pairs={{0,16},{16,32},{32,48},{48,64},{64,80},{80,96},{96,112},{112,128},... | collective-permute-start | bytes 1179656 | tf_op jit(solution)/shard_map/ppermute | solution.py:50
  41.9 13.0 %collective-permute-start.4 = (bf16[3,2,128,256]{3,2,1,0:T(8,128)(2,1)S(1)}, bf16[3,2,128,256]{3,2,1,0:T(8,128)(2,1)S(1)}, u32[]{:S(2)}, u32[]{:S(2)}) collective-permute-start(bf16[3,2,128,256]{3,2,1,0:T(8,128)(2,1)S(1)} %collective-permute-done.2), channel_id=1, source_target_pairs={{0,240},{16,0},{32,16},{48,32},{64,48},{80,64},{96,80},{112,96},{1... | collective-permute-start | bytes 1179656 | tf_op jit(solution)/shard_map/ppermute | solution.py:51
  54.9 13.3 %collective-permute-start.5 = (bf16[3,2,128,256]{3,2,1,0:T(8,128)(2,1)S(1)}, bf16[3,2,128,256]{3,2,1,0:T(8,128)(2,1)S(1)}, u32[]{:S(2)}, u32[]{:S(2)}) collective-permute-start(bf16[3,2,128,256]{3,2,1,0:T(8,128)(2,1)S(1)} %collective-permute-done.3), channel_id=1, source_target_pairs={{0,16},{16,32},{32,48},{48,64},{64,80},{80,96},{96,112},{112,128},... | collective-permute-start | bytes 1179656 | tf_op jit(solution)/shard_map/ppermute | solution.py:50
  56.8 12.2 %collective-permute-start.6 = (bf16[3,2,128,256]{3,2,1,0:T(8,128)(2,1)S(1)}, bf16[3,2,128,256]{3,2,1,0:T(8,128)(2,1)S(1)}, u32[]{:S(2)}, u32[]{:S(2)}) collective-permute-start(bf16[3,2,128,256]{3,2,1,0:T(8,128)(2,1)S(1)} %collective-permute-done.4), channel_id=1, source_target_pairs={{0,240},{16,0},{32,16},{48,32},{64,48},{80,64},{96,80},{112,96},{1... | collective-permute-start | bytes 1179656 | tf_op jit(solution)/shard_map/ppermute | solution.py:51
  68.9 12.1 %collective-permute-start.7 = (bf16[3,2,128,256]{3,2,1,0:T(8,128)(2,1)S(1)}, bf16[3,2,128,256]{3,2,1,0:T(8,128)(2,1)S(1)}, u32[]{:S(2)}, u32[]{:S(2)}) collective-permute-start(bf16[3,2,128,256]{3,2,1,0:T(8,128)(2,1)S(1)} %collective-permute-done.5), channel_id=1, source_target_pairs={{0,16},{16,32},{32,48},{48,64},{64,80},{80,96},{96,112},{112,128},... | collective-permute-start | bytes 1179656 | tf_op jit(solution)/shard_map/ppermute | solution.py:50
  70.9 11.1 %collective-permute-start.8 = (bf16[3,2,128,256]{3,2,1,0:T(8,128)(2,1)S(1)}, bf16[3,2,128,256]{3,2,1,0:T(8,128)(2,1)S(1)}, u32[]{:S(2)}, u32[]{:S(2)}) collective-permute-start(bf16[3,2,128,256]{3,2,1,0:T(8,128)(2,1)S(1)} %collective-permute-done.6), channel_id=1, source_target_pairs={{0,240},{16,0},{32,16},{48,32},{64,48},{80,64},{96,80},{112,96},{1... | collective-permute-start | bytes 1179656 | tf_op jit(solution)/shard_map/ppermute | solution.py:51
  82.0 10.0 %collective-permute-start.10 = (bf16[3,2,128,256]{3,2,1,0:T(8,128)(2,1)S(1)}, bf16[3,2,128,256]{3,2,1,0:T(8,128)(2,1)S(1)}, u32[]{:S(2)}, u32[]{:S(2)}) collective-permute-start(bf16[3,2,128,256]{3,2,1,0:T(8,128)(2,1)S(1)} %collective-permute-done.8), channel_id=1, source_target_pairs={{0,240},{16,0},{32,16},{48,32},{64,48},{80,64},{96,80},{112,96},{1... | collective-permute-start | bytes 1179656 | tf_op jit(solution)/shard_map/ppermute | solution.py:51
  87.3 9.7 %collective-permute-start.9 = (bf16[3,2,128,256]{3,2,1,0:T(8,128)(2,1)S(1)}, bf16[3,2,128,256]{3,2,1,0:T(8,128)(2,1)S(1)}, u32[]{:S(2)}, u32[]{:S(2)}) collective-permute-start(bf16[3,2,128,256]{3,2,1,0:T(8,128)(2,1)S(1)} %collective-permute-done.7), channel_id=1, source_target_pairs={{0,16},{16,32},{32,48},{48,64},{64,80},{80,96},{96,112},{112,128},... | collective-permute-start | bytes 1179656 | tf_op jit(solution)/shard_map/ppermute | solution.py:50
  97.0 9.7 %collective-permute-start.11 = (bf16[3,2,128,256]{3,2,1,0:T(8,128)(2,1)S(1)}, bf16[3,2,128,256]{3,2,1,0:T(8,128)(2,1)S(1)}, u32[]{:S(2)}, u32[]{:S(2)}) collective-permute-start(bf16[3,2,128,256]{3,2,1,0:T(8,128)(2,1)S(1)} %collective-permute-done.9), channel_id=1, source_target_pairs={{0,16},{16,32},{32,48},{48,64},{64,80},{80,96},{96,112},{112,128},... | collective-permute-start | bytes 1179656 | tf_op jit(solution)/shard_map/ppermute | solution.py:50
  98.9 9.3 %collective-permute-start.12 = (bf16[3,2,128,256]{3,2,1,0:T(8,128)(2,1)S(1)}, bf16[3,2,128,256]{3,2,1,0:T(8,128)(2,1)S(1)}, u32[]{:S(2)}, u32[]{:S(2)}) collective-permute-start(bf16[3,2,128,256]{3,2,1,0:T(8,128)(2,1)S(1)} %collective-permute-done.10), channel_id=1, source_target_pairs={{0,240},{16,0},{32,16},{48,32},{64,48},{80,64},{96,80},{112,96},{1... | collective-permute-start | bytes 1179656 | tf_op jit(solution)/shard_map/ppermute | solution.py:51
  108.2 10.2 %collective-permute-start.13 = (bf16[3,2,128,256]{3,2,1,0:T(8,128)(2,1)S(1)}, bf16[3,2,128,256]{3,2,1,0:T(8,128)(2,1)S(1)}, u32[]{:S(2)}, u32[]{:S(2)}) collective-permute-start(bf16[3,2,128,256]{3,2,1,0:T(8,128)(2,1)S(1)} %collective-permute-done.11), channel_id=1, source_target_pairs={{0,16},{16,32},{32,48},{48,64},{64,80},{80,96},{96,112},{112,128},... | collective-permute-start | bytes 1179656 | tf_op jit(solution)/shard_map/ppermute | solution.py:50
  110.1 9.7 %collective-permute-start.14 = (bf16[3,2,128,256]{3,2,1,0:T(8,128)(2,1)S(1)}, bf16[3,2,128,256]{3,2,1,0:T(8,128)(2,1)S(1)}, u32[]{:S(2)}, u32[]{:S(2)}) collective-permute-start(bf16[3,2,128,256]{3,2,1,0:T(8,128)(2,1)S(1)} %collective-permute-done.12), channel_id=1, source_target_pairs={{0,240},{16,0},{32,16},{48,32},{64,48},{80,64},{96,80},{112,96},{1... | collective-permute-start | bytes 1179656 | tf_op jit(solution)/shard_map/ppermute | solution.py:51
  119.9 8.5 %collective-permute-start.15 = (bf16[3,1,128,256]{3,2,1,0:T(8,128)(2,1)S(1)}, bf16[3,1,128,256]{3,2,1,0:T(8,128)(2,1)S(1)}, u32[]{:S(2)}, u32[]{:S(2)}) collective-permute-start(bf16[3,1,128,256]{3,2,1,0:T(8,128)(2,1)S(1)} %slice.143), channel_id=1, source_target_pairs={{0,16},{16,32},{32,48},{48,64},{64,80},{80,96},{96,112},{112,128},... | collective-permute-start | bytes 589832 | tf_op jit(solution)/shard_map/ppermute | solution.py:55
  123.0 6.5 %collective-permute-start.16 = (bf16[3,1,128,256]{3,2,1,0:T(8,128)(2,1)S(1)}, bf16[3,1,128,256]{3,2,1,0:T(8,128)(2,1)S(1)}, u32[]{:S(2)}, u32[]{:S(2)}) collective-permute-start(bf16[3,1,128,256]{3,2,1,0:T(8,128)(2,1)S(1)} %slice.144), channel_id=1, source_target_pairs={{0,240},{16,0},{32,16},{48,32},{64,48},{80,64},{96,80},{112,96},{1... | collective-permute-start | bytes 589832 | tf_op jit(solution)/shard_map/ppermute | solution.py:56
  130.2 8.0 %copy-start.3 = (s32[1,16]{1,0:T(1,128)S(1)}, s32[1,16]{1,0:T(1,128)}, u32[]{:S(2)}) copy-start(s32[1,16]{1,0:T(1,128)} %param.16) | copy-start | bytes 196

commit v9 on v5

--- a/solution.py
+++ b/solution.py
@@ -87,20 +87,25 @@
     rounded = lax.reduce_precision(partial_sum, exponent_bits=8, mantissa_bits=7)
     high = rounded.astype(jnp.bfloat16)
     low = (partial_sum - rounded).astype(jnp.bfloat16)
+    lanes = 128
     extra_rows = 16
-    extra = jnp.zeros((extra_rows, channels), jnp.bfloat16)
+    extra = jnp.zeros((extra_rows, lanes), jnp.bfloat16)
     extra = extra.at[0, : high.shape[0]].set(high).at[1, : low.shape[0]].set(low)
-    blocks = mixed_local.reshape(tp_size, local_rows, channels)
+    pieces = channels // lanes
+    blocks = jnp.transpose(
+        mixed_local.reshape(tp_size, local_rows, pieces, lanes), (0, 2, 1, 3)
+    ).reshape(tp_size, pieces * local_rows, lanes)
     payload = jnp.concatenate(
-        [blocks, jnp.broadcast_to(extra[None], (tp_size, extra_rows, channels))], axis=1
+        [blocks, jnp.broadcast_to(extra[None], (tp_size, extra_rows, lanes))], axis=1
     )
     gathered = lax.all_to_all(payload, "tp", 0, 0, tiled=False)
-    own_rows = jnp.transpose(gathered[:, :local_rows], (1, 0, 2)).reshape(
-        local_rows, tp_size * channels
-    )
+    own_rows = jnp.transpose(
+        gathered[:, : pieces * local_rows].reshape(tp_size, pieces, local_rows, lanes), (2, 0, 1, 3)
+    ).reshape(local_rows, tp_size * channels)
+    data_rows = pieces * local_rows
     count = positions.shape[0]
-    received = gathered[:, local_rows, :count].astype(jnp.float32) + gathered[
-        :, local_rows + 1, :count
+    received = gathered[:, data_rows, :count].astype(jnp.float32) + gathered[
+        :, data_rows + 1, :count
     ].astype(jnp.float32)
     needle_score = (jnp.sum(received, axis=0) / math.sqrt(model_width))[None, :]
     return (own_rows, needle_score)

time: 163 us -> 162 us (level)
    unnamed x22 -> x21, local copies, waits for them, and re-layouts: 11.2 us -> 11.2 us
where the time goes in v9:
time: 162 us; the launch traced here: 161 us
  starting transfers between devices  78.7 us (49%)
  waiting for transfers between devices  31.2 us (19%)
  blocking collectives  19.8 us (12%)
  local copies, waits for them, and re-layouts  16.9 us (10%)
  matrix products  7.34 us (5%)
  other arithmetic  6.49 us (4%)
    ppermute x7, starting transfers between devices, gather_weights(): left = lax.ppermute(left, 'fsdp', z_down)  44.2 us
    all_to_all x1, blocking collectives, local(): gathered = lax.all_to_all(payload, 'tp', 0, 0, tiled=False)  19.8 us
    ppermute x7, waiting for transfers between devices, gather_weights(): left = lax.ppermute(left, 'fsdp', z_down)  18.8 us
    ppermute x7, starting transfers between devices, gather_weights(): right = lax.ppermute(right, 'fsdp', z_up)  13.4 us
    unnamed x21, local copies, waits for them, and re-layouts  11.2 us
    all_to_all x1, starting transfers between devices, local(): lax.all_to_all(spread, 'tp', 0, 0, tiled=False)  10.6 us
    ppermute x7, waiting for transfers between devices, gather_weights(): right = lax.ppermute(right, 'fsdp', z_up)  7.39 us
    dot_general x1, matrix products, local(): jnp.einsum('sk,ikc->isc', slab_rows, weights, preferred_element_type=jnp....  7.05 us
  transfers between devices with their start and end apart: 18, of which 9 were waited for; matrix products, arithmetic and copies ran while one was open for 12% of the time, Pallas kernels for 0%

profile of v9, /device:TPU:1, one launch (start us, length us, event | category | flops | bytes accessed | tf_op | source)
XLA Modules:
  0.0 161.5 jit_solution(7986566617121111698)
XLA Ops:
  0.6 3.9 %collective-permute-start = (bf16[3,128,256]{2,1,0:T(8,128)(2,1)}, bf16[3,128,256]{2,1,0:T(8,128)(2,1)S(1)}, u32[]{:S(2)}, u32[]{:S(2)}) collective-permute-start(bf16[3,128,256]{2,1,0:T(8,128)(2,1)} %param.13), channel_id=1, source_target_pairs={{0,256},{16,272},{32,288},{48,304},{64,320},{80,336},{96,352},{112... | collective-permute-start | bytes 589832 | tf_op jit(solution)/shard_map/ppermute | solution.py:29
  4.6 3.2 %collective-permute-done = bf16[3,128,256]{2,1,0:T(8,128)(2,1)S(1)} collective-permute-done((bf16[3,128,256]{2,1,0:T(8,128)(2,1)}, bf16[3,128,256]{2,1,0:T(8,128)(2,1)S(1)}, u32[]{:S(2)}, u32[]{:S(2)}) %collective-permute-start) | collective-permute-done | bytes 196640 | tf_op jit(solution)/shard_map/ppermute | solution.py:29
  8.8 12.6 %collective-permute-start.1 = (bf16[3,2,128,256]{3,2,1,0:T(8,128)(2,1)S(1)}, bf16[3,2,128,256]{3,2,1,0:T(8,128)(2,1)S(1)}, u32[]{:S(2)}, u32[]{:S(2)}) collective-permute-start(bf16[3,2,128,256]{3,2,1,0:T(8,128)(2,1)S(1)} %pad_maximum_fusion), channel_id=1, source_target_pairs={{0,240},{16,0},{32,16},{48,32},{64,48},{80,64},{96,80},{112,96},{1... | collective-permute-start | bytes 1179656 | tf_op jit(solution)/shard_map/ppermute | solution.py:39
  21.5 1.9 %collective-permute-start.8 = (bf16[3,2,128,256]{3,2,1,0:T(8,128)(2,1)S(1)}, bf16[3,2,128,256]{3,2,1,0:T(8,128)(2,1)S(1)}, u32[]{:S(2)}, u32[]{:S(2)}) collective-permute-start(bf16[3,2,128,256]{3,2,1,0:T(8,128)(2,1)S(1)} %pad_maximum_fusion), channel_id=1, source_target_pairs={{0,16},{16,32},{32,48},{48,64},{64,80},{80,96},{96,112},{112,128},... | collective-permute-start | bytes 1179656 | tf_op jit(solution)/shard_map/ppermute | solution.py:38
  23.4 4.9 %collective-permute-done.1 = bf16[3,2,128,256]{3,2,1,0:T(8,128)(2,1)S(1)} collective-permute-done((bf16[3,2,128,256]{3,2,1,0:T(8,128)(2,1)S(1)}, bf16[3,2,128,256]{3,2,1,0:T(8,128)(2,1)S(1)}, u32[]{:S(2)}, u32[]{:S(2)}) %collective-permute-start.1) | collective-permute-done | bytes 393248 | tf_op jit(solution)/shard_map/ppermute | solution.py:39
  28.3 5.3 %collective-permute-start.2 = (bf16[3,2,128,256]{3,2,1,0:T(8,128)(2,1)S(1)}, bf16[3,2,128,256]{3,2,1,0:T(8,128)(2,1)S(1)}, u32[]{:S(2)}, u32[]{:S(2)}) collective-permute-start(bf16[3,2,128,256]{3,2,1,0:T(8,128)(2,1)S(1)} %collective-permute-done.1), channel_id=1, source_target_pairs={{0,240},{16,0},{32,16},{48,32},{64,48},{80,64},{96,80},{112,96},{1... | collective-permute-start | bytes 1179656 | tf_op jit(solution)/shard_map/ppermute | solution.py:39
  33.6 1.9 %collective-permute-start.9 = (bf16[3,2,128,256]{3,2,1,0:T(8,128)(2,1)S(1)}, bf16[3,2,128,256]{3,2,1,0:T(8,128)(2,1)S(1)}, u32[]{:S(2)}, u32[]{:S(2)}) collective-permute-start(bf16[3,2,128,256]{3,2,1,0:T(8,128)(2,1)S(1)} %collective-permute-done.8), channel_id=1, source_target_pairs={{0,16},{16,32},{32,48},{48,64},{64,80},{80,96},{96,112},{112,128},... | collective-permute-start | bytes 1179656 | tf_op jit(solution)/shard_map/ppermute | solution.py:38
  36.7 2.9 %collective-permute-done.2 = bf16[3,2,128,256]{3,2,1,0:T(8,128)(2,1)S(1)} collective-permute-done((bf16[3,2,128,256]{3,2,1,0:T(8,128)(2,1)S(1)}, bf16[3,2,128,256]{3,2,1,0:T(8,128)(2,1)S(1)}, u32[]{:S(2)}, u32[]{:S(2)}) %collective-permute-start.2) | collective-permute-done | bytes 393248 | tf_op jit(solution)/shard_map/ppermute | solution.py:39
  39.5 5.3 %collective-permute-start.3 = (bf16[3,2,128,256]{3,2,1,0:T(8,128)(2,1)S(1)}, bf16[3,2,128,256]{3,2,1,0:T(8,128)(2,1)S(1)}, u32[]{:S(2)}, u32[]{:S(2)}) collective-permute-start(bf16[3,2,128,256]{3,2,1,0:T(8,128)(2,1)S(1)} %collective-permute-done.2), channel_id=1, source_target_pairs={{0,240},{16,0},{32,16},{48,32},{64,48},{80,64},{96,80},{112,96},{1... | collective-permute-start | bytes 1179656 | tf_op jit(solution)/shard_map/ppermute | solution.py:39
  48.3 2.6 %broadcast_in_dim.9 = bf16[16,32,4096]{2,1,0:T(8,128)(2,1)} broadcast(bf16[32,4096]{1,0:T(8,128)(2,1)S(1)} %bitcast.116), dimensions={1,2} | broadcast | bytes 4456448 | tf_op jit(solution)/shard_map/broadcast_in_dim | solution.py:68
  50.9 10.6 %all-to-all-start = ((bf16[16,32,4096]{2,1,0:T(8,128)(2,1)}), bf16[16,32,4096]{2,1,0:T(8,128)(2,1)}, u32[]{:S(2)}, u32[]{:S(2)}) async-start(bf16[16,32,4096]{2,1,0:T(8,128)(2,1)} %broadcast_in_dim.9), calls=%async_computation | async-start | bytes 8388608 | tf_op jit(solution)/shard_map/all_to_all | solution.py:69
  61.5 4.9 %collective-permute-start.4 = (bf16[3,2,128,256]{3,2,1,0:T(8,128)(2,1)S(1)}, bf16[3,2,128,256]{3,2,1,0:T(8,128)(2,1)}, u32[]{:S(2)}, u32[]{:S(2)}) collective-permute-start(bf16[3,2,128,256]{3,2,1,0:T(8,128)(2,1)S(1)} %collective-permute-done.3), channel_id=1, source_target_pairs={{0,240},{16,0},{32,16},{48,32},{64,48},{80,64},{96,80},{112,96},{1... | collective-permute-start | bytes 1179656 | tf_op jit(solution)/shard_map/ppermute | solution.py:39
  66.4 1.9 %collective-permute-start.11 = (bf16[3,2,128,256]{3,2,1,0:T(8,128)(2,1)S(1)}, bf16[3,2,128,256]{3,2,1,0:T(8,128)(2,1)S(1)}, u32[]{:S(2)}, u32[]{:S(2)}) collective-permute-start(bf16[3,2,128,256]{3,2,1,0:T(8,128)(2,1)S(1)} %collective-permute-done.10), channel_id=1, source_target_pairs={{0,16},{16,32},{32,48},{48,64},{64,80},{80,96},{96,112},{112,128},... | collective-permute-start | bytes 1179656 | tf_op jit(solution)/shard_map/ppermute | solution.py:38
  70.1 4.6 %collective-permute-done.4 = bf16[3,2,128,256]{3,2,1,0:T(8,128)(2,1)} collective-permute-done((bf16[3,2,128,256]{3,2,1,0:T(8,128)(2,1)S(1)}, bf16[3,2,128,256]{3,2,1,0:T(8,128)(2,1)}, u32[]{:S(2)}, u32[]{:S(2)}) %collective-permute-start.4) | collective-permute-done | bytes 393248 | tf_op jit(solution)/shard_map/ppermute | solution.py:39
  74.7 5.4 %collective-permute-start.5 = (bf16[3,2,128,256]{3,2,1,0:T(8,128)(2,1)}, bf16[3,2,128,256]{3,2,1,0:T(8,128)(2,1)S(1)}, u32[]{:S(2)}, u32[]{:S(2)}) collective-permute-start(bf16[3,2,128,256]{3,2,1,0:T(8,128)(2,1)} %collective-permute-done.4), channel_id=1, source_target_pairs={{0,240},{16,0},{32,16},{48,32},{64,48},{80,64},{96,80},{112,96},{1... | collective-permute-start | bytes 1179656 | tf_op jit(solution)/shard_map/ppermute | solution.py:39
  83.6 4.3 %collective-permute-done.5 = bf16[3,2,128,256]{3,2,1,0:T(8,128)(2,1)S(1)} collective-permute-done((bf16[3,2,128,256]{3,2,1,0:T(8,128)(2,1)}, bf16[3,2,128,256]{3,2,1,0:T(8,128)(2,1)S(1)}, u32[]{:S(2)}, u32[]{:S(2)}) %collective-permute-start.5) | collective-permute-done | bytes 393248 | tf_op jit(solution)/shard_map/ppermute | solution.py:39
  87.9 5.3 %collective-permute-start.6 = (bf16[3,2,128,256]{3,2,1,0:T(8,128)(2,1)S(1)}, bf16[3,2,128,256]{3,2,1,0:T(8,128)(2,1)S(1)}, u32[]{:S(2)}, u32[]{:S(2)}) collective-permute-start(bf16[3,2,128,256]{3,2,1,0:T(8,128)(2,1)S(1)} %collective-permute-done.5), channel_id=1, source_target_pairs={{0,240},{16,0},{32,16},{48,32},{64,48},{80,64},{96,80},{112,96},{1... | collective-permute-start | bytes 1179656 | tf_op jit(solution)/shard_map/ppermute | solution.py:39
  93.2 1.9 %collective-permute-start.13 = (bf16[3,2,128,256]{3,2,1,0:T(8,128)(2,1)S(1)}, bf16[3,2,128,256]{3,2,1,0:T(8,128)(2,1)S(1)}, u32[]{:S(2)}, u32[]{:S(2)}) collective-permute-start(bf16[3,2,128,256]{3,2,1,0:T(8,128)(2,1)S(1)} %collective-permute-done.12), channel_id=1, source_target_pairs={{0,16},{16,32},{32,48},{48,64},{64,80},{80,96},{96,112},{112,128},... | collective-permute-start | bytes 1179656 | tf_op jit(solution)/shard_map/ppermute | solution.py:38
  97.7 2.2 %collective-permute-done.6 = bf16[3,2,128,256]{3,2,1,0:T(8,128)(2,1)S(1)} collective-permute-done((bf16[3,2,128,256]{3,2,1,0:T(8,128)(2,1)S(1)}, bf16[3,2,128,256]{3,2,1,0:T(8,128)(2,1)S(1)}, u32[]{:S(2)}, u32[]{:S(2)}) %collective-permute-start.6) | collective-permute-done | bytes 393248 | tf_op jit(solution)/shard_map/ppermute | solution.py:39
  99.8 5.4 %collective-permute-start.7 = (bf16[3,2,128,256]{3,2,1,0:T(8,128)(2,1)S(1)}, bf16[3,2,128,256]{3,2,1,0:T(8,128)(2,1)S(1)}, u32[]{:S(2)}, u32[]{:S(2)}) collective-permute-start(bf16[3,2,128,256]{3,2,1,0:T(8,128)(2,1)S(1)} %collective-permute-done.6), channel_id=1, source_target_pairs={{0,240},{16,0},{32,16},{48,32},{64,48},{80,64},{96,80},{112,96},{1... | collective-permute-start | bytes 1179656 | tf_op jit(solution)/shard_map/ppermute | solution.py:39
  108.7 7.4 %collective-permute-done.14 = bf16[3,2,128,256]{3,2,1,0:T(8,128)(2,1)S(1)} collective-permute-done((bf16[3,2,128,256]{3,2,1,0:T(8,128)(2,1)S(1)}, bf16[3,2,128,256]{3,2,1,0:T(8,128)(2,1)S(1)}, u32[]{:S(2)}, u32[]{:S(2)}) %collective-permute-start.14) | collective-permute-done | bytes 393248 | tf_op jit(solution)/shard_map/ppermute | solution.py:38
  118.1 4.6 %collective-permute-start.16 = (bf16[3,1,128,256]{3,2,1,0:T(8,128)(2,1)S(1)}, bf16[3,1,128,256]{3,2,1,0:T(8,128)(2,1)S(1)}, u32[]{:S(2)}, u32[]{:S(2)}) collective-permute-start(bf16[3,1,128,256]{3,2,1,0:T(8,128)(2,1)S(1)} %slice.144), channel_id=1, source_target_pairs={{0,240},{16,0},{32,16},{48,32},{64,48},{80,64},{96,80},{112,96},{1... | collective-permute-start | bytes 589832 | tf_op jit(solution)/shard_map/ppermute | solution.py:43
  131.4 7.0 %convolution_bitcast_fusion = f32[3,512,256]{2,1,0:T(8,128)S(1)} fusion(bf16[512,4096,1]{1,0,2:T(8,128)(2,1)} %bitcast.36, bf16[3,4096,256]{2,1,0:T(8,128)(2,1)} %bitcast.34), kind=kOutput, calls=%fused_computation | convolution fusion | flops 3221225472 | bytes 12058624 | tf_op jit(solution)/shard_map/sk,ikc->isc/dot_general | solution.py:72
  140.0 19.8 %all_to_all.10 = bf16[16,80,128]{2,1,0:T(8,128)(2,1)S(1)} all-to-all(bf16[16,80,128]{2,1,0:T(8,128)(2,1)S(1)} %pad_maximum_fusion.1), channel_id=1, replica_groups=mesh['fsdp'=32,'tp'=16] {'tp'}, dimensions={0} | all-to-all | bytes 655360 | tf_op jit(solution)/shard_map/all_to_all | solution.py:101
  (67 shorter events, 30.6 us)
Async XLA Ops:
  0.6 7.2 %collective-permute-start = (bf16[3,128,256]{2,1,0:T(8,128)(2,1)}, bf16[3,128,256]{2,1,0:T(8,128)(2,1)S(1)}, u32[]{:S(2)}, u32[]{:S(2)}) collective-permute-start(bf16[3,128,256]{2,1,0:T(8,128)(2,1)} %param.13), channel_id=1, source_target_pairs={{0,256},{16,272},{32,288},{48,304},{64,320},{80,336},{96,352},{112... | collective-permute-start | bytes 589832 | tf_op jit(solution)/shard_map/ppermute | solution.py:29
  8.8 19.5 %collective-permute-start.1 = (bf16[3,2,128,256]{3,2,1,0:T(8,128)(2,1)S(1)}, bf16[3,2,128,256]{3,2,1,0:T(8,128)(2,1)S(1)}, u32[]{:S(2)}, u32[]{:S(2)}) collective-permute-start(bf16[3,2,128,256]{3,2,1,0:T(8,128)(2,1)S(1)} %pad_maximum_fusion), channel_id=1, source_target_pairs={{0,240},{16,0},{32,16},{48,32},{64,48},{80,64},{96,80},{112,96},{1... | collective-permute-start | bytes 1179656 | tf_op jit(solution)/shard_map/ppermute | solution.py:39
  21.5 12.2 %collective-permute-start.8 = (bf16[3,2,128,256]{3,2,1,0:T(8,128)(2,1)S(1)}, bf16[3,2,128,256]{3,2,1,0:T(8,128)(2,1)S(1)}, u32[]{:S(2)}, u32[]{:S(2)}) collective-permute-start(bf16[3,2,128,256]{3,2,1,0:T(8,128)(2,1)S(1)} %pad_maximum_fusion), channel_id=1, source_target_pairs={{0,16},{16,32},{32,48},{48,64},{64,80},{80,96},{96,112},{112,128},... | collective-permute-start | bytes 1179656 | tf_op jit(solution)/shard_map/ppermute | solution.py:38
  28.3 11.2 %collective-permute-start.2 = (bf16[3,2,128,256]{3,2,1,0:T(8,128)(2,1)S(1)}, bf16[3,2,128,256]{3,2,1,0:T(8,128)(2,1)S(1)}, u32[]{:S(2)}, u32[]{:S(2)}) collective-permute-start(bf16[3,2,128,256]{3,2,1,0:T(8,128)(2,1)S(1)} %collective-permute-done.1), channel_id=1, source_target_pairs={{0,240},{16,0},{32,16},{48,32},{64,48},{80,64},{96,80},{112,96},{1... | collective-permute-start | bytes 1179656 | tf_op jit(solution)/shard_map/ppermute | solution.py:39
  33.6 11.2 %collective-permute-start.9 = (bf16[3,2,128,256]{3,2,1,0:T(8,128)(2,1)S(1)}, bf16[3,2,128,256]{3,2,1,0:T(8,128)(2,1)S(1)}, u32[]{:S(2)}, u32[]{:S(2)}) collective-permute-start(bf16[3,2,128,256]{3,2,1,0:T(8,128)(2,1)S(1)} %collective-permute-done.8), channel_id=1, source_target_pairs={{0,16},{16,32},{32,48},{48,64},{64,80},{80,96},{96,112},{112,128},... | collective-permute-start | bytes 1179656 | tf_op jit(solution)/shard_map/ppermute | solution.py:38
  39.5 22.0 %collective-permute-start.3 = (bf16[3,2,128,256]{3,2,1,0:T(8,128)(2,1)S(1)}, bf16[3,2,128,256]{3,2,1,0:T(8,128)(2,1)S(1)}, u32[]{:S(2)}, u32[]{:S(2)}) collective-permute-start(bf16[3,2,128,256]{3,2,1,0:T(8,128)(2,1)S(1)} %collective-permute-done.2), channel_id=1, source_target_pairs={{0,240},{16,0},{32,16},{48,32},{64,48},{80,64},{96,80},{112,96},{1... | collective-permute-start | bytes 1179656 | tf_op jit(solution)/shard_map/ppermute | solution.py:39
  44.9 21.5 %collective-permute-start.10 = (bf16[3,2,128,256]{3,2,1,0:T(8,128)(2,1)S(1)}, bf16[3,2,128,256]{3,2,1,0:T(8,128)(2,1)S(1)}, u32[]{:S(2)}, u32[]{:S(2)}) collective-permute-start(bf16[3,2,128,256]{3,2,1,0:T(8,128)(2,1)S(1)} %collective-permute-done.9), channel_id=1, source_target_pairs={{0,16},{16,32},{32,48},{48,64},{64,80},{80,96},{96,112},{112,128},... | collective-permute-start | bytes 1179656 | tf_op jit(solution)/shard_map/ppermute | solution.py:38
  48.3 20.0 %copy-start.1 = (s32[1,512]{1,0:T(1,128)S(1)}, s32[1,512]{1,0:T(1,128)}, u32[]{:S(2)}) copy-start(s32[1,512]{1,0:T(1,128)} %param.15) | copy-start | bytes 6148
  48.3 20.1 %copy-start = (f32[16,7]{0,1:T(8,128)S(1)}, f32[16,7]{0,1:T(8,128)}, u32[]{:S(2)}) copy-start(f32[16,7]{0,1:T(8,128)} %param.14) | copy-start | bytes 1348
  50.9 80.5 %all-to-all-start = ((bf16[16,32,4096]{2,1,0:T(8,128)(2,1)}), bf16[16,32,4096]{2,1,0:T(8,128)(2,1)}, u32[]{:S(2)}, u32[]{:S(2)}) async-start(bf16[16,32,4096]{2,1,0:T(8,128)(2,1)} %broadcast_in_dim.9), calls=%async_computation | async-start | bytes 8388608 | tf_op jit(solution)/shard_map/all_to_all | solution.py:69
  61.5 13.2 %collective-permute-start.4 = (bf16[3,2,128,256]{3,2,1,0:T(8,128)(2,1)S(1)}, bf16[3,2,128,256]{3,2,1,0:T(8,128)(2,1)}, u32[]{:S(2)}, u32[]{:S(2)}) collective-permute-start(bf16[3,2,128,256]{3,2,1,0:T(8,128)(2,1)S(1)} %collective-permute-done.3), channel_id=1, source_target_pairs={{0,240},{16,0},{32,16},{48,32},{64,48},{80,64},{96,80},{112,96},{1... | collective-permute-start | bytes 1179656 | tf_op jit(solution)/shard_map/ppermute | solution.py:39
  66.4 13.8 %collective-permute-start.11 = (bf16[3,2,128,256]{3,2,1,0:T(8,128)(2,1)S(1)}, bf16[3,2,128,256]{3,2,1,0:T(8,128)(2,1)S(1)}, u32[]{:S(2)}, u32[]{:S(2)}) collective-permute-start(bf16[3,2,128,256]{3,2,1,0:T(8,128)(2,1)S(1)} %collective-permute-done.10), channel_id=1, source_target_pairs={{0,16},{16,32},{32,48},{48,64},{64,80},{80,96},{96,112},{112,128},... | collective-permute-start | bytes 1179656 | tf_op jit(solution)/shard_map/ppermute | solution.py:38
  74.7 13.2 %collective-permute-start.5 = (bf16[3,2,128,256]{3,2,1,0:T(8,128)(2,1)}, bf16[3,2,128,256]{3,2,1,0:T(8,128)(2,1)S(1)}, u32[]{:S(2)}, u32[]{:S(2)}) collective-permute-start(bf16[3,2,128,256]{3,2,1,0:T(8,128)(2,1)} %collective-permute-done.4), channel_id=1, source_target_pairs={{0,240},{16,0},{32,16},{48,32},{64,48},{80,64},{96,80},{112,96},{1... | collective-permute-start | bytes 1179656 | tf_op jit(solution)/shard_map/ppermute | solution.py:39
  80.2 13.1 %collective-permute-start.12 = (bf16[3,2,128,256]{3,2,1,0:T(8,128)(2,1)S(1)}, bf16[3,2,128,256]{3,2,1,0:T(8,128)(2,1)S(1)}, u32[]{:S(2)}, u32[]{:S(2)}) collective-permute-start(bf16[3,2,128,256]{3,2,1,0:T(8,128)(2,1)S(1)} %collective-permute-done.11), channel_id=1, source_target_pairs={{0,16},{16,32},{32,48},{48,64},{64,80},{80,96},{96,112},{112,128},... | collective-permute-start | bytes 1179656 | tf_op jit(solution)/shard_map/ppermute | solution.py:38
  87.9 11.9 %collective-permute-start.6 = (bf16[3,2,128,256]{3,2,1,0:T(8,128)(2,1)S(1)}, bf16[3,2,128,256]{3,2,1,0:T(8,128)(2,1)S(1)}, u32[]{:S(2)}, u32[]{:S(2)}) collective-permute-start(bf16[3,2,128,256]{3,2,1,0:T(8,128)(2,1)S(1)} %collective-permute-done.5), channel_id=1, source_target_pairs={{0,240},{16,0},{32,16},{48,32},{64,48},{80,64},{96,80},{112,96},{1... | collective-permute-start | bytes 1179656 | tf_op jit(solution)/shard_map/ppermute | solution.py:39
  93.2 12.0 %collective-permute-start.13 = (bf16[3,2,128,256]{3,2,1,0:T(8,128)(2,1)S(1)}, bf16[3,2,128,256]{3,2,1,0:T(8,128)(2,1)S(1)}, u32[]{:S(2)}, u32[]{:S(2)}) collective-permute-start(bf16[3,2,128,256]{3,2,1,0:T(8,128)(2,1)S(1)} %collective-permute-done.12), channel_id=1, source_target_pairs={{0,16},{16,32},{32,48},{48,64},{64,80},{80,96},{96,112},{112,128},... | collective-permute-start | bytes 1179656 | tf_op jit(solution)/shard_map/ppermute | solution.py:38
  99.8 18.2 %collective-permute-start.7 = (bf16[3,2,128,256]{3,2,1,0:T(8,128)(2,1)S(1)}, bf16[3,2,128,256]{3,2,1,0:T(8,128)(2,1)S(1)}, u32[]{:S(2)}, u32[]{:S(2)}) collective-permute-start(bf16[3,2,128,256]{3,2,1,0:T(8,128)(2,1)S(1)} %collective-permute-done.6), channel_id=1, source_target_pairs={{0,240},{16,0},{32,16},{48,32},{64,48},{80,64},{96,80},{112,96},{1... | collective-permute-start | bytes 1179656 | tf_op jit(solution)/shard_map/ppermute | solution.py:39
  105.3 10.8 %collective-permute-start.14 = (bf16[3,2,128,256]{3,2,1,0:T(8,128)(2,1)S(1)}, bf16[3,2,128,256]{3,2,1,0:T(8,128)(2,1)S(1)}, u32[]{:S(2)}, u32[]{:S(2)}) collective-permute-start(bf16[3,2,128,256]{3,2,1,0:T(8,128)(2,1)S(1)} %collective-permute-done.13), channel_id=1, source_target_pairs={{0,16},{16,32},{32,48},{48,64},{64,80},{80,96},{96,112},{112,128},... | collective-permute-start | bytes 1179656 | tf_op jit(solution)/shard_map/ppermute | solution.py:38
  116.1 7.6 %collective-permute-start.15 = (bf16[3,1,128,256]{3,2,1,0:T(8,128)(2,1)S(1)}, bf16[3,1,128,256]{3,2,1,0:T(8,128)(2,1)S(1)}, u32[]{:S(2)}, u32[]{:S(2)}) collective-permute-start(bf16[3,1,128,256]{3,2,1,0:T(8,128)(2,1)S(1)} %slice.143), channel_id=1, source_target_pairs={{0,16},{16,32},{32,48},{48,64},{64,80},{80,96},{96,112},{112,128},... | collective-permute-start | bytes 589832 | tf_op jit(solution)/shard_map/ppermute | solution.py:42
  118.1 7.2 %collective-permute-start.16 = (bf16[3,1,128,256]{3,2,1,0:T(8,128)(2,1)S(1)}, bf16[3,1,128,256]{3,2,1,0:T(8,128)(2,1)S(1)}, u32[]{:S(2)}, u32[]{:S(2)}) collective-permute-start(bf16[3,1,128,256]{3,2,1,0:T(8,128)(2,1)S(1)} %slice.144), channel_id=1, source_target_pairs={{0,240},{16,0},{32,16},{48,32},{64,48},{80,64},{96,80},{112,96},{1... | collective-permute-start | bytes 589832 | tf_op jit(solution)/shard_map/ppermute | solution.py:43
  131.4 8.1 %copy-start.2 = (s32[1,16]{1,0:T(1,128)S(1)}, s32[1,16]{1,0:T(1,128)}, u32[]{:S(2)}) copy-start(s32[1,16]{1,0:T(1,128)} %param.16) | copy-start | bytes 196

commit v10 on v9

--- a/solution.py
+++ b/solution.py
@@ -57,7 +57,6 @@
     z_size = fsdp_size // 2
     channels = proj_weight.shape[2]
     block = proj_weight.shape[1]
-    weights = gather_weights(proj_weight, fsdp_size, z_size)
     values = activations.astype(jnp.float32)
     scaled = lax.rsqrt(jnp.mean(values * values, axis=1, keepdims=True) + EPSILON)
     normed = (values * scaled * norm_gain[None, :]).astype(jnp.bfloat16)
@@ -66,6 +65,8 @@
     doubled = jnp.concatenate([grid, grid], axis=2)
     rotated = lax.dynamic_slice_in_dim(doubled, z, z_size, axis=2).reshape(local_rows, model_width)
     spread = jnp.broadcast_to(rotated[None], (tp_size,) + rotated.shape)
+    spread, own_weights = lax.optimization_barrier((spread, proj_weight))
+    weights = gather_weights(own_weights, fsdp_size, z_size)
     slab_rows = lax.all_to_all(spread, "tp", 0, 0, tiled=False).reshape(
         tp_size * local_rows, model_width
     )

time: 162 us -> 162 us (level)
  waiting for transfers between devices: 31.2 us -> 27.9 us
  local copies, waits for them, and re-layouts: 16.9 us -> 18.8 us
    ppermute x7, waiting for transfers between devices: 7.39 us -> 0.02 us  [gather_weights(): right = lax.ppermute(right, 'fsdp', z_up)]
    ppermute x1, waiting for transfers between devices: 0.31 us -> 4.91 us  [gather_weights(): last_a = lax.ppermute(right[:, :1], 'fsdp', z_up)]
    unnamed x21 -> x47, local copies, waits for them, and re-layouts: 11.2 us -> 10.5 us
  transfers between devices with their start and end apart: 18 -> 18, of which waited for: 9 -> 8; matrix products, arithmetic and copies ran while one was open for 12% -> 11% of each run, Pallas kernels for 0% -> 0%
where the time goes in v10:
time: 162 us; the launch traced here: 161 us
  starting transfers between devices  79.7 us (49%)
  waiting for transfers between devices  27.9 us (17%)
  blocking collectives  19.5 us (12%)
  local copies, waits for them, and re-layouts  18.8 us (12%)
  matrix products  7.34 us (5%)
  other arithmetic  6.25 us (4%)
    ppermute x7, starting transfers between devices, gather_weights(): left = lax.ppermute(left, 'fsdp', z_down)  44.3 us
    ppermute x7, waiting for transfers between devices, gather_weights(): left = lax.ppermute(left, 'fsdp', z_down)  19.9 us
    all_to_all x1, blocking collectives, local(): gathered = lax.all_to_all(payload, 'tp', 0, 0, tiled=False)  19.5 us
    ppermute x7, starting transfers between devices, gather_weights(): right = lax.ppermute(right, 'fsdp', z_up)  13.4 us
    all_to_all x1, starting transfers between devices, local(): lax.all_to_all(spread, 'tp', 0, 0, tiled=False)  10.6 us
    unnamed x47, local copies, waits for them, and re-layouts  10.5 us
    dot_general x1, matrix products, local(): jnp.einsum('sk,ikc->isc', slab_rows, weights, preferred_element_type=jnp....  7.04 us
    ppermute x1, starting transfers between devices, gather_weights(): last_b = lax.ppermute(left[:, 1:], 'fsdp', z_down)  5.42 us
  transfers between devices with their start and end apart: 18, of which 8 were waited for; matrix products, arithmetic and copies ran while one was open for 11% of the time, Pallas kernels for 0%

profile of v10, /device:TPU:1, one launch (start us, length us, event | category | flops | bytes accessed | tf_op | source)
XLA Modules:
  0.0 160.7 jit_solution(10062698265948326582)
XLA Ops:
  3.3 2.6 %broadcast_in_dim.9 = bf16[16,32,4096]{2,1,0:T(8,128)(2,1)} broadcast(bf16[32,4096]{1,0:T(8,128)(2,1)S(1)} %bitcast.116), dimensions={1,2} | broadcast | bytes 4456448 | tf_op jit(solution)/shard_map/broadcast_in_dim | solution.py:67
  5.9 3.9 %collective-permute-start = (bf16[3,128,256]{2,1,0:T(8,128)(2,1)S(1)}, bf16[3,128,256]{2,1,0:T(8,128)(2,1)S(1)}, u32[]{:S(2)}, u32[]{:S(2)}) collective-permute-start(bf16[3,128,256]{2,1,0:T(8,128)(2,1)S(1)} %copy-done), channel_id=1, source_target_pairs={{0,256},{16,272},{32,288},{48,304},{64,320},{80,336},{96,352},{112... | collective-permute-start | bytes 589832 | tf_op jit(solution)/shard_map/ppermute | solution.py:29
  9.9 3.0 %collective-permute-done = bf16[3,128,256]{2,1,0:T(8,128)(2,1)S(1)} collective-permute-done((bf16[3,128,256]{2,1,0:T(8,128)(2,1)S(1)}, bf16[3,128,256]{2,1,0:T(8,128)(2,1)S(1)}, u32[]{:S(2)}, u32[]{:S(2)}) %collective-permute-start) | collective-permute-done | bytes 196640 | tf_op jit(solution)/shard_map/ppermute | solution.py:29
  13.0 12.6 %collective-permute-start.1 = (bf16[3,2,128,256]{3,2,1,0:T(8,128)(2,1)S(1)}, bf16[3,2,128,256]{3,2,1,0:T(8,128)(2,1)S(1)}, u32[]{:S(2)}, u32[]{:S(2)}) collective-permute-start(bf16[3,2,128,256]{3,2,1,0:T(8,128)(2,1)S(1)} %pad_maximum_fusion), channel_id=1, source_target_pairs={{0,240},{16,0},{32,16},{48,32},{64,48},{80,64},{96,80},{112,96},{1... | collective-permute-start | bytes 1179656 | tf_op jit(solution)/shard_map/ppermute | solution.py:39
  25.6 1.9 %collective-permute-start.8 = (bf16[3,2,128,256]{3,2,1,0:T(8,128)(2,1)S(1)}, bf16[3,2,128,256]{3,2,1,0:T(8,128)(2,1)S(1)}, u32[]{:S(2)}, u32[]{:S(2)}) collective-permute-start(bf16[3,2,128,256]{3,2,1,0:T(8,128)(2,1)S(1)} %pad_maximum_fusion), channel_id=1, source_target_pairs={{0,16},{16,32},{32,48},{48,64},{64,80},{80,96},{96,112},{112,128},... | collective-permute-start | bytes 1179656 | tf_op jit(solution)/shard_map/ppermute | solution.py:38
  27.5 4.9 %collective-permute-done.1 = bf16[3,2,128,256]{3,2,1,0:T(8,128)(2,1)S(1)} collective-permute-done((bf16[3,2,128,256]{3,2,1,0:T(8,128)(2,1)S(1)}, bf16[3,2,128,256]{3,2,1,0:T(8,128)(2,1)S(1)}, u32[]{:S(2)}, u32[]{:S(2)}) %collective-permute-start.1) | collective-permute-done | bytes 393248 | tf_op jit(solution)/shard_map/ppermute | solution.py:39
  32.4 5.3 %collective-permute-start.2 = (bf16[3,2,128,256]{3,2,1,0:T(8,128)(2,1)S(1)}, bf16[3,2,128,256]{3,2,1,0:T(8,128)(2,1)S(1)}, u32[]{:S(2)}, u32[]{:S(2)}) collective-permute-start(bf16[3,2,128,256]{3,2,1,0:T(8,128)(2,1)S(1)} %collective-permute-done.1), channel_id=1, source_target_pairs={{0,240},{16,0},{32,16},{48,32},{64,48},{80,64},{96,80},{112,96},{1... | collective-permute-start | bytes 1179656 | tf_op jit(solution)/shard_map/ppermute | solution.py:39
  37.8 1.9 %collective-permute-start.9 = (bf16[3,2,128,256]{3,2,1,0:T(8,128)(2,1)S(1)}, bf16[3,2,128,256]{3,2,1,0:T(8,128)(2,1)S(1)}, u32[]{:S(2)}, u32[]{:S(2)}) collective-permute-start(bf16[3,2,128,256]{3,2,1,0:T(8,128)(2,1)S(1)} %collective-permute-done.8), channel_id=1, source_target_pairs={{0,16},{16,32},{32,48},{48,64},{64,80},{80,96},{96,112},{112,128},... | collective-permute-start | bytes 1179656 | tf_op jit(solution)/shard_map/ppermute | solution.py:38
  39.7 4.0 %collective-permute-done.2 = bf16[3,2,128,256]{3,2,1,0:T(8,128)(2,1)S(1)} collective-permute-done((bf16[3,2,128,256]{3,2,1,0:T(8,128)(2,1)S(1)}, bf16[3,2,128,256]{3,2,1,0:T(8,128)(2,1)S(1)}, u32[]{:S(2)}, u32[]{:S(2)}) %collective-permute-start.2) | collective-permute-done | bytes 393248 | tf_op jit(solution)/shard_map/ppermute | solution.py:39
  43.7 5.3 %collective-permute-start.3 = (bf16[3,2,128,256]{3,2,1,0:T(8,128)(2,1)S(1)}, bf16[3,2,128,256]{3,2,1,0:T(8,128)(2,1)S(1)}, u32[]{:S(2)}, u32[]{:S(2)}) collective-permute-start(bf16[3,2,128,256]{3,2,1,0:T(8,128)(2,1)S(1)} %collective-permute-done.2), channel_id=1, source_target_pairs={{0,240},{16,0},{32,16},{48,32},{64,48},{80,64},{96,80},{112,96},{1... | collective-permute-start | bytes 1179656 | tf_op jit(solution)/shard_map/ppermute | solution.py:39
  49.0 1.9 %collective-permute-start.10 = (bf16[3,2,128,256]{3,2,1,0:T(8,128)(2,1)S(1)}, bf16[3,2,128,256]{3,2,1,0:T(8,128)(2,1)S(1)}, u32[]{:S(2)}, u32[]{:S(2)}) collective-permute-start(bf16[3,2,128,256]{3,2,1,0:T(8,128)(2,1)S(1)} %collective-permute-done.9), channel_id=1, source_target_pairs={{0,16},{16,32},{32,48},{48,64},{64,80},{80,96},{96,112},{112,128},... | collective-permute-start | bytes 1179656 | tf_op jit(solution)/shard_map/ppermute | solution.py:38
  50.9 10.6 %all-to-all-start = ((bf16[16,32,4096]{2,1,0:T(8,128)(2,1)}), bf16[16,32,4096]{2,1,0:T(8,128)(2,1)}, u32[]{:S(2)}, u32[]{:S(2)}) async-start(bf16[16,32,4096]{2,1,0:T(8,128)(2,1)} %broadcast_in_dim.9), calls=%async_computation | async-start | bytes 8388608 | tf_op jit(solution)/shard_map/all_to_all | solution.py:70
  61.5 4.9 %collective-permute-start.4 = (bf16[3,2,128,256]{3,2,1,0:T(8,128)(2,1)S(1)}, bf16[3,2,128,256]{3,2,1,0:T(8,128)(2,1)S(1)}, u32[]{:S(2)}, u32[]{:S(2)}) collective-permute-start(bf16[3,2,128,256]{3,2,1,0:T(8,128)(2,1)S(1)} %collective-permute-done.3), channel_id=1, source_target_pairs={{0,240},{16,0},{32,16},{48,32},{64,48},{80,64},{96,80},{112,96},{1... | collective-permute-start | bytes 1179656 | tf_op jit(solution)/shard_map/ppermute | solution.py:39
  74.8 5.4 %collective-permute-start.5 = (bf16[3,2,128,256]{3,2,1,0:T(8,128)(2,1)S(1)}, bf16[3,2,128,256]{3,2,1,0:T(8,128)(2,1)S(1)}, u32[]{:S(2)}, u32[]{:S(2)}) collective-permute-start(bf16[3,2,128,256]{3,2,1,0:T(8,128)(2,1)S(1)} %collective-permute-done.4), channel_id=1, source_target_pairs={{0,240},{16,0},{32,16},{48,32},{64,48},{80,64},{96,80},{112,96},{1... | collective-permute-start | bytes 1179656 | tf_op jit(solution)/shard_map/ppermute | solution.py:39
  83.7 4.0 %collective-permute-done.5 = bf16[3,2,128,256]{3,2,1,0:T(8,128)(2,1)S(1)} collective-permute-done((bf16[3,2,128,256]{3,2,1,0:T(8,128)(2,1)S(1)}, bf16[3,2,128,256]{3,2,1,0:T(8,128)(2,1)S(1)}, u32[]{:S(2)}, u32[]{:S(2)}) %collective-permute-start.5) | collective-permute-done | bytes 393248 | tf_op jit(solution)/shard_map/ppermute | solution.py:39
  87.7 5.4 %collective-permute-start.6 = (bf16[3,2,128,256]{3,2,1,0:T(8,128)(2,1)S(1)}, bf16[3,2,128,256]{3,2,1,0:T(8,128)(2,1)S(1)}, u32[]{:S(2)}, u32[]{:S(2)}) collective-permute-start(bf16[3,2,128,256]{3,2,1,0:T(8,128)(2,1)S(1)} %collective-permute-done.5), channel_id=1, source_target_pairs={{0,240},{16,0},{32,16},{48,32},{64,48},{80,64},{96,80},{112,96},{1... | collective-permute-start | bytes 1179656 | tf_op jit(solution)/shard_map/ppermute | solution.py:39
  93.2 1.9 %collective-permute-start.13 = (bf16[3,2,128,256]{3,2,1,0:T(8,128)(2,1)S(1)}, bf16[3,2,128,256]{3,2,1,0:T(8,128)(2,1)S(1)}, u32[]{:S(2)}, u32[]{:S(2)}) collective-permute-start(bf16[3,2,128,256]{3,2,1,0:T(8,128)(2,1)S(1)} %collective-permute-done.12), channel_id=1, source_target_pairs={{0,16},{16,32},{32,48},{48,64},{64,80},{80,96},{96,112},{112,128},... | collective-permute-start | bytes 1179656 | tf_op jit(solution)/shard_map/ppermute | solution.py:38
  96.7 3.2 %collective-permute-done.6 = bf16[3,2,128,256]{3,2,1,0:T(8,128)(2,1)S(1)} collective-permute-done((bf16[3,2,128,256]{3,2,1,0:T(8,128)(2,1)S(1)}, bf16[3,2,128,256]{3,2,1,0:T(8,128)(2,1)S(1)}, u32[]{:S(2)}, u32[]{:S(2)}) %collective-permute-start.6) | collective-permute-done | bytes 393248 | tf_op jit(solution)/shard_map/ppermute | solution.py:39
  99.9 5.4 %collective-permute-start.7 = (bf16[3,2,128,256]{3,2,1,0:T(8,128)(2,1)S(1)}, bf16[3,2,128,256]{3,2,1,0:T(8,128)(2,1)S(1)}, u32[]{:S(2)}, u32[]{:S(2)}) collective-permute-start(bf16[3,2,128,256]{3,2,1,0:T(8,128)(2,1)S(1)} %collective-permute-done.6), channel_id=1, source_target_pairs={{0,240},{16,0},{32,16},{48,32},{64,48},{80,64},{96,80},{112,96},{1... | collective-permute-start | bytes 1179656 | tf_op jit(solution)/shard_map/ppermute | solution.py:39
  108.8 2.4 %collective-permute-done.7 = bf16[3,2,128,256]{3,2,1,0:T(8,128)(2,1)S(1)} collective-permute-done((bf16[3,2,128,256]{3,2,1,0:T(8,128)(2,1)S(1)}, bf16[3,2,128,256]{3,2,1,0:T(8,128)(2,1)S(1)}, u32[]{:S(2)}, u32[]{:S(2)}) %collective-permute-start.7) | collective-permute-done | bytes 393248 | tf_op jit(solution)/shard_map/ppermute | solution.py:39
  111.2 5.4 %collective-permute-start.16 = (bf16[3,1,128,256]{3,2,1,0:T(8,128)(2,1)S(1)}, bf16[3,1,128,256]{3,2,1,0:T(8,128)(2,1)S(1)}, u32[]{:S(2)}, u32[]{:S(2)}) collective-permute-start(bf16[3,1,128,256]{3,2,1,0:T(8,128)(2,1)S(1)} %slice.144), channel_id=1, source_target_pairs={{0,240},{16,0},{32,16},{48,32},{64,48},{80,64},{96,80},{112,96},{1... | collective-permute-start | bytes 589832 | tf_op jit(solution)/shard_map/ppermute | solution.py:43
  119.4 4.9 %collective-permute-done.15 = bf16[3,1,128,256]{3,2,1,0:T(8,128)(2,1)S(1)} collective-permute-done((bf16[3,1,128,256]{3,2,1,0:T(8,128)(2,1)S(1)}, bf16[3,1,128,256]{3,2,1,0:T(8,128)(2,1)S(1)}, u32[]{:S(2)}, u32[]{:S(2)}) %collective-permute-start.15) | collective-permute-done | bytes 196640 | tf_op jit(solution)/shard_map/ppermute | solution.py:42
  130.8 7.0 %convolution_bitcast_fusion = f32[3,512,256]{2,1,0:T(8,128)S(1)} fusion(bf16[512,4096,1]{1,0,2:T(8,128)(2,1)} %bitcast.36, bf16[3,4096,256]{2,1,0:T(8,128)(2,1)} %bitcast.34), kind=kOutput, calls=%fused_computation | convolution fusion | flops 3221225472 | bytes 12058624 | tf_op jit(solution)/shard_map/sk,ikc->isc/dot_general | solution.py:73
  139.5 19.5 %all_to_all.10 = bf16[16,80,128]{2,1,0:T(8,128)(2,1)S(1)} all-to-all(bf16[16,80,128]{2,1,0:T(8,128)(2,1)S(1)} %pad_maximum_fusion.1), channel_id=1, replica_groups=mesh['fsdp'=32,'tp'=16] {'tp'}, dimensions={0} | all-to-all | bytes 655360 | tf_op jit(solution)/shard_map/all_to_all | solution.py:102
  (93 shorter events, 31.9 us)
Async XLA Ops:
  3.3 65.0 %copy-start.13 = (s32[1,512]{1,0:T(1,128)S(1)}, s32[1,512]{1,0:T(1,128)}, u32[]{:S(2)}) copy-start(s32[1,512]{1,0:T(1,128)} %param.15) | copy-start | bytes 6148
  3.3 65.7 %copy-start.12 = (f32[16,7]{0,1:T(8,128)S(1)}, f32[16,7]{0,1:T(8,128)}, u32[]{:S(2)}) copy-start(f32[16,7]{0,1:T(8,128)} %param.14) | copy-start | bytes 1348
  5.9 7.0 %collective-permute-start = (bf16[3,128,256]{2,1,0:T(8,128)(2,1)S(1)}, bf16[3,128,256]{2,1,0:T(8,128)(2,1)S(1)}, u32[]{:S(2)}, u32[]{:S(2)}) collective-permute-start(bf16[3,128,256]{2,1,0:T(8,128)(2,1)S(1)} %copy-done), channel_id=1, source_target_pairs={{0,256},{16,272},{32,288},{48,304},{64,320},{80,336},{96,352},{112... | collective-permute-start | bytes 589832 | tf_op jit(solution)/shard_map/ppermute | solution.py:29
  13.0 19.5 %collective-permute-start.1 = (bf16[3,2,128,256]{3,2,1,0:T(8,128)(2,1)S(1)}, bf16[3,2,128,256]{3,2,1,0:T(8,128)(2,1)S(1)}, u32[]{:S(2)}, u32[]{:S(2)}) collective-permute-start(bf16[3,2,128,256]{3,2,1,0:T(8,128)(2,1)S(1)} %pad_maximum_fusion), channel_id=1, source_target_pairs={{0,240},{16,0},{32,16},{48,32},{64,48},{80,64},{96,80},{112,96},{1... | collective-permute-start | bytes 1179656 | tf_op jit(solution)/shard_map/ppermute | solution.py:39
  25.6 12.2 %collective-permute-start.8 = (bf16[3,2,128,256]{3,2,1,0:T(8,128)(2,1)S(1)}, bf16[3,2,128,256]{3,2,1,0:T(8,128)(2,1)S(1)}, u32[]{:S(2)}, u32[]{:S(2)}) collective-permute-start(bf16[3,2,128,256]{3,2,1,0:T(8,128)(2,1)S(1)} %pad_maximum_fusion), channel_id=1, source_target_pairs={{0,16},{16,32},{32,48},{48,64},{64,80},{80,96},{96,112},{112,128},... | collective-permute-start | bytes 1179656 | tf_op jit(solution)/shard_map/ppermute | solution.py:38
  32.4 11.2 %collective-permute-start.2 = (bf16[3,2,128,256]{3,2,1,0:T(8,128)(2,1)S(1)}, bf16[3,2,128,256]{3,2,1,0:T(8,128)(2,1)S(1)}, u32[]{:S(2)}, u32[]{:S(2)}) collective-permute-start(bf16[3,2,128,256]{3,2,1,0:T(8,128)(2,1)S(1)} %collective-permute-done.1), channel_id=1, source_target_pairs={{0,240},{16,0},{32,16},{48,32},{64,48},{80,64},{96,80},{112,96},{1... | collective-permute-start | bytes 1179656 | tf_op jit(solution)/shard_map/ppermute | solution.py:39
  37.8 11.2 %collective-permute-start.9 = (bf16[3,2,128,256]{3,2,1,0:T(8,128)(2,1)S(1)}, bf16[3,2,128,256]{3,2,1,0:T(8,128)(2,1)S(1)}, u32[]{:S(2)}, u32[]{:S(2)}) collective-permute-start(bf16[3,2,128,256]{3,2,1,0:T(8,128)(2,1)S(1)} %collective-permute-done.8), channel_id=1, source_target_pairs={{0,16},{16,32},{32,48},{48,64},{64,80},{80,96},{96,112},{112,128},... | collective-permute-start | bytes 1179656 | tf_op jit(solution)/shard_map/ppermute | solution.py:38
  43.7 17.9 %collective-permute-start.3 = (bf16[3,2,128,256]{3,2,1,0:T(8,128)(2,1)S(1)}, bf16[3,2,128,256]{3,2,1,0:T(8,128)(2,1)S(1)}, u32[]{:S(2)}, u32[]{:S(2)}) collective-permute-start(bf16[3,2,128,256]{3,2,1,0:T(8,128)(2,1)S(1)} %collective-permute-done.2), channel_id=1, source_target_pairs={{0,240},{16,0},{32,16},{48,32},{64,48},{80,64},{96,80},{112,96},{1... | collective-permute-start | bytes 1179656 | tf_op jit(solution)/shard_map/ppermute | solution.py:39
  49.0 17.4 %collective-permute-start.10 = (bf16[3,2,128,256]{3,2,1,0:T(8,128)(2,1)S(1)}, bf16[3,2,128,256]{3,2,1,0:T(8,128)(2,1)S(1)}, u32[]{:S(2)}, u32[]{:S(2)}) collective-permute-start(bf16[3,2,128,256]{3,2,1,0:T(8,128)(2,1)S(1)} %collective-permute-done.9), channel_id=1, source_target_pairs={{0,16},{16,32},{32,48},{48,64},{64,80},{80,96},{96,112},{112,128},... | collective-permute-start | bytes 1179656 | tf_op jit(solution)/shard_map/ppermute | solution.py:38
  50.9 79.8 %all-to-all-start = ((bf16[16,32,4096]{2,1,0:T(8,128)(2,1)}), bf16[16,32,4096]{2,1,0:T(8,128)(2,1)}, u32[]{:S(2)}, u32[]{:S(2)}) async-start(bf16[16,32,4096]{2,1,0:T(8,128)(2,1)} %broadcast_in_dim.9), calls=%async_computation | async-start | bytes 8388608 | tf_op jit(solution)/shard_map/all_to_all | solution.py:70
  61.5 13.2 %collective-permute-start.4 = (bf16[3,2,128,256]{3,2,1,0:T(8,128)(2,1)S(1)}, bf16[3,2,128,256]{3,2,1,0:T(8,128)(2,1)S(1)}, u32[]{:S(2)}, u32[]{:S(2)}) collective-permute-start(bf16[3,2,128,256]{3,2,1,0:T(8,128)(2,1)S(1)} %collective-permute-done.3), channel_id=1, source_target_pairs={{0,240},{16,0},{32,16},{48,32},{64,48},{80,64},{96,80},{112,96},{1... | collective-permute-start | bytes 1179656 | tf_op jit(solution)/shard_map/ppermute | solution.py:39
  66.4 13.8 %collective-permute-start.11 = (bf16[3,2,128,256]{3,2,1,0:T(8,128)(2,1)S(1)}, bf16[3,2,128,256]{3,2,1,0:T(8,128)(2,1)S(1)}, u32[]{:S(2)}, u32[]{:S(2)}) collective-permute-start(bf16[3,2,128,256]{3,2,1,0:T(8,128)(2,1)S(1)} %collective-permute-done.10), channel_id=1, source_target_pairs={{0,16},{16,32},{32,48},{48,64},{64,80},{80,96},{96,112},{112,128},... | collective-permute-start | bytes 1179656 | tf_op jit(solution)/shard_map/ppermute | solution.py:38
  74.8 13.0 %collective-permute-start.5 = (bf16[3,2,128,256]{3,2,1,0:T(8,128)(2,1)S(1)}, bf16[3,2,128,256]{3,2,1,0:T(8,128)(2,1)S(1)}, u32[]{:S(2)}, u32[]{:S(2)}) collective-permute-start(bf16[3,2,128,256]{3,2,1,0:T(8,128)(2,1)S(1)} %collective-permute-done.4), channel_id=1, source_target_pairs={{0,240},{16,0},{32,16},{48,32},{64,48},{80,64},{96,80},{112,96},{1... | collective-permute-start | bytes 1179656 | tf_op jit(solution)/shard_map/ppermute | solution.py:39
  80.2 13.0 %collective-permute-start.12 = (bf16[3,2,128,256]{3,2,1,0:T(8,128)(2,1)S(1)}, bf16[3,2,128,256]{3,2,1,0:T(8,128)(2,1)S(1)}, u32[]{:S(2)}, u32[]{:S(2)}) collective-permute-start(bf16[3,2,128,256]{3,2,1,0:T(8,128)(2,1)S(1)} %collective-permute-done.11), channel_id=1, source_target_pairs={{0,16},{16,32},{32,48},{48,64},{64,80},{80,96},{96,112},{112,128},... | collective-permute-start | bytes 1179656 | tf_op jit(solution)/shard_map/ppermute | solution.py:38
  87.7 12.2 %collective-permute-start.6 = (bf16[3,2,128,256]{3,2,1,0:T(8,128)(2,1)S(1)}, bf16[3,2,128,256]{3,2,1,0:T(8,128)(2,1)S(1)}, u32[]{:S(2)}, u32[]{:S(2)}) collective-permute-start(bf16[3,2,128,256]{3,2,1,0:T(8,128)(2,1)S(1)} %collective-permute-done.5), channel_id=1, source_target_pairs={{0,240},{16,0},{32,16},{48,32},{64,48},{80,64},{96,80},{112,96},{1... | collective-permute-start | bytes 1179656 | tf_op jit(solution)/shard_map/ppermute | solution.py:39
  93.2 12.1 %collective-permute-start.13 = (bf16[3,2,128,256]{3,2,1,0:T(8,128)(2,1)S(1)}, bf16[3,2,128,256]{3,2,1,0:T(8,128)(2,1)S(1)}, u32[]{:S(2)}, u32[]{:S(2)}) collective-permute-start(bf16[3,2,128,256]{3,2,1,0:T(8,128)(2,1)S(1)} %collective-permute-done.12), channel_id=1, source_target_pairs={{0,16},{16,32},{32,48},{48,64},{64,80},{80,96},{96,112},{112,128},... | collective-permute-start | bytes 1179656 | tf_op jit(solution)/shard_map/ppermute | solution.py:38
  99.9 11.3 %collective-permute-start.7 = (bf16[3,2,128,256]{3,2,1,0:T(8,128)(2,1)S(1)}, bf16[3,2,128,256]{3,2,1,0:T(8,128)(2,1)S(1)}, u32[]{:S(2)}, u32[]{:S(2)}) collective-permute-start(bf16[3,2,128,256]{3,2,1,0:T(8,128)(2,1)S(1)} %collective-permute-done.6), channel_id=1, source_target_pairs={{0,240},{16,0},{32,16},{48,32},{64,48},{80,64},{96,80},{112,96},{1... | collective-permute-start | bytes 1179656 | tf_op jit(solution)/shard_map/ppermute | solution.py:39
  105.3 11.4 %collective-permute-start.14 = (bf16[3,2,128,256]{3,2,1,0:T(8,128)(2,1)S(1)}, bf16[3,2,128,256]{3,2,1,0:T(8,128)(2,1)S(1)}, u32[]{:S(2)}, u32[]{:S(2)}) collective-permute-start(bf16[3,2,128,256]{3,2,1,0:T(8,128)(2,1)S(1)} %collective-permute-done.13), channel_id=1, source_target_pairs={{0,16},{16,32},{32,48},{48,64},{64,80},{80,96},{96,112},{112,128},... | collective-permute-start | bytes 1179656 | tf_op jit(solution)/shard_map/ppermute | solution.py:38
  111.2 8.2 %collective-permute-start.16 = (bf16[3,1,128,256]{3,2,1,0:T(8,128)(2,1)S(1)}, bf16[3,1,128,256]{3,2,1,0:T(8,128)(2,1)S(1)}, u32[]{:S(2)}, u32[]{:S(2)}) collective-permute-start(bf16[3,1,128,256]{3,2,1,0:T(8,128)(2,1)S(1)} %slice.144), channel_id=1, source_target_pairs={{0,240},{16,0},{32,16},{48,32},{64,48},{80,64},{96,80},{112,96},{1... | collective-permute-start | bytes 589832 | tf_op jit(solution)/shard_map/ppermute | solution.py:43
  116.7 7.6 %collective-permute-start.15 = (bf16[3,1,128,256]{3,2,1,0:T(8,128)(2,1)S(1)}, bf16[3,1,128,256]{3,2,1,0:T(8,128)(2,1)S(1)}, u32[]{:S(2)}, u32[]{:S(2)}) collective-permute-start(bf16[3,1,128,256]{3,2,1,0:T(8,128)(2,1)S(1)} %slice.143), channel_id=1, source_target_pairs={{0,16},{16,32},{32,48},{48,64},{64,80},{80,96},{96,112},{112,128},... | collective-permute-start | bytes 589832 | tf_op jit(solution)/shard_map/ppermute | solution.py:42
  130.7 7.3 %copy-start.4 = (f32[512]{0:T(512)S(1)}, f32[512]{0:T(512)}, u32[]{:S(2)}) copy-start(f32[512]{0:T(512)} %get-tuple-element.44) | copy-start | bytes 6148
  130.7 7.3 %copy-start.5 = (f32[256,1]{0,1:T(1,128)S(1)}, f32[256,1]{0,1:T(1,128)}, u32[]{:S(2)}) copy-start(f32[256,1]{0,1:T(1,128)} %get-tuple-element.32) | copy-start | bytes 3076
  130.8 8.1 %copy-start.14 = (f32[256]{0:T(256)S(1)}, f32[256]{0:T(256)}, u32[]{:S(2)}) copy-start(f32[256]{0:T(256)} %dynamic_slice.7) | copy-start | bytes 3076
  130.8 8.1 %copy-start.15 = (s32[1,16]{1,0:T(1,128)S(1)}, s32[1,16]{1,0:T(1,128)}, u32[]{:S(2)}) copy-start(s32[1,16]{1,0:T(1,128)} %param.16) | copy-start | bytes 196
  (10 other events, 70.6 us)

commit v11 on v6

--- a/solution.py
+++ b/solution.py
@@ -82,9 +82,11 @@
         proj_weight, fsdp_size, z_size, slab_rows
     )
     split = early_weights.shape[1]
-    projected = jnp.einsum(
+    early = jnp.einsum(
         "sk,ikc->isc", slab_rows[:, :split], early_weights, preferred_element_type=jnp.float32
-    ) + jnp.einsum(
+    )
+    early = lax.optimization_barrier(early)
+    projected = early + jnp.einsum(
         "sk,ikc->isc", slab_rows[:, split:], last_weights, preferred_element_type=jnp.float32
     )
     projected = with_layout_constraint(projected, Layout((0, 1, 2)))
@@ -104,20 +106,25 @@
     rounded = lax.reduce_precision(partial_sum, exponent_bits=8, mantissa_bits=7)
     high = rounded.astype(jnp.bfloat16)
     low = (partial_sum - rounded).astype(jnp.bfloat16)
+    lanes = 128
     extra_rows = 16
-    extra = jnp.zeros((extra_rows, channels), jnp.bfloat16)
+    extra = jnp.zeros((extra_rows, lanes), jnp.bfloat16)
     extra = extra.at[0, : high.shape[0]].set(high).at[1, : low.shape[0]].set(low)
-    blocks = mixed_local.reshape(tp_size, local_rows, channels)
+    pieces = channels // lanes
+    blocks = jnp.transpose(
+        mixed_local.reshape(tp_size, local_rows, pieces, lanes), (0, 2, 1, 3)
+    ).reshape(tp_size, pieces * local_rows, lanes)
     payload = jnp.concatenate(
-        [blocks, jnp.broadcast_to(extra[None], (tp_size, extra_rows, channels))], axis=1
+        [blocks, jnp.broadcast_to(extra[None], (tp_size, extra_rows, lanes))], axis=1
     )
     gathered = lax.all_to_all(payload, "tp", 0, 0, tiled=False)
-    own_rows = jnp.transpose(gathered[:, :local_rows], (1, 0, 2)).reshape(
-        local_rows, tp_size * channels
-    )
+    own_rows = jnp.transpose(
+        gathered[:, : pieces * local_rows].reshape(tp_size, pieces, local_rows, lanes), (2, 0, 1, 3)
+    ).reshape(local_rows, tp_size * channels)
+    data_rows = pieces * local_rows
     count = positions.shape[0]
-    received = gathered[:, local_rows, :count].astype(jnp.float32) + gathered[
-        :, local_rows + 1, :count
+    received = gathered[:, data_rows, :count].astype(jnp.float32) + gathered[
+        :, data_rows + 1, :count
     ].astype(jnp.float32)
     needle_score = (jnp.sum(received, axis=0) / math.sqrt(model_width))[None, :]
     return (own_rows, needle_score)

time: 163 us -> 160 us (0.982)
    ppermute x1, starting transfers between devices: 4.57 us -> 1.91 us  [gather_weights(): last_b = lax.ppermute(sent_b, 'fsdp', z_down)]
    unnamed x21 -> x20, local copies, waits for them, and re-layouts: 12.3 us -> 12.2 us
  transfers between devices with their start and end apart: 18 -> 18, of which waited for: 9 -> 7; matrix products, arithmetic and copies ran while one was open for 13% -> 18% of each run, Pallas kernels for 0% -> 0%
where the time goes in v11:
time: 160 us; the launch traced here: 159 us
  starting transfers between devices  77.5 us (48%)
  waiting for transfers between devices  28 us (18%)
  blocking collectives  19.2 us (12%)
  local copies, waits for them, and re-layouts  18.3 us (11%)
  matrix products  8.69 us (5%)
  other arithmetic  6.64 us (4%)
    ppermute x7, starting transfers between devices, gather_weights(): left = lax.ppermute(left, 'fsdp', z_down)  44.2 us
    all_to_all x1, blocking collectives, local(): gathered = lax.all_to_all(payload, 'tp', 0, 0, tiled=False)  19.2 us
    ppermute x7, waiting for transfers between devices, gather_weights(): left = lax.ppermute(left, 'fsdp', z_down)  17.4 us
    ppermute x7, starting transfers between devices, gather_weights(): right = lax.ppermute(right, 'fsdp', z_up)  13.4 us
    unnamed x20, local copies, waits for them, and re-layouts  12.2 us
    all_to_all x1, starting transfers between devices, local(): lax.all_to_all(spread, 'tp', 0, 0, tiled=False)  10.6 us
    ppermute x7, waiting for transfers between devices, gather_weights(): right = lax.ppermute(right, 'fsdp', z_up)  7.35 us
    dot_general x1, matrix products, local(): jnp.einsum('sk,ikc->isc', slab_rows[:, :split], early_weights, preferred_...  7.07 us
  transfers between devices with their start and end apart: 18, of which 7 were waited for; matrix products, arithmetic and copies ran while one was open for 18% of the time, Pallas kernels for 0%

profile of v11, /device:TPU:1, one launch (start us, length us, event | category | flops | bytes accessed | tf_op | source)
XLA Modules:
  0.0 159.5 jit_solution(15517675280936666488)
XLA Ops:
  0.6 3.9 %collective-permute-start = (bf16[3,128,256]{2,1,0:T(8,128)(2,1)}, bf16[3,128,256]{2,1,0:T(8,128)(2,1)S(1)}, u32[]{:S(2)}, u32[]{:S(2)}) collective-permute-start(bf16[3,128,256]{2,1,0:T(8,128)(2,1)} %param.13), channel_id=1, source_target_pairs={{0,256},{16,272},{32,288},{48,304},{64,320},{80,336},{96,352},{112... | collective-permute-start | bytes 589832 | tf_op jit(solution)/shard_map/ppermute | solution.py:29
  4.6 3.2 %collective-permute-done = bf16[3,128,256]{2,1,0:T(8,128)(2,1)S(1)} collective-permute-done((bf16[3,128,256]{2,1,0:T(8,128)(2,1)}, bf16[3,128,256]{2,1,0:T(8,128)(2,1)S(1)}, u32[]{:S(2)}, u32[]{:S(2)}) %collective-permute-start) | collective-permute-done | bytes 196640 | tf_op jit(solution)/shard_map/ppermute | solution.py:29
  8.8 12.6 %collective-permute-start.1 = (bf16[3,2,128,256]{3,2,1,0:T(8,128)(2,1)S(1)}, bf16[3,2,128,256]{3,2,1,0:T(8,128)(2,1)S(1)}, u32[]{:S(2)}, u32[]{:S(2)}) collective-permute-start(bf16[3,2,128,256]{3,2,1,0:T(8,128)(2,1)S(1)} %pad_maximum_fusion), channel_id=1, source_target_pairs={{0,240},{16,0},{32,16},{48,32},{64,48},{80,64},{96,80},{112,96},{1... | collective-permute-start | bytes 1179656 | tf_op jit(solution)/shard_map/ppermute | solution.py:39
  21.5 1.9 %collective-permute-start.8 = (bf16[3,2,128,256]{3,2,1,0:T(8,128)(2,1)S(1)}, bf16[3,2,128,256]{3,2,1,0:T(8,128)(2,1)S(1)}, u32[]{:S(2)}, u32[]{:S(2)}) collective-permute-start(bf16[3,2,128,256]{3,2,1,0:T(8,128)(2,1)S(1)} %pad_maximum_fusion), channel_id=1, source_target_pairs={{0,16},{16,32},{32,48},{48,64},{64,80},{80,96},{96,112},{112,128},... | collective-permute-start | bytes 1179656 | tf_op jit(solution)/shard_map/ppermute | solution.py:38
  24.5 3.8 %collective-permute-done.1 = bf16[3,2,128,256]{3,2,1,0:T(8,128)(2,1)S(1)} collective-permute-done((bf16[3,2,128,256]{3,2,1,0:T(8,128)(2,1)S(1)}, bf16[3,2,128,256]{3,2,1,0:T(8,128)(2,1)S(1)}, u32[]{:S(2)}, u32[]{:S(2)}) %collective-permute-start.1) | collective-permute-done | bytes 393248 | tf_op jit(solution)/shard_map/ppermute | solution.py:39
  28.3 5.3 %collective-permute-start.2 = (bf16[3,2,128,256]{3,2,1,0:T(8,128)(2,1)S(1)}, bf16[3,2,128,256]{3,2,1,0:T(8,128)(2,1)S(1)}, u32[]{:S(2)}, u32[]{:S(2)}) collective-permute-start(bf16[3,2,128,256]{3,2,1,0:T(8,128)(2,1)S(1)} %collective-permute-done.1), channel_id=1, source_target_pairs={{0,240},{16,0},{32,16},{48,32},{64,48},{80,64},{96,80},{112,96},{1... | collective-permute-start | bytes 1179656 | tf_op jit(solution)/shard_map/ppermute | solution.py:39
  33.6 1.9 %collective-permute-start.9 = (bf16[3,2,128,256]{3,2,1,0:T(8,128)(2,1)S(1)}, bf16[3,2,128,256]{3,2,1,0:T(8,128)(2,1)S(1)}, u32[]{:S(2)}, u32[]{:S(2)}) collective-permute-start(bf16[3,2,128,256]{3,2,1,0:T(8,128)(2,1)S(1)} %collective-permute-done.8), channel_id=1, source_target_pairs={{0,16},{16,32},{32,48},{48,64},{64,80},{80,96},{96,112},{112,128},... | collective-permute-start | bytes 1179656 | tf_op jit(solution)/shard_map/ppermute | solution.py:38
  36.9 2.6 %collective-permute-done.2 = bf16[3,2,128,256]{3,2,1,0:T(8,128)(2,1)S(1)} collective-permute-done((bf16[3,2,128,256]{3,2,1,0:T(8,128)(2,1)S(1)}, bf16[3,2,128,256]{3,2,1,0:T(8,128)(2,1)S(1)}, u32[]{:S(2)}, u32[]{:S(2)}) %collective-permute-start.2) | collective-permute-done | bytes 393248 | tf_op jit(solution)/shard_map/ppermute | solution.py:39
  39.5 5.3 %collective-permute-start.3 = (bf16[3,2,128,256]{3,2,1,0:T(8,128)(2,1)S(1)}, bf16[3,2,128,256]{3,2,1,0:T(8,128)(2,1)S(1)}, u32[]{:S(2)}, u32[]{:S(2)}) collective-permute-start(bf16[3,2,128,256]{3,2,1,0:T(8,128)(2,1)S(1)} %collective-permute-done.2), channel_id=1, source_target_pairs={{0,240},{16,0},{32,16},{48,32},{64,48},{80,64},{96,80},{112,96},{1... | collective-permute-start | bytes 1179656 | tf_op jit(solution)/shard_map/ppermute | solution.py:39
  44.9 1.9 %collective-permute-start.10 = (bf16[3,2,128,256]{3,2,1,0:T(8,128)(2,1)S(1)}, bf16[3,2,128,256]{3,2,1,0:T(8,128)(2,1)S(1)}, u32[]{:S(2)}, u32[]{:S(2)}) collective-permute-start(bf16[3,2,128,256]{3,2,1,0:T(8,128)(2,1)S(1)} %collective-permute-done.9), channel_id=1, source_target_pairs={{0,16},{16,32},{32,48},{48,64},{64,80},{80,96},{96,112},{112,128},... | collective-permute-start | bytes 1179656 | tf_op jit(solution)/shard_map/ppermute | solution.py:38
  48.1 2.6 %broadcast_in_dim.9 = bf16[16,32,4096]{2,1,0:T(8,128)(2,1)} broadcast(bf16[32,4096]{1,0:T(8,128)(2,1)S(1)} %broadcast_in_dim.8), dimensions={1,2} | broadcast | bytes 4456448 | tf_op jit(solution)/shard_map/broadcast_in_dim | solution.py:77
  50.7 10.6 %all-to-all-start = ((bf16[16,32,4096]{2,1,0:T(8,128)(2,1)}), bf16[16,32,4096]{2,1,0:T(8,128)(2,1)}, u32[]{:S(2)}, u32[]{:S(2)}) async-start(bf16[16,32,4096]{2,1,0:T(8,128)(2,1)} %broadcast_in_dim.9), calls=%async_computation | async-start | bytes 8388608 | tf_op jit(solution)/shard_map/all_to_all | solution.py:78
  61.3 4.9 %collective-permute-start.4 = (bf16[3,2,128,256]{3,2,1,0:T(8,128)(2,1)S(1)}, bf16[3,2,128,256]{3,2,1,0:T(8,128)(2,1)}, u32[]{:S(2)}, u32[]{:S(2)}) collective-permute-start(bf16[3,2,128,256]{3,2,1,0:T(8,128)(2,1)S(1)} %collective-permute-done.3), channel_id=1, source_target_pairs={{0,240},{16,0},{32,16},{48,32},{64,48},{80,64},{96,80},{112,96},{1... | collective-permute-start | bytes 1179656 | tf_op jit(solution)/shard_map/ppermute | solution.py:39
  66.2 1.9 %collective-permute-start.11 = (bf16[3,2,128,256]{3,2,1,0:T(8,128)(2,1)S(1)}, bf16[3,2,128,256]{3,2,1,0:T(8,128)(2,1)}, u32[]{:S(2)}, u32[]{:S(2)}) collective-permute-start(bf16[3,2,128,256]{3,2,1,0:T(8,128)(2,1)S(1)} %collective-permute-done.10), channel_id=1, source_target_pairs={{0,16},{16,32},{32,48},{48,64},{64,80},{80,96},{96,112},{112,128},... | collective-permute-start | bytes 1179656 | tf_op jit(solution)/shard_map/ppermute | solution.py:38
  69.9 4.6 %collective-permute-done.4 = bf16[3,2,128,256]{3,2,1,0:T(8,128)(2,1)} collective-permute-done((bf16[3,2,128,256]{3,2,1,0:T(8,128)(2,1)S(1)}, bf16[3,2,128,256]{3,2,1,0:T(8,128)(2,1)}, u32[]{:S(2)}, u32[]{:S(2)}) %collective-permute-start.4) | collective-permute-done | bytes 393248 | tf_op jit(solution)/shard_map/ppermute | solution.py:39
  74.5 5.4 %collective-permute-start.5 = (bf16[3,2,128,256]{3,2,1,0:T(8,128)(2,1)}, bf16[3,2,128,256]{3,2,1,0:T(8,128)(2,1)S(1)}, u32[]{:S(2)}, u32[]{:S(2)}) collective-permute-start(bf16[3,2,128,256]{3,2,1,0:T(8,128)(2,1)} %collective-permute-done.4), channel_id=1, source_target_pairs={{0,240},{16,0},{32,16},{48,32},{64,48},{80,64},{96,80},{112,96},{1... | collective-permute-start | bytes 1179656 | tf_op jit(solution)/shard_map/ppermute | solution.py:39
  83.4 4.3 %collective-permute-done.5 = bf16[3,2,128,256]{3,2,1,0:T(8,128)(2,1)S(1)} collective-permute-done((bf16[3,2,128,256]{3,2,1,0:T(8,128)(2,1)}, bf16[3,2,128,256]{3,2,1,0:T(8,128)(2,1)S(1)}, u32[]{:S(2)}, u32[]{:S(2)}) %collective-permute-start.5) | collective-permute-done | bytes 393248 | tf_op jit(solution)/shard_map/ppermute | solution.py:39
  87.7 5.3 %collective-permute-start.6 = (bf16[3,2,128,256]{3,2,1,0:T(8,128)(2,1)S(1)}, bf16[3,2,128,256]{3,2,1,0:T(8,128)(2,1)S(1)}, u32[]{:S(2)}, u32[]{:S(2)}) collective-permute-start(bf16[3,2,128,256]{3,2,1,0:T(8,128)(2,1)S(1)} %collective-permute-done.5), channel_id=1, source_target_pairs={{0,240},{16,0},{32,16},{48,32},{64,48},{80,64},{96,80},{112,96},{1... | collective-permute-start | bytes 1179656 | tf_op jit(solution)/shard_map/ppermute | solution.py:39
  97.5 2.1 %collective-permute-done.6 = bf16[3,2,128,256]{3,2,1,0:T(8,128)(2,1)S(1)} collective-permute-done((bf16[3,2,128,256]{3,2,1,0:T(8,128)(2,1)S(1)}, bf16[3,2,128,256]{3,2,1,0:T(8,128)(2,1)S(1)}, u32[]{:S(2)}, u32[]{:S(2)}) %collective-permute-start.6) | collective-permute-done | bytes 393248 | tf_op jit(solution)/shard_map/ppermute | solution.py:39
  99.6 5.4 %collective-permute-start.7 = (bf16[3,2,128,256]{3,2,1,0:T(8,128)(2,1)S(1)}, bf16[3,2,128,256]{3,2,1,0:T(8,128)(2,1)S(1)}, u32[]{:S(2)}, u32[]{:S(2)}) collective-permute-start(bf16[3,2,128,256]{3,2,1,0:T(8,128)(2,1)S(1)} %collective-permute-done.6), channel_id=1, source_target_pairs={{0,240},{16,0},{32,16},{48,32},{64,48},{80,64},{96,80},{112,96},{1... | collective-permute-start | bytes 1179656 | tf_op jit(solution)/shard_map/ppermute | solution.py:39
  108.6 7.3 %collective-permute-done.14 = bf16[3,2,128,256]{3,2,1,0:T(8,128)(2,1)S(1)} collective-permute-done((bf16[3,2,128,256]{3,2,1,0:T(8,128)(2,1)S(1)}, bf16[3,2,128,256]{3,2,1,0:T(8,128)(2,1)S(1)}, u32[]{:S(2)}, u32[]{:S(2)}) %collective-permute-start.14) | collective-permute-done | bytes 393248 | tf_op jit(solution)/shard_map/ppermute | solution.py:38
  125.2 3.4 %collective-permute-start.15 = (bf16[3,1,128,256]{3,2,1,0:T(8,128)(2,1)S(1)}, bf16[3,1,128,256]{3,2,1,0:T(8,128)(2,1)S(1)}, u32[]{:S(2)}, u32[]{:S(2)}) collective-permute-start(bf16[3,1,128,256]{3,2,1,0:T(8,128)(2,1)S(1)} %slice.151), channel_id=1, source_target_pairs={{0,16},{16,32},{32,48},{48,64},{64,80},{80,96},{96,112},{112,128},... | collective-permute-start | bytes 589832 | tf_op jit(solution)/shard_map/ppermute | solution.py:43
  128.5 7.1 %fusion.3 = f32[3,512,256]{2,1,0:T(8,128)S(1)} fusion(bf16[3,3840,256]{2,1,0:T(8,128)(2,1)} %bitcast.32, bf16[512,4096]{1,0:T(8,128)(2,1)} %bitcast.34), kind=kOutput, calls=%fused_computation.4 | convolution fusion | flops 3019898880 | bytes 11403264 | tf_op jit(solution)/shard_map/sk,ikc->isc/dot_general | solution.py:85
  138.6 19.2 %all_to_all.10 = bf16[16,80,128]{2,1,0:T(8,128)(2,1)S(1)} all-to-all(bf16[16,80,128]{2,1,0:T(8,128)(2,1)S(1)} %pad_maximum_fusion.2), channel_id=1, replica_groups=mesh['fsdp'=32,'tp'=16] {'tp'}, dimensions={0} | all-to-all | bytes 655360 | tf_op jit(solution)/shard_map/all_to_all | solution.py:120
  (72 shorter events, 31.7 us)
Async XLA Ops:
  0.6 7.2 %collective-permute-start = (bf16[3,128,256]{2,1,0:T(8,128)(2,1)}, bf16[3,128,256]{2,1,0:T(8,128)(2,1)S(1)}, u32[]{:S(2)}, u32[]{:S(2)}) collective-permute-start(bf16[3,128,256]{2,1,0:T(8,128)(2,1)} %param.13), channel_id=1, source_target_pairs={{0,256},{16,272},{32,288},{48,304},{64,320},{80,336},{96,352},{112... | collective-permute-start | bytes 589832 | tf_op jit(solution)/shard_map/ppermute | solution.py:29
  8.8 19.5 %collective-permute-start.1 = (bf16[3,2,128,256]{3,2,1,0:T(8,128)(2,1)S(1)}, bf16[3,2,128,256]{3,2,1,0:T(8,128)(2,1)S(1)}, u32[]{:S(2)}, u32[]{:S(2)}) collective-permute-start(bf16[3,2,128,256]{3,2,1,0:T(8,128)(2,1)S(1)} %pad_maximum_fusion), channel_id=1, source_target_pairs={{0,240},{16,0},{32,16},{48,32},{64,48},{80,64},{96,80},{112,96},{1... | collective-permute-start | bytes 1179656 | tf_op jit(solution)/shard_map/ppermute | solution.py:39
  21.5 12.2 %collective-permute-start.8 = (bf16[3,2,128,256]{3,2,1,0:T(8,128)(2,1)S(1)}, bf16[3,2,128,256]{3,2,1,0:T(8,128)(2,1)S(1)}, u32[]{:S(2)}, u32[]{:S(2)}) collective-permute-start(bf16[3,2,128,256]{3,2,1,0:T(8,128)(2,1)S(1)} %pad_maximum_fusion), channel_id=1, source_target_pairs={{0,16},{16,32},{32,48},{48,64},{64,80},{80,96},{96,112},{112,128},... | collective-permute-start | bytes 1179656 | tf_op jit(solution)/shard_map/ppermute | solution.py:38
  28.3 11.2 %collective-permute-start.2 = (bf16[3,2,128,256]{3,2,1,0:T(8,128)(2,1)S(1)}, bf16[3,2,128,256]{3,2,1,0:T(8,128)(2,1)S(1)}, u32[]{:S(2)}, u32[]{:S(2)}) collective-permute-start(bf16[3,2,128,256]{3,2,1,0:T(8,128)(2,1)S(1)} %collective-permute-done.1), channel_id=1, source_target_pairs={{0,240},{16,0},{32,16},{48,32},{64,48},{80,64},{96,80},{112,96},{1... | collective-permute-start | bytes 1179656 | tf_op jit(solution)/shard_map/ppermute | solution.py:39
  33.6 11.2 %collective-permute-start.9 = (bf16[3,2,128,256]{3,2,1,0:T(8,128)(2,1)S(1)}, bf16[3,2,128,256]{3,2,1,0:T(8,128)(2,1)S(1)}, u32[]{:S(2)}, u32[]{:S(2)}) collective-permute-start(bf16[3,2,128,256]{3,2,1,0:T(8,128)(2,1)S(1)} %collective-permute-done.8), channel_id=1, source_target_pairs={{0,16},{16,32},{32,48},{48,64},{64,80},{80,96},{96,112},{112,128},... | collective-permute-start | bytes 1179656 | tf_op jit(solution)/shard_map/ppermute | solution.py:38
  39.5 21.8 %collective-permute-start.3 = (bf16[3,2,128,256]{3,2,1,0:T(8,128)(2,1)S(1)}, bf16[3,2,128,256]{3,2,1,0:T(8,128)(2,1)S(1)}, u32[]{:S(2)}, u32[]{:S(2)}) collective-permute-start(bf16[3,2,128,256]{3,2,1,0:T(8,128)(2,1)S(1)} %collective-permute-done.2), channel_id=1, source_target_pairs={{0,240},{16,0},{32,16},{48,32},{64,48},{80,64},{96,80},{112,96},{1... | collective-permute-start | bytes 1179656 | tf_op jit(solution)/shard_map/ppermute | solution.py:39
  44.9 21.3 %collective-permute-start.10 = (bf16[3,2,128,256]{3,2,1,0:T(8,128)(2,1)S(1)}, bf16[3,2,128,256]{3,2,1,0:T(8,128)(2,1)S(1)}, u32[]{:S(2)}, u32[]{:S(2)}) collective-permute-start(bf16[3,2,128,256]{3,2,1,0:T(8,128)(2,1)S(1)} %collective-permute-done.9), channel_id=1, source_target_pairs={{0,16},{16,32},{32,48},{48,64},{64,80},{80,96},{96,112},{112,128},... | collective-permute-start | bytes 1179656 | tf_op jit(solution)/shard_map/ppermute | solution.py:38
  48.1 20.0 %copy-start.1 = (s32[1,512]{1,0:T(1,128)S(1)}, s32[1,512]{1,0:T(1,128)}, u32[]{:S(2)}) copy-start(s32[1,512]{1,0:T(1,128)} %param.15) | copy-start | bytes 6148
  48.1 20.1 %copy-start = (f32[16,7]{0,1:T(8,128)S(1)}, f32[16,7]{0,1:T(8,128)}, u32[]{:S(2)}) copy-start(f32[16,7]{0,1:T(8,128)} %param.14) | copy-start | bytes 1348
  50.7 72.5 %all-to-all-start = ((bf16[16,32,4096]{2,1,0:T(8,128)(2,1)}), bf16[16,32,4096]{2,1,0:T(8,128)(2,1)}, u32[]{:S(2)}, u32[]{:S(2)}) async-start(bf16[16,32,4096]{2,1,0:T(8,128)(2,1)} %broadcast_in_dim.9), calls=%async_computation | async-start | bytes 8388608 | tf_op jit(solution)/shard_map/all_to_all | solution.py:78
  61.3 13.2 %collective-permute-start.4 = (bf16[3,2,128,256]{3,2,1,0:T(8,128)(2,1)S(1)}, bf16[3,2,128,256]{3,2,1,0:T(8,128)(2,1)}, u32[]{:S(2)}, u32[]{:S(2)}) collective-permute-start(bf16[3,2,128,256]{3,2,1,0:T(8,128)(2,1)S(1)} %collective-permute-done.3), channel_id=1, source_target_pairs={{0,240},{16,0},{32,16},{48,32},{64,48},{80,64},{96,80},{112,96},{1... | collective-permute-start | bytes 1179656 | tf_op jit(solution)/shard_map/ppermute | solution.py:39
  66.2 13.8 %collective-permute-start.11 = (bf16[3,2,128,256]{3,2,1,0:T(8,128)(2,1)S(1)}, bf16[3,2,128,256]{3,2,1,0:T(8,128)(2,1)}, u32[]{:S(2)}, u32[]{:S(2)}) collective-permute-start(bf16[3,2,128,256]{3,2,1,0:T(8,128)(2,1)S(1)} %collective-permute-done.10), channel_id=1, source_target_pairs={{0,16},{16,32},{32,48},{48,64},{64,80},{80,96},{96,112},{112,128},... | collective-permute-start | bytes 1179656 | tf_op jit(solution)/shard_map/ppermute | solution.py:38
  74.5 13.2 %collective-permute-start.5 = (bf16[3,2,128,256]{3,2,1,0:T(8,128)(2,1)}, bf16[3,2,128,256]{3,2,1,0:T(8,128)(2,1)S(1)}, u32[]{:S(2)}, u32[]{:S(2)}) collective-permute-start(bf16[3,2,128,256]{3,2,1,0:T(8,128)(2,1)} %collective-permute-done.4), channel_id=1, source_target_pairs={{0,240},{16,0},{32,16},{48,32},{64,48},{80,64},{96,80},{112,96},{1... | collective-permute-start | bytes 1179656 | tf_op jit(solution)/shard_map/ppermute | solution.py:39
  80.0 13.1 %collective-permute-start.12 = (bf16[3,2,128,256]{3,2,1,0:T(8,128)(2,1)}, bf16[3,2,128,256]{3,2,1,0:T(8,128)(2,1)S(1)}, u32[]{:S(2)}, u32[]{:S(2)}) collective-permute-start(bf16[3,2,128,256]{3,2,1,0:T(8,128)(2,1)} %collective-permute-done.11), channel_id=1, source_target_pairs={{0,16},{16,32},{32,48},{48,64},{64,80},{80,96},{96,112},{112,128},... | collective-permute-start | bytes 1179656 | tf_op jit(solution)/shard_map/ppermute | solution.py:38
  87.7 11.9 %collective-permute-start.6 = (bf16[3,2,128,256]{3,2,1,0:T(8,128)(2,1)S(1)}, bf16[3,2,128,256]{3,2,1,0:T(8,128)(2,1)S(1)}, u32[]{:S(2)}, u32[]{:S(2)}) collective-permute-start(bf16[3,2,128,256]{3,2,1,0:T(8,128)(2,1)S(1)} %collective-permute-done.5), channel_id=1, source_target_pairs={{0,240},{16,0},{32,16},{48,32},{64,48},{80,64},{96,80},{112,96},{1... | collective-permute-start | bytes 1179656 | tf_op jit(solution)/shard_map/ppermute | solution.py:39
  93.0 12.0 %collective-permute-start.13 = (bf16[3,2,128,256]{3,2,1,0:T(8,128)(2,1)S(1)}, bf16[3,2,128,256]{3,2,1,0:T(8,128)(2,1)S(1)}, u32[]{:S(2)}, u32[]{:S(2)}) collective-permute-start(bf16[3,2,128,256]{3,2,1,0:T(8,128)(2,1)S(1)} %collective-permute-done.12), channel_id=1, source_target_pairs={{0,16},{16,32},{32,48},{48,64},{64,80},{80,96},{96,112},{112,128},... | collective-permute-start | bytes 1179656 | tf_op jit(solution)/shard_map/ppermute | solution.py:38
  99.6 16.3 %collective-permute-start.7 = (bf16[3,2,128,256]{3,2,1,0:T(8,128)(2,1)S(1)}, bf16[3,2,128,256]{3,2,1,0:T(8,128)(2,1)S(1)}, u32[]{:S(2)}, u32[]{:S(2)}) collective-permute-start(bf16[3,2,128,256]{3,2,1,0:T(8,128)(2,1)S(1)} %collective-permute-done.6), channel_id=1, source_target_pairs={{0,240},{16,0},{32,16},{48,32},{64,48},{80,64},{96,80},{112,96},{1... | collective-permute-start | bytes 1179656 | tf_op jit(solution)/shard_map/ppermute | solution.py:39
  105.1 10.8 %collective-permute-start.14 = (bf16[3,2,128,256]{3,2,1,0:T(8,128)(2,1)S(1)}, bf16[3,2,128,256]{3,2,1,0:T(8,128)(2,1)S(1)}, u32[]{:S(2)}, u32[]{:S(2)}) collective-permute-start(bf16[3,2,128,256]{3,2,1,0:T(8,128)(2,1)S(1)} %collective-permute-done.13), channel_id=1, source_target_pairs={{0,16},{16,32},{32,48},{48,64},{64,80},{80,96},{96,112},{112,128},... | collective-permute-start | bytes 1179656 | tf_op jit(solution)/shard_map/ppermute | solution.py:38
  123.2 12.4 %collective-permute-start.16 = (bf16[3,1,128,256]{3,2,1,0:T(8,128)(2,1)S(1)}, bf16[3,1,128,256]{3,2,1,0:T(8,128)(2,1)S(1)}, u32[]{:S(2)}, u32[]{:S(2)}) collective-permute-start(bf16[3,1,128,256]{3,2,1,0:T(8,128)(2,1)S(1)} %slice.152), channel_id=1, source_target_pairs={{0,240},{16,0},{32,16},{48,32},{64,48},{80,64},{96,80},{112,96},{1... | collective-permute-start | bytes 589832 | tf_op jit(solution)/shard_map/ppermute | solution.py:44
  125.2 10.5 %collective-permute-start.15 = (bf16[3,1,128,256]{3,2,1,0:T(8,128)(2,1)S(1)}, bf16[3,1,128,256]{3,2,1,0:T(8,128)(2,1)S(1)}, u32[]{:S(2)}, u32[]{:S(2)}) collective-permute-start(bf16[3,1,128,256]{3,2,1,0:T(8,128)(2,1)S(1)} %slice.151), channel_id=1, source_target_pairs={{0,16},{16,32},{32,48},{48,64},{64,80},{80,96},{96,112},{112,128},... | collective-permute-start | bytes 589832 | tf_op jit(solution)/shard_map/ppermute | solution.py:43
  135.6 2.4 %copy-start.2 = (s32[1,16]{1,0:T(1,128)S(1)}, s32[1,16]{1,0:T(1,128)}, u32[]{:S(2)}) copy-start(s32[1,16]{1,0:T(1,128)} %param.16) | copy-start | bytes 196

commit v12 on v11

--- a/solution.py
+++ b/solution.py
@@ -34,21 +34,25 @@
     behind = []
     right = pair
     left = pair
-    for _ in range(1, z_size // 2):
+    last_ring_step = z_size // 2 - 1
+    for step in range(1, last_ring_step + 1):
+        if step == last_ring_step:
+            right, left, companion = lax.optimization_barrier((right, left, companion))
         right = lax.ppermute(right, "fsdp", z_up)
         left = lax.ppermute(left, "fsdp", z_down)
         behind.append(right)
         ahead.append(left)
-    sent_a, sent_b, companion = lax.optimization_barrier((right[:, :1], left[:, 1:], companion))
-    last_a = lax.ppermute(sent_a, "fsdp", z_up)
-    last_b = lax.ppermute(sent_b, "fsdp", z_down)
+    last_a = lax.ppermute(right[:, :1], "fsdp", z_up)
+    last_b = lax.ppermute(left[:, 1:], "fsdp", z_down)
     last = jnp.concatenate([last_a, last_b], axis=1)
-    stacked = with_layout_constraint(
-        jnp.stack(ahead + behind[::-1], axis=1), Layout((0, 1, 2, 3, 4))
-    )
-    lead, count, halves, block, width = stacked.shape
-    early = stacked.reshape(lead, count * halves * block, width)
-    return early, last.reshape(lead, halves * block, width), companion
+    lead, halves, block, width = pair.shape
+    kept = last_ring_step - 1
+    groups = [ahead[: kept + 1] + behind[: kept][::-1], ahead[kept + 1 :] + behind[kept:]]
+    stacks = []
+    for group in groups:
+        stacked = with_layout_constraint(jnp.stack(group, axis=1), Layout((0, 1, 2, 3, 4)))
+        stacks.append(stacked.reshape(lead, len(group) * halves * block, width))
+    return stacks, last.reshape(lead, halves * block, width), companion
 
 
 def local(activations, norm_gain, proj_weight, short_filter, segment_ids, needle_pos, readout):
@@ -63,29 +67,31 @@
     scaled = lax.rsqrt(jnp.mean(values * values, axis=1, keepdims=True) + EPSILON)
     normed = (values * scaled * norm_gain[None, :]).astype(jnp.bfloat16)
     z = lax.axis_index("fsdp") % z_size
-    half = z_size // 2
     grid = jnp.transpose(normed.reshape(local_rows, 2, z_size, block), (0, 2, 1, 3))
     doubled = jnp.concatenate([grid, grid], axis=1)
+    runs = [(0, 7), (10, 6), (7, 1), (9, 1), (8, 1)]
     ordered = jnp.concatenate(
-        [
-            lax.dynamic_slice_in_dim(doubled, z, half, axis=1),
-            lax.dynamic_slice_in_dim(doubled, z + half + 1, half - 1, axis=1),
-            lax.dynamic_slice_in_dim(doubled, z + half, 1, axis=1),
-        ],
+        [lax.dynamic_slice_in_dim(doubled, z + first, size, axis=1) for first, size in runs],
         axis=1,
     ).reshape(local_rows, model_width)
     spread = jnp.broadcast_to(ordered[None], (tp_size,) + ordered.shape)
     slab_rows = lax.all_to_all(spread, "tp", 0, 0, tiled=False).reshape(
         tp_size * local_rows, model_width
     )
-    early_weights, last_weights, slab_rows = gather_weights(
+    (first_weights, second_weights), last_weights, slab_rows = gather_weights(
         proj_weight, fsdp_size, z_size, slab_rows
     )
-    split = early_weights.shape[1]
-    early = jnp.einsum(
-        "sk,ikc->isc", slab_rows[:, :split], early_weights, preferred_element_type=jnp.float32
+    cut = first_weights.shape[1]
+    split = cut + second_weights.shape[1]
+    early = lax.optimization_barrier(
+        jnp.einsum("sk,ikc->isc", slab_rows[:, :cut], first_weights, preferred_element_type=jnp.float32)
     )
-    early = lax.optimization_barrier(early)
+    early = lax.optimization_barrier(
+        early
+        + jnp.einsum(
+            "sk,ikc->isc", slab_rows[:, cut:split], second_weights, preferred_element_type=jnp.float32
+        )
+    )
     projected = early + jnp.einsum(
         "sk,ikc->isc", slab_rows[:, split:], last_weights, preferred_element_type=jnp.float32
     )

time: 160 us -> 159 us (level)
  waiting for transfers between devices: 28 us -> 37.8 us
  local copies, waits for them, and re-layouts: 18.3 us -> 9.31 us
  starting transfers between devices: 77.5 us -> 73.2 us
  blocking collectives: 19.2 us -> 21 us
    ppermute x7, waiting for transfers between devices: 7.35 us -> 30.5 us  [gather_weights(): right = lax.ppermute(right, 'fsdp', z_up)]
    ppermute x7, waiting for transfers between devices: 17.4 us -> 2.96 us  [gather_weights(): left = lax.ppermute(left, 'fsdp', z_down)]
    unnamed x20 -> x18, local copies, waits for them, and re-layouts: 12.2 us -> 1.36 us
    ppermute x7, starting transfers between devices: 44.2 us -> 38.1 us  [gather_weights(): left = lax.ppermute(left, 'fsdp', z_down)]
    ppermute x2, waiting for transfers between devices: 0.01 us -> 2.28 us  [the longest x1 1.5 us: gather_weights(): last_b = lax.ppermute(left[:, 1:], 'fsdp', z_down)]
    another operation x1 -> x2, local copies, waits for them, and re-layouts: 0.78 us -> 2.62 us  [gather_weights(): jnp.stack(group, axis=1)]
    all_to_all x1, blocking collectives: 19.2 us -> 21 us  [local(): gathered = lax.all_to_all(payload, 'tp', 0, 0, tiled=False)]
    dot_general x1 -> x2, matrix products: 7.07 us -> 7.9 us  [the longest x1 6.29 us: local(): jnp.einsum('sk,ikc->isc', slab_rows[:, :cut], first_weights, preferred_el...]
  transfers between devices with their start and end apart: 18 -> 18, of which waited for: 7 -> 10; matrix products, arithmetic and copies ran while one was open for 18% -> 11% of each run, Pallas kernels for 0% -> 0%
where the time goes in v12:
time: 159 us; the launch traced here: 158 us
  starting transfers between devices  73.2 us (46%)
  waiting for transfers between devices  37.8 us (24%)
  blocking collectives  21 us (13%)
  matrix products  9.52 us (6%)
  local copies, waits for them, and re-layouts  9.31 us (6%)
  other arithmetic  5.87 us (4%)
    ppermute x7, starting transfers between devices, gather_weights(): left = lax.ppermute(left, 'fsdp', z_down)  38.1 us
    ppermute x7, waiting for transfers between devices, gather_weights(): right = lax.ppermute(right, 'fsdp', z_up)  30.5 us
    all_to_all x1, blocking collectives, local(): gathered = lax.all_to_all(payload, 'tp', 0, 0, tiled=False)  21 us
    ppermute x7, starting transfers between devices, gather_weights(): right = lax.ppermute(right, 'fsdp', z_up)  14.8 us
    all_to_all x1, starting transfers between devices, local(): lax.all_to_all(spread, 'tp', 0, 0, tiled=False)  9.82 us
    dot_general x1, matrix products, local(): jnp.einsum('sk,ikc->isc', slab_rows[:, :cut], first_weights, preferred_el...  6.29 us
    ppermute x1, starting transfers between devices, gather_weights(): last_b = lax.ppermute(left[:, 1:], 'fsdp', z_down)  4.04 us
    ppermute x1, starting transfers between devices, gather_weights(): other = lax.ppermute(proj_weight, 'fsdp', x_swap)  3.95 us
  transfers between devices with their start and end apart: 18, of which 10 were waited for; matrix products, arithmetic and copies ran while one was open for 11% of the time, Pallas kernels for 0%

profile of v12, /device:TPU:1, one launch (start us, length us, event | category | flops | bytes accessed | tf_op | source)
XLA Modules:
  0.0 157.9 jit_solution(3417570241508789014)
XLA Ops:
  0.6 4.0 %collective-permute-start = (bf16[3,128,256]{2,1,0:T(8,128)(2,1)}, bf16[3,128,256]{2,1,0:T(8,128)(2,1)S(1)}, u32[]{:S(2)}, u32[]{:S(2)}) collective-permute-start(bf16[3,128,256]{2,1,0:T(8,128)(2,1)} %param.13), channel_id=1, source_target_pairs={{0,256},{16,272},{32,288},{48,304},{64,320},{80,336},{96,352},{112... | collective-permute-start | bytes 589832 | tf_op jit(solution)/shard_map/ppermute | solution.py:29
  5.7 2.1 %collective-permute-done = bf16[3,128,256]{2,1,0:T(8,128)(2,1)S(1)} collective-permute-done((bf16[3,128,256]{2,1,0:T(8,128)(2,1)}, bf16[3,128,256]{2,1,0:T(8,128)(2,1)S(1)}, u32[]{:S(2)}, u32[]{:S(2)}) %collective-permute-start) | collective-permute-done | bytes 196640 | tf_op jit(solution)/shard_map/ppermute | solution.py:29
  8.8 12.6 %collective-permute-start.1 = (bf16[3,2,128,256]{3,2,1,0:T(8,128)(2,1)S(1)}, bf16[3,2,128,256]{3,2,1,0:T(8,128)(2,1)S(1)}, u32[]{:S(2)}, u32[]{:S(2)}) collective-permute-start(bf16[3,2,128,256]{3,2,1,0:T(8,128)(2,1)S(1)} %pad_maximum_fusion.1), channel_id=1, source_target_pairs={{0,240},{16,0},{32,16},{48,32},{64,48},{80,64},{96,80},{112,96},{1... | collective-permute-start | bytes 1179656 | tf_op jit(solution)/shard_map/ppermute | solution.py:42
  23.1 1.9 %collective-permute-start.7 = (bf16[3,2,128,256]{3,2,1,0:T(8,128)(2,1)S(1)}, bf16[3,2,128,256]{3,2,1,0:T(8,128)(2,1)S(1)}, u32[]{:S(2)}, u32[]{:S(2)}) collective-permute-start(bf16[3,2,128,256]{3,2,1,0:T(8,128)(2,1)S(1)} %pad_maximum_fusion.1), channel_id=1, source_target_pairs={{0,16},{16,32},{32,48},{48,64},{64,80},{80,96},{96,112},{112,128},... | collective-permute-start | bytes 1179656 | tf_op jit(solution)/shard_map/ppermute | solution.py:41
  25.4 2.9 %collective-permute-done.1 = bf16[3,2,128,256]{3,2,1,0:T(8,128)(2,1)S(1)} collective-permute-done((bf16[3,2,128,256]{3,2,1,0:T(8,128)(2,1)S(1)}, bf16[3,2,128,256]{3,2,1,0:T(8,128)(2,1)S(1)}, u32[]{:S(2)}, u32[]{:S(2)}) %collective-permute-start.1) | collective-permute-done | bytes 393248 | tf_op jit(solution)/shard_map/ppermute | solution.py:42
  28.3 5.3 %collective-permute-start.2 = (bf16[3,2,128,256]{3,2,1,0:T(8,128)(2,1)S(1)}, bf16[3,2,128,256]{3,2,1,0:T(8,128)(2,1)S(1)}, u32[]{:S(2)}, u32[]{:S(2)}) collective-permute-start(bf16[3,2,128,256]{3,2,1,0:T(8,128)(2,1)S(1)} %collective-permute-done.1), channel_id=1, source_target_pairs={{0,240},{16,0},{32,16},{48,32},{64,48},{80,64},{96,80},{112,96},{1... | collective-permute-start | bytes 1179656 | tf_op jit(solution)/shard_map/ppermute | solution.py:42
  34.0 2.6 %broadcast_in_dim.9 = bf16[16,32,4096]{2,1,0:T(8,128)(2,1)} broadcast(bf16[32,4096]{1,0:T(8,128)(2,1)S(1)} %broadcast_in_dim.8), dimensions={1,2} | broadcast | bytes 4456448 | tf_op jit(solution)/shard_map/broadcast_in_dim | solution.py:77
  36.5 9.8 %all-to-all-start = ((bf16[16,32,4096]{2,1,0:T(8,128)(2,1)}), bf16[16,32,4096]{2,1,0:T(8,128)(2,1)}, u32[]{:S(2)}, u32[]{:S(2)}) async-start(bf16[16,32,4096]{2,1,0:T(8,128)(2,1)} %broadcast_in_dim.9), calls=%async_computation | async-start | bytes 8388608 | tf_op jit(solution)/shard_map/all_to_all | solution.py:78
  46.4 1.9 %collective-permute-start.8 = (bf16[3,2,128,256]{3,2,1,0:T(8,128)(2,1)S(1)}, bf16[3,2,128,256]{3,2,1,0:T(8,128)(2,1)S(1)}, u32[]{:S(2)}, u32[]{:S(2)}) collective-permute-start(bf16[3,2,128,256]{3,2,1,0:T(8,128)(2,1)S(1)} %collective-permute-done.7), channel_id=1, source_target_pairs={{0,16},{16,32},{32,48},{48,64},{64,80},{80,96},{96,112},{112,128},... | collective-permute-start | bytes 1179656 | tf_op jit(solution)/shard_map/ppermute | solution.py:41
  48.3 4.6 %collective-permute-start.3 = (bf16[3,2,128,256]{3,2,1,0:T(8,128)(2,1)S(1)}, bf16[3,2,128,256]{3,2,1,0:T(8,128)(2,1)S(1)}, u32[]{:S(2)}, u32[]{:S(2)}) collective-permute-start(bf16[3,2,128,256]{3,2,1,0:T(8,128)(2,1)S(1)} %collective-permute-done.2), channel_id=1, source_target_pairs={{0,240},{16,0},{32,16},{48,32},{64,48},{80,64},{96,80},{112,96},{1... | collective-permute-start | bytes 1179656 | tf_op jit(solution)/shard_map/ppermute | solution.py:42
  53.1 7.1 %collective-permute-done.8 = bf16[3,2,128,256]{3,2,1,0:T(8,128)(2,1)S(1)} collective-permute-done((bf16[3,2,128,256]{3,2,1,0:T(8,128)(2,1)S(1)}, bf16[3,2,128,256]{3,2,1,0:T(8,128)(2,1)S(1)}, u32[]{:S(2)}, u32[]{:S(2)}) %collective-permute-start.8) | collective-permute-done | bytes 393248 | tf_op jit(solution)/shard_map/ppermute | solution.py:41
  62.1 4.6 %collective-permute-start.4 = (bf16[3,2,128,256]{3,2,1,0:T(8,128)(2,1)S(1)}, bf16[3,2,128,256]{3,2,1,0:T(8,128)(2,1)}, u32[]{:S(2)}, u32[]{:S(2)}) collective-permute-start(bf16[3,2,128,256]{3,2,1,0:T(8,128)(2,1)S(1)} %collective-permute-done.3), channel_id=1, source_target_pairs={{0,240},{16,0},{32,16},{48,32},{64,48},{80,64},{96,80},{112,96},{1... | collective-permute-start | bytes 1179656 | tf_op jit(solution)/shard_map/ppermute | solution.py:42
  67.6 5.6 %collective-permute-done.9 = bf16[3,2,128,256]{3,2,1,0:T(8,128)(2,1)S(1)} collective-permute-done((bf16[3,2,128,256]{3,2,1,0:T(8,128)(2,1)S(1)}, bf16[3,2,128,256]{3,2,1,0:T(8,128)(2,1)S(1)}, u32[]{:S(2)}, u32[]{:S(2)}) %collective-permute-start.9) | collective-permute-done | bytes 393248 | tf_op jit(solution)/shard_map/ppermute | solution.py:41
  75.1 4.6 %collective-permute-start.5 = (bf16[3,2,128,256]{3,2,1,0:T(8,128)(2,1)}, bf16[3,2,128,256]{3,2,1,0:T(8,128)(2,1)S(1)}, u32[]{:S(2)}, u32[]{:S(2)}) collective-permute-start(bf16[3,2,128,256]{3,2,1,0:T(8,128)(2,1)} %collective-permute-done.4), channel_id=1, source_target_pairs={{0,240},{16,0},{32,16},{48,32},{64,48},{80,64},{96,80},{112,96},{1... | collective-permute-start | bytes 1179656 | tf_op jit(solution)/shard_map/ppermute | solution.py:42
  79.7 5.6 %collective-permute-done.10 = bf16[3,2,128,256]{3,2,1,0:T(8,128)(2,1)S(1)} collective-permute-done((bf16[3,2,128,256]{3,2,1,0:T(8,128)(2,1)S(1)}, bf16[3,2,128,256]{3,2,1,0:T(8,128)(2,1)S(1)}, u32[]{:S(2)}, u32[]{:S(2)}) %collective-permute-start.10) | collective-permute-done | bytes 393248 | tf_op jit(solution)/shard_map/ppermute | solution.py:41
  87.2 4.6 %collective-permute-start.6 = (bf16[3,2,128,256]{3,2,1,0:T(8,128)(2,1)S(1)}, bf16[3,2,128,256]{3,2,1,0:T(8,128)(2,1)S(1)}, u32[]{:S(2)}, u32[]{:S(2)}) collective-permute-start(bf16[3,2,128,256]{3,2,1,0:T(8,128)(2,1)S(1)} %collective-permute-done.5), channel_id=1, source_target_pairs={{0,240},{16,0},{32,16},{48,32},{64,48},{80,64},{96,80},{112,96},{1... | collective-permute-start | bytes 1179656 | tf_op jit(solution)/shard_map/ppermute | solution.py:42
  92.9 3.8 %collective-permute-done.11 = bf16[3,2,128,256]{3,2,1,0:T(8,128)(2,1)S(1)} collective-permute-done((bf16[3,2,128,256]{3,2,1,0:T(8,128)(2,1)S(1)}, bf16[3,2,128,256]{3,2,1,0:T(8,128)(2,1)S(1)}, u32[]{:S(2)}, u32[]{:S(2)}) %collective-permute-start.11) | collective-permute-done | bytes 393248 | tf_op jit(solution)/shard_map/ppermute | solution.py:41
  98.6 8.4 %collective-permute-done.12 = bf16[3,2,128,256]{3,2,1,0:T(8,128)(2,1)S(1)} collective-permute-done((bf16[3,2,128,256]{3,2,1,0:T(8,128)(2,1)S(1)}, bf16[3,2,128,256]{3,2,1,0:T(8,128)(2,1)S(1)}, u32[]{:S(2)}, u32[]{:S(2)}) %collective-permute-start.12) | collective-permute-done | bytes 393248 | tf_op jit(solution)/shard_map/ppermute | solution.py:41
  107.2 2.6 %copy.23 = bf16[3,13,2,128,256]{4,3,2,1,0:T(8,128)(2,1)} copy(bf16[3,13,2,128,256]{4,3,2,0,1:T(8,128)(2,1)S(1)} %bitcast_dynamic-update-slice_fusion) | data formatting | bytes 10223616 | tf_op jit(solution)/shard_map/stack | solution.py:53
  111.8 3.4 %collective-permute-start.14 = (bf16[3,2,128,256]{3,2,1,0:T(8,128)(2,1)S(1)}, bf16[3,2,128,256]{3,2,1,0:T(8,128)(2,1)S(1)}, u32[]{:S(2)}, u32[]{:S(2)}) collective-permute-start(bf16[3,2,128,256]{3,2,1,0:T(8,128)(2,1)S(1)} %collective-permute-done.12), channel_id=1, source_target_pairs={{0,16},{16,32},{32,48},{48,64},{64,80},{80,96},{96,112},{112,128},... | collective-permute-start | bytes 1179656 | tf_op jit(solution)/shard_map/ppermute | solution.py:41
  115.1 6.3 %fusion.3 = f32[3,512,256]{2,1,0:T(8,128)S(1)} fusion(bf16[3,3328,256]{2,1,0:T(8,128)(2,1)} %bitcast.101, bf16[512,4096]{1,0:T(8,128)(2,1)} %bitcast.18), kind=kOutput, calls=%fused_computation.5 | convolution fusion | flops 2617245696 | bytes 10092544 | tf_op jit(solution)/shard_map/sk,ikc->isc/dot_general | solution.py:87
  123.2 2.4 %collective-permute-start.15 = (bf16[3,1,128,256]{3,2,1,0:T(8,128)(2,1)S(1)}, bf16[3,1,128,256]{3,2,1,0:T(8,128)(2,1)S(1)}, u32[]{:S(2)}, u32[]{:S(2)}) collective-permute-start(bf16[3,1,128,256]{3,2,1,0:T(8,128)(2,1)S(1)} %slice.155), channel_id=1, source_target_pairs={{0,16},{16,32},{32,48},{48,64},{64,80},{80,96},{96,112},{112,128},... | collective-permute-start | bytes 589832 | tf_op jit(solution)/shard_map/ppermute | solution.py:45
  125.7 4.0 %collective-permute-start.16 = (bf16[3,1,128,256]{3,2,1,0:T(8,128)(2,1)S(1)}, bf16[3,1,128,256]{3,2,1,0:T(8,128)(2,1)S(1)}, u32[]{:S(2)}, u32[]{:S(2)}) collective-permute-start(bf16[3,1,128,256]{3,2,1,0:T(8,128)(2,1)S(1)} %slice.156), channel_id=1, source_target_pairs={{0,240},{16,0},{32,16},{48,32},{64,48},{80,64},{96,80},{112,96},{1... | collective-permute-start | bytes 589832 | tf_op jit(solution)/shard_map/ppermute | solution.py:46
  135.3 21.0 %all_to_all.10 = bf16[16,80,128]{2,1,0:T(8,128)(2,1)S(1)} all-to-all(bf16[16,80,128]{2,1,0:T(8,128)(2,1)S(1)} %pad_maximum_fusion.3), channel_id=1, replica_groups=mesh['fsdp'=32,'tp'=16] {'tp'}, dimensions={0} | all-to-all | bytes 655360 | tf_op jit(solution)/shard_map/all_to_all | solution.py:126
  (75 shorter events, 25.1 us)
Async XLA Ops:
  0.6 7.2 %collective-permute-start = (bf16[3,128,256]{2,1,0:T(8,128)(2,1)}, bf16[3,128,256]{2,1,0:T(8,128)(2,1)S(1)}, u32[]{:S(2)}, u32[]{:S(2)}) collective-permute-start(bf16[3,128,256]{2,1,0:T(8,128)(2,1)} %param.13), channel_id=1, source_target_pairs={{0,256},{16,272},{32,288},{48,304},{64,320},{80,336},{96,352},{112... | collective-permute-start | bytes 589832 | tf_op jit(solution)/shard_map/ppermute | solution.py:29
  8.8 19.5 %collective-permute-start.1 = (bf16[3,2,128,256]{3,2,1,0:T(8,128)(2,1)S(1)}, bf16[3,2,128,256]{3,2,1,0:T(8,128)(2,1)S(1)}, u32[]{:S(2)}, u32[]{:S(2)}) collective-permute-start(bf16[3,2,128,256]{3,2,1,0:T(8,128)(2,1)S(1)} %pad_maximum_fusion.1), channel_id=1, source_target_pairs={{0,240},{16,0},{32,16},{48,32},{64,48},{80,64},{96,80},{112,96},{1... | collective-permute-start | bytes 1179656 | tf_op jit(solution)/shard_map/ppermute | solution.py:42
  23.1 23.2 %collective-permute-start.7 = (bf16[3,2,128,256]{3,2,1,0:T(8,128)(2,1)S(1)}, bf16[3,2,128,256]{3,2,1,0:T(8,128)(2,1)S(1)}, u32[]{:S(2)}, u32[]{:S(2)}) collective-permute-start(bf16[3,2,128,256]{3,2,1,0:T(8,128)(2,1)S(1)} %pad_maximum_fusion.1), channel_id=1, source_target_pairs={{0,16},{16,32},{32,48},{48,64},{64,80},{80,96},{96,112},{112,128},... | collective-permute-start | bytes 1179656 | tf_op jit(solution)/shard_map/ppermute | solution.py:41
  28.3 20.0 %collective-permute-start.2 = (bf16[3,2,128,256]{3,2,1,0:T(8,128)(2,1)S(1)}, bf16[3,2,128,256]{3,2,1,0:T(8,128)(2,1)S(1)}, u32[]{:S(2)}, u32[]{:S(2)}) collective-permute-start(bf16[3,2,128,256]{3,2,1,0:T(8,128)(2,1)S(1)} %collective-permute-done.1), channel_id=1, source_target_pairs={{0,240},{16,0},{32,16},{48,32},{64,48},{80,64},{96,80},{112,96},{1... | collective-permute-start | bytes 1179656 | tf_op jit(solution)/shard_map/ppermute | solution.py:42
  36.5 16.4 %copy-start = (f32[16,7]{0,1:T(8,128)S(1)}, f32[16,7]{0,1:T(8,128)}, u32[]{:S(2)}) copy-start(f32[16,7]{0,1:T(8,128)} %param.14) | copy-start | bytes 1348
  36.5 30.1 %copy-start.1 = (s32[1,512]{1,0:T(1,128)S(1)}, s32[1,512]{1,0:T(1,128)}, u32[]{:S(2)}) copy-start(s32[1,512]{1,0:T(1,128)} %param.15) | copy-start | bytes 6148
  36.5 73.3 %all-to-all-start = ((bf16[16,32,4096]{2,1,0:T(8,128)(2,1)}), bf16[16,32,4096]{2,1,0:T(8,128)(2,1)}, u32[]{:S(2)}, u32[]{:S(2)}) async-start(bf16[16,32,4096]{2,1,0:T(8,128)(2,1)} %broadcast_in_dim.9), calls=%async_computation | async-start | bytes 8388608 | tf_op jit(solution)/shard_map/all_to_all | solution.py:78
  46.4 13.8 %collective-permute-start.8 = (bf16[3,2,128,256]{3,2,1,0:T(8,128)(2,1)S(1)}, bf16[3,2,128,256]{3,2,1,0:T(8,128)(2,1)S(1)}, u32[]{:S(2)}, u32[]{:S(2)}) collective-permute-start(bf16[3,2,128,256]{3,2,1,0:T(8,128)(2,1)S(1)} %collective-permute-done.7), channel_id=1, source_target_pairs={{0,16},{16,32},{32,48},{48,64},{64,80},{80,96},{96,112},{112,128},... | collective-permute-start | bytes 1179656 | tf_op jit(solution)/shard_map/ppermute | solution.py:41
  48.3 13.8 %collective-permute-start.3 = (bf16[3,2,128,256]{3,2,1,0:T(8,128)(2,1)S(1)}, bf16[3,2,128,256]{3,2,1,0:T(8,128)(2,1)S(1)}, u32[]{:S(2)}, u32[]{:S(2)}) collective-permute-start(bf16[3,2,128,256]{3,2,1,0:T(8,128)(2,1)S(1)} %collective-permute-done.2), channel_id=1, source_target_pairs={{0,240},{16,0},{32,16},{48,32},{64,48},{80,64},{96,80},{112,96},{1... | collective-permute-start | bytes 1179656 | tf_op jit(solution)/shard_map/ppermute | solution.py:42
  60.2 13.0 %collective-permute-start.9 = (bf16[3,2,128,256]{3,2,1,0:T(8,128)(2,1)S(1)}, bf16[3,2,128,256]{3,2,1,0:T(8,128)(2,1)S(1)}, u32[]{:S(2)}, u32[]{:S(2)}) collective-permute-start(bf16[3,2,128,256]{3,2,1,0:T(8,128)(2,1)S(1)} %collective-permute-done.8), channel_id=1, source_target_pairs={{0,16},{16,32},{32,48},{48,64},{64,80},{80,96},{96,112},{112,128},... | collective-permute-start | bytes 1179656 | tf_op jit(solution)/shard_map/ppermute | solution.py:41
  62.1 13.0 %collective-permute-start.4 = (bf16[3,2,128,256]{3,2,1,0:T(8,128)(2,1)S(1)}, bf16[3,2,128,256]{3,2,1,0:T(8,128)(2,1)}, u32[]{:S(2)}, u32[]{:S(2)}) collective-permute-start(bf16[3,2,128,256]{3,2,1,0:T(8,128)(2,1)S(1)} %collective-permute-done.3), channel_id=1, source_target_pairs={{0,240},{16,0},{32,16},{48,32},{64,48},{80,64},{96,80},{112,96},{1... | collective-permute-start | bytes 1179656 | tf_op jit(solution)/shard_map/ppermute | solution.py:42
  73.1 12.2 %collective-permute-start.10 = (bf16[3,2,128,256]{3,2,1,0:T(8,128)(2,1)S(1)}, bf16[3,2,128,256]{3,2,1,0:T(8,128)(2,1)S(1)}, u32[]{:S(2)}, u32[]{:S(2)}) collective-permute-start(bf16[3,2,128,256]{3,2,1,0:T(8,128)(2,1)S(1)} %collective-permute-done.9), channel_id=1, source_target_pairs={{0,16},{16,32},{32,48},{48,64},{64,80},{80,96},{96,112},{112,128},... | collective-permute-start | bytes 1179656 | tf_op jit(solution)/shard_map/ppermute | solution.py:41
  75.1 12.1 %collective-permute-start.5 = (bf16[3,2,128,256]{3,2,1,0:T(8,128)(2,1)}, bf16[3,2,128,256]{3,2,1,0:T(8,128)(2,1)S(1)}, u32[]{:S(2)}, u32[]{:S(2)}) collective-permute-start(bf16[3,2,128,256]{3,2,1,0:T(8,128)(2,1)} %collective-permute-done.4), channel_id=1, source_target_pairs={{0,240},{16,0},{32,16},{48,32},{64,48},{80,64},{96,80},{112,96},{1... | collective-permute-start | bytes 1179656 | tf_op jit(solution)/shard_map/ppermute | solution.py:42
  85.3 11.3 %collective-permute-start.11 = (bf16[3,2,128,256]{3,2,1,0:T(8,128)(2,1)S(1)}, bf16[3,2,128,256]{3,2,1,0:T(8,128)(2,1)S(1)}, u32[]{:S(2)}, u32[]{:S(2)}) collective-permute-start(bf16[3,2,128,256]{3,2,1,0:T(8,128)(2,1)S(1)} %collective-permute-done.10), channel_id=1, source_target_pairs={{0,16},{16,32},{32,48},{48,64},{64,80},{80,96},{96,112},{112,128},... | collective-permute-start | bytes 1179656 | tf_op jit(solution)/shard_map/ppermute | solution.py:41
  87.2 11.3 %collective-permute-start.6 = (bf16[3,2,128,256]{3,2,1,0:T(8,128)(2,1)S(1)}, bf16[3,2,128,256]{3,2,1,0:T(8,128)(2,1)S(1)}, u32[]{:S(2)}, u32[]{:S(2)}) collective-permute-start(bf16[3,2,128,256]{3,2,1,0:T(8,128)(2,1)S(1)} %collective-permute-done.5), channel_id=1, source_target_pairs={{0,240},{16,0},{32,16},{48,32},{64,48},{80,64},{96,80},{112,96},{1... | collective-permute-start | bytes 1179656 | tf_op jit(solution)/shard_map/ppermute | solution.py:42
  96.6 10.4 %collective-permute-start.12 = (bf16[3,2,128,256]{3,2,1,0:T(8,128)(2,1)S(1)}, bf16[3,2,128,256]{3,2,1,0:T(8,128)(2,1)S(1)}, u32[]{:S(2)}, u32[]{:S(2)}) collective-permute-start(bf16[3,2,128,256]{3,2,1,0:T(8,128)(2,1)S(1)} %collective-permute-done.11), channel_id=1, source_target_pairs={{0,16},{16,32},{32,48},{48,64},{64,80},{80,96},{96,112},{112,128},... | collective-permute-start | bytes 1179656 | tf_op jit(solution)/shard_map/ppermute | solution.py:41
  109.8 11.6 %collective-permute-start.13 = (bf16[3,2,128,256]{3,2,1,0:T(8,128)(2,1)S(1)}, bf16[3,2,128,256]{3,2,1,0:T(8,128)(2,1)S(1)}, u32[]{:S(2)}, u32[]{:S(2)}) collective-permute-start(bf16[3,2,128,256]{3,2,1,0:T(8,128)(2,1)S(1)} %collective-permute-done.6), channel_id=1, source_target_pairs={{0,240},{16,0},{32,16},{48,32},{64,48},{80,64},{96,80},{112,96},{1... | collective-permute-start | bytes 1179656 | tf_op jit(solution)/shard_map/ppermute | solution.py:42
  111.8 9.7 %collective-permute-start.14 = (bf16[3,2,128,256]{3,2,1,0:T(8,128)(2,1)S(1)}, bf16[3,2,128,256]{3,2,1,0:T(8,128)(2,1)S(1)}, u32[]{:S(2)}, u32[]{:S(2)}) collective-permute-start(bf16[3,2,128,256]{3,2,1,0:T(8,128)(2,1)S(1)} %collective-permute-done.12), channel_id=1, source_target_pairs={{0,16},{16,32},{32,48},{48,64},{64,80},{80,96},{96,112},{112,128},... | collective-permute-start | bytes 1179656 | tf_op jit(solution)/shard_map/ppermute | solution.py:41
  123.2 7.6 %collective-permute-start.15 = (bf16[3,1,128,256]{3,2,1,0:T(8,128)(2,1)S(1)}, bf16[3,1,128,256]{3,2,1,0:T(8,128)(2,1)S(1)}, u32[]{:S(2)}, u32[]{:S(2)}) collective-permute-start(bf16[3,1,128,256]{3,2,1,0:T(8,128)(2,1)S(1)} %slice.155), channel_id=1, source_target_pairs={{0,16},{16,32},{32,48},{48,64},{64,80},{80,96},{96,112},{112,128},... | collective-permute-start | bytes 589832 | tf_op jit(solution)/shard_map/ppermute | solution.py:45
  125.7 6.6 %collective-permute-start.16 = (bf16[3,1,128,256]{3,2,1,0:T(8,128)(2,1)S(1)}, bf16[3,1,128,256]{3,2,1,0:T(8,128)(2,1)S(1)}, u32[]{:S(2)}, u32[]{:S(2)}) collective-permute-start(bf16[3,1,128,256]{3,2,1,0:T(8,128)(2,1)S(1)} %slice.156), channel_id=1, source_target_pairs={{0,240},{16,0},{32,16},{48,32},{64,48},{80,64},{96,80},{112,96},{1... | collective-permute-start | bytes 589832 | tf_op jit(solution)/shard_map/ppermute | solution.py:46
  130.0 4.7 %copy-start.2 = (s32[1,16]{1,0:T(1,128)S(1)}, s32[1,16]{1,0:T(1,128)}, u32[]{:S(2)}) copy-start(s32[1,16]{1,0:T(1,128)} %param.16) | copy-start | bytes 196
